TPU v7x, 32 devices: a whole 2x2x4 slice. The times are simulated.
32 devices in a mesh: slab: 4 (over y, x), gx: 8 (over z, core).
Axes of the slice: x: 2, y: 2, z: 4, core: 2. Of those that a mesh axis runs over, the one named last changes fastest.
Arguments:
- wavefield: bfloat16 [4, 2, 2048, 2048], P('slab', None, 'gx'), may hold values from -6 to 6
- boundary: bfloat16 [4, 2, 2048, 2048], P('slab', None, 'gx'), may hold values from -6 to 6
- source: bfloat16 [4, 2, 2048, 2048], P('slab', None, 'gx'), may hold values from -6 to 6
- slowness: float32 [4, 2048, 2048], P('slab', 'gx'), may hold values from 0.6 to 1.4
- reflectivity: float32 [4, 2048, 2048], P('slab', 'gx'), may hold values from -0.6 to 0.6
- ref_slowness: float32 [4], P('slab'), may hold values from 0.8 to 1.2
Outputs:
- extrapolated: bfloat16 [4, 2, 2048, 2048], P('slab', None, 'gx')
- image: float32 [4, 2048, 2048], P('slab', 'gx')
All inputs are finite; a program needn't handle non-finite values.
Results may differ from a plain program's by a relative error of at most 0.001.
Values may be sent and summed in bfloat16 or wider, within the bound.
No kernel may reach another device: no remote copies, remote signals or barrier semaphores. Data moves between devices by JAX's collectives and lax.ppermute only.
A program may use at most 64 MiB of HBM per device.

v0:
```python
from functools import partial
import math

import jax
import jax.numpy as jnp
from jax import lax
from jax.sharding import PartitionSpec as P
from jax.experimental import pallas as pl
from jax.experimental.pallas import tpu as pltpu

OMEGA = 2.5
DEPTH_STEP = 1.0
precise = lax.Precision.HIGHEST


def shifted(block, axis, distance):
    devices = range(lax.axis_size(axis))
    route = [(i - distance, i) for i in devices if i - distance in devices]
    return lax.ppermute(block, axis, route)


def factor_pair(length):
    outer = math.gcd(length, 16)
    return (outer, length // outer)


def dft_table(length, orient):
    position = jnp.arange(length, dtype=jnp.int32)
    product = position[:, None] * position[None, :] % length
    angle = orient * 2.0 * math.pi * product.astype(jnp.float32) / length
    return (jnp.cos(angle), jnp.sin(angle))


def twiddle_table(first, second, length, orient):
    product = (
        jnp.arange(first, dtype=jnp.int32)[:, None]
        * jnp.arange(second, dtype=jnp.int32)[None, :]
        % length
    )
    angle = orient * 2.0 * math.pi * product.astype(jnp.float32) / length
    return (jnp.cos(angle), jnp.sin(angle))


def complex_einsum(form, table, field):
    mixing = partial(jnp.einsum, form, precision=precise)
    return (
        mixing(table[0], field[0]) - mixing(table[1], field[1]),
        mixing(table[0], field[1]) + mixing(table[1], field[0]),
    )


def times_complex(field, factor):
    return (
        field[0] * factor[0] - field[1] * factor[1],
        field[0] * factor[1] + field[1] * factor[0],
    )


def columns_forward(field):
    count, length = field[0].shape
    outer, inner = factor_pair(length)
    shaped = tuple((part.reshape(count, outer, inner) for part in field))
    section = complex_einsum("ka,rab->rkb", dft_table(outer, -1.0), shaped)
    section = times_complex(section, twiddle_table(outer, inner, length, -1.0))
    section = complex_einsum("mb,rkb->rkm", dft_table(inner, -1.0), section)
    return tuple((part.reshape(count, length) for part in section))


def columns_inverse(field):
    count, length = field[0].shape
    outer, inner = factor_pair(length)
    shaped = tuple((part.reshape(count, outer, inner) for part in field))
    section = complex_einsum("mb,rkm->rkb", dft_table(inner, 1.0), shaped)
    section = times_complex(section, twiddle_table(outer, inner, length, 1.0))
    section = complex_einsum("ka,rkb->rab", dft_table(outer, 1.0), section)
    return tuple((part.reshape(count, length) for part in section))


def rows_forward(field):
    length, count = field[0].shape
    outer, inner = factor_pair(length)
    shaped = tuple((part.reshape(outer, inner, count) for part in field))
    section = complex_einsum("ka,abc->kbc", dft_table(outer, -1.0), shaped)
    turned = twiddle_table(outer, inner, length, -1.0)
    section = times_complex(section, (turned[0][:, :, None], turned[1][:, :, None]))
    section = complex_einsum("mb,kbc->kmc", dft_table(inner, -1.0), section)
    return tuple((part.reshape(length, count) for part in section))


def rows_inverse(field):
    length, count = field[0].shape
    outer, inner = factor_pair(length)
    shaped = tuple((part.reshape(outer, inner, count) for part in field))
    section = complex_einsum("mb,kmc->kbc", dft_table(inner, 1.0), shaped)
    turned = twiddle_table(outer, inner, length, 1.0)
    section = times_complex(section, (turned[0][:, :, None], turned[1][:, :, None]))
    section = complex_einsum("ka,kbc->abc", dft_table(outer, 1.0), section)
    return tuple((part.reshape(length, count) for part in section))


def rotate(part, step, count):
    step %= count
    if step == 0:
        return part
    if 4 * step == count:
        return (-part[1], part[0])
    if 2 * step == count:
        return (-part[0], -part[1])
    if 4 * step == 3 * count:
        return (part[1], -part[0])
    cosine = math.cos(2.0 * math.pi * step / count)
    sine = math.sin(2.0 * math.pi * step / count)
    return (part[0] * cosine - part[1] * sine, part[0] * sine + part[1] * cosine)


def fft_slabs(parts, orient):
    count = len(parts)
    if count == 1:
        return list(parts)
    even = fft_slabs(parts[0::2], orient)
    odd = fft_slabs(parts[1::2], orient)
    half = count // 2
    out = [None] * count
    for k in range(half):
        turned = rotate(odd[k], orient * k, count)
        out[k] = (even[k][0] + turned[0], even[k][1] + turned[1])
        out[k + half] = (even[k][0] - turned[0], even[k][1] - turned[1])
    return out


def stacked_matmul(stacked, real, imag):
    size = real.shape[1]
    rows = stacked.shape[0] // 2
    both = jnp.concatenate([real, imag], axis=1)
    prod = jnp.dot(stacked, both, precision=lax.Precision.HIGH, preferred_element_type=jnp.float32)
    return (
        prod[:rows, :size] - prod[rows:, size:],
        prod[:rows, size:] + prod[rows:, :size],
    )


def rows_kernel(x_ref, p_ref, w_ref, tw_ref, o_ref):
    outer = tw_ref.shape[1]
    inner = tw_ref.shape[2]
    slabs = [
        (x_ref[0, a * inner:(a + 1) * inner, :], x_ref[1, a * inner:(a + 1) * inner, :])
        for a in range(outer)
    ]
    spec = fft_slabs(slabs, -1)
    wr = w_ref[0]
    wi = w_ref[1]
    forward = jnp.concatenate([wr, wi], axis=0)
    backward = jnp.concatenate([wr, -wi], axis=0)
    outs = []
    for k in range(outer):
        zr, zi = spec[k]
        tr = tw_ref[0, k]
        ti = tw_ref[1, k]
        zr, zi = zr * tr - zi * ti, zr * ti + zi * tr
        yr, yi = stacked_matmul(forward, zr, zi)
        pr = p_ref[0, k * inner:(k + 1) * inner, :]
        pi = p_ref[1, k * inner:(k + 1) * inner, :]
        yr, yi = yr * pr - yi * pi, yr * pi + yi * pr
        sr, si = stacked_matmul(backward, yr, yi)
        outs.append((sr * tr + si * ti, si * tr - sr * ti))
    res = fft_slabs(outs, 1)
    for a in range(outer):
        o_ref[0, a * inner:(a + 1) * inner, :] = res[a][0]
        o_ref[1, a * inner:(a + 1) * inner, :] = res[a][1]


def rows_shift(turned, factor):
    _, length, width = turned.shape
    outer, inner = factor_pair(length)
    block = min(width, 128)
    table = dft_table(inner, -1.0)
    turn = twiddle_table(outer, inner, length, -1.0)
    table = jnp.stack(table)
    turn = jnp.stack(turn)[..., None]
    field_spec = pl.BlockSpec((2, length, block), lambda j: (0, 0, j))
    return pl.pallas_call(
        rows_kernel,
        grid=(width // block,),
        in_specs=[
            field_spec,
            field_spec,
            pl.BlockSpec((2, inner, inner), lambda j: (0, 0, 0)),
            pl.BlockSpec((2, outer, inner, 1), lambda j: (0, 0, 0, 0)),
        ],
        out_specs=field_spec,
        out_shape=jax.ShapeDtypeStruct(turned.shape, jnp.float32),
    )(turned, factor, table, turn)


def lanes_forward_kernel(base_ref, wave_ref, hand_ref, src_ref, slow_ref, refl_ref, w_ref, tw_ref, o_ref):
    outer = tw_ref.shape[1]
    inner = tw_ref.shape[2]
    base = base_ref[0, 0]
    gain = OMEGA * OMEGA * refl_ref[0]
    real_in = (
        wave_ref[0, 0].astype(jnp.float32)
        + hand_ref[0].astype(jnp.float32)
        + gain * src_ref[0, 0].astype(jnp.float32)
    )
    imag_in = (
        wave_ref[0, 1].astype(jnp.float32)
        + hand_ref[1].astype(jnp.float32)
        + gain * src_ref[0, 1].astype(jnp.float32)
    )
    angle = -OMEGA * (slow_ref[0] - base) * DEPTH_STEP
    cosine = jnp.cos(angle)
    sine = jnp.sin(angle)
    lensed_real = real_in * cosine - imag_in * sine
    lensed_imag = real_in * sine + imag_in * cosine
    slabs = [
        (lensed_real[:, a * inner:(a + 1) * inner], lensed_imag[:, a * inner:(a + 1) * inner])
        for a in range(outer)
    ]
    spec = fft_slabs(slabs, -1)
    both = jnp.concatenate([w_ref[0], w_ref[1]], axis=1)
    count = lensed_real.shape[0]
    for k in range(outer):
        zr, zi = spec[k]
        tr = tw_ref[0, k:k + 1, :]
        ti = tw_ref[1, k:k + 1, :]
        zr, zi = zr * tr - zi * ti, zr * ti + zi * tr
        prod = jnp.dot(
            jnp.concatenate([zr, zi], axis=0), both,
            precision=lax.Precision.HIGH, preferred_element_type=jnp.float32,
        )
        o_ref[0, :, k * inner:(k + 1) * inner] = prod[:count, :inner] - prod[count:, inner:]
        o_ref[1, :, k * inner:(k + 1) * inner] = prod[:count, inner:] + prod[count:, :inner]


def lanes_inverse_kernel(x_ref, src_ref, w_ref, tw_ref, ext_ref, img_ref):
    outer = tw_ref.shape[1]
    inner = tw_ref.shape[2]
    count = x_ref.shape[1]
    both = jnp.concatenate([w_ref[0], -w_ref[1]], axis=1)
    outs = []
    for k in range(outer):
        yr = x_ref[0, :, k * inner:(k + 1) * inner]
        yi = x_ref[1, :, k * inner:(k + 1) * inner]
        prod = jnp.dot(
            jnp.concatenate([yr, yi], axis=0), both,
            precision=lax.Precision.HIGH, preferred_element_type=jnp.float32,
        )
        sr = prod[:count, :inner] - prod[count:, inner:]
        si = prod[:count, inner:] + prod[count:, :inner]
        tr = tw_ref[0, k:k + 1, :]
        ti = tw_ref[1, k:k + 1, :]
        outs.append((sr * tr + si * ti, si * tr - sr * ti))
    res = fft_slabs(outs, 1)
    for a in range(outer):
        out_real, out_imag = res[a]
        lanes = slice(a * inner, (a + 1) * inner)
        ext_ref[0, 0, :, lanes] = out_real.astype(ext_ref.dtype)
        ext_ref[0, 1, :, lanes] = out_imag.astype(ext_ref.dtype)
        img_ref[0, :, lanes] = (
            src_ref[0, 0, :, lanes].astype(jnp.float32) * out_real
            + src_ref[0, 1, :, lanes].astype(jnp.float32) * out_imag
        )


def lane_tables(length):
    outer, inner = factor_pair(length)
    table = jnp.stack(dft_table(inner, -1.0))
    turn = jnp.stack(twiddle_table(outer, inner, length, -1.0))
    return outer, inner, table, turn


def lanes_forward(wavefield, handed, source, slowness, reflectivity, base, first, step):
    length = wavefield.shape[3]
    outer, inner, table, turn = lane_tables(length)
    block = min(step, 32)
    offset = first // block
    quad = lambda i: (0, 0, offset + i, 0)
    flat = lambda i: (0, offset + i, 0)
    return pl.pallas_call(
        lanes_forward_kernel,
        grid=(step // block,),
        in_specs=[
            pl.BlockSpec(memory_space=pltpu.SMEM),
            pl.BlockSpec((1, 2, block, length), quad),
            pl.BlockSpec((2, block, length), lambda i: (0, i, 0)),
            pl.BlockSpec((1, 2, block, length), quad),
            pl.BlockSpec((1, block, length), flat),
            pl.BlockSpec((1, block, length), flat),
            pl.BlockSpec((2, inner, inner), lambda i: (0, 0, 0)),
            pl.BlockSpec((2, outer, inner), lambda i: (0, 0, 0)),
        ],
        out_specs=pl.BlockSpec((2, block, length), lambda i: (0, i, 0)),
        out_shape=jax.ShapeDtypeStruct((2, step, length), jnp.float32),
    )(base.reshape(1, 1), wavefield, handed, source, slowness, reflectivity, table, turn)


def lanes_inverse(back, source):
    _, step, length = back.shape
    outer, inner, table, turn = lane_tables(length)
    block = min(step, 32)
    return pl.pallas_call(
        lanes_inverse_kernel,
        grid=(step // block,),
        in_specs=[
            pl.BlockSpec((2, block, length), lambda i: (0, i, 0)),
            pl.BlockSpec((1, 2, block, length), lambda i: (0, 0, i, 0)),
            pl.BlockSpec((2, inner, inner), lambda i: (0, 0, 0)),
            pl.BlockSpec((2, outer, inner), lambda i: (0, 0, 0)),
        ],
        out_specs=[
            pl.BlockSpec((1, 2, block, length), lambda i: (0, 0, i, 0)),
            pl.BlockSpec((1, block, length), lambda i: (0, i, 0)),
        ],
        out_shape=[
            jax.ShapeDtypeStruct((1, 2, step, length), jnp.bfloat16),
            jax.ShapeDtypeStruct((1, step, length), jnp.float32),
        ],
    )(back, source, table, turn)


def signed_freq(index, length):
    signed = jnp.where(index < length // 2, index, index - length)
    return signed.astype(jnp.float32) * (2.0 * math.pi / length)


def permuted_freq(position, length):
    outer, inner = factor_pair(length)
    index = position // inner + outer * (position % inner)
    return signed_freq(index, length)


def propagator(freq_row, freq_col, base, scale):
    kz_square = (OMEGA * base) ** 2 - freq_row * freq_row - freq_col * freq_col
    root = jnp.sqrt(jnp.abs(kz_square))
    upward = kz_square >= 0.0
    real_part = jnp.where(upward, jnp.cos(root * DEPTH_STEP), jnp.exp(-root * DEPTH_STEP))
    imag_part = jnp.where(upward, -jnp.sin(root * DEPTH_STEP), jnp.zeros_like(root))
    return (real_part * scale, imag_part * scale)


CHUNKS = 1


def lens_rows(wave, handed, source, slow, refl, base):
    wave = wave.astype(jnp.float32)
    handed = handed.astype(jnp.float32)
    source = source.astype(jnp.float32)
    real_in = wave[0] + handed[0] + OMEGA * OMEGA * refl * source[0]
    imag_in = wave[1] + handed[1] + OMEGA * OMEGA * refl * source[1]
    angle = -OMEGA * (slow - base) * DEPTH_STEP
    cosine = jnp.cos(angle)
    sine = jnp.sin(angle)
    return (real_in * cosine - imag_in * sine, real_in * sine + imag_in * cosine)


def body(wavefield, boundary, source, slowness, reflectivity, ref_slowness):
    count = wavefield.shape[2]
    columns = wavefield.shape[3]
    chunks = CHUNKS if count % CHUNKS == 0 else 1
    step = count // chunks
    groups = lax.axis_size("gx")
    device = lax.axis_index("gx")
    total_rows = count * groups
    width = columns // groups
    scale = 1.0 / (total_rows * columns)
    base = ref_slowness[0]
    pieces = []
    for c in range(chunks):
        rows = slice(c * step, (c + 1) * step)
        handed = shifted(boundary[0, :, rows], "slab", -1)
        field = lanes_forward(wavefield, handed, source, slowness, reflectivity, base, c * step, step)
        sent = lax.all_to_all(field, "gx", split_axis=2, concat_axis=1, tiled=True)
        pieces.append(sent.reshape(2, groups, step, width))
    turned = jnp.stack(pieces, axis=2).reshape(2, total_rows, width)
    freq_row = permuted_freq(jnp.arange(total_rows, dtype=jnp.int32), total_rows)
    freq_col = permuted_freq(device * width + jnp.arange(width, dtype=jnp.int32), columns)
    factor = propagator(freq_row[:, None], freq_col[None, :], base, scale)
    spatial = rows_shift(turned, jnp.stack(factor)).reshape(2, groups, chunks, step, width)
    extrapolated = []
    images = []
    for c in range(chunks):
        part = spatial[:, :, c].reshape(2, groups * step, width)
        back = lax.all_to_all(part, "gx", split_axis=1, concat_axis=2, tiled=True)
        ext, img = lanes_inverse(back, source[:, :, c * step:(c + 1) * step])
        extrapolated.append(ext)
        images.append(img)
    return (jnp.concatenate(extrapolated, axis=2), jnp.concatenate(images, axis=1))


def solution(mesh):
    return jax.shard_map(
        body,
        mesh=mesh,
        in_specs=(
            P("slab", None, "gx", None),
            P("slab", None, "gx", None),
            P("slab", None, "gx", None),
            P("slab", "gx", None),
            P("slab", "gx", None),
            P("slab"),
        ),
        out_specs=(P("slab", None, "gx", None), P("slab", "gx", None)),
        check_vma=False,
    )
```

profile of v0, /device:TPU:0, one launch (start us, length us, event | category | flops | bytes accessed | tf_op | source)
XLA Modules:
  0.0 319.7 jit_solution(7840320375034750724)
XLA Ops:
  0.6 1.3 collective-permute-start
  2.6 0.1 fusion.37
  2.6 0.6 fusion.44
  3.2 0.3 fusion.16
  3.5 0.7 pad_maximum_fusion.1.w_ref
  4.2 47.1 %collective-permute-done.hand_ref = bf16[2,256,2048]{2,1,0:T(8,128)(2,1)S(1)} collective-permute-done((bf16[2,256,2048]{2,1,0:T(8,128)(2,1)}, bf16[2,256,2048]{2,1,0:T(8,128)(2,1)S(1)}, u32[]{:S(2)}, u32[]{:S(2)}) %collective-permute-start) | collective-permute-done | bytes 2097184 | tf_op jit(solution)/shard_map/ppermute | solution.py:19
  51.3 0.0 copy-start
  51.3 1.3 copy-done
  52.6 16.4 %shard_map.77 = f32[2,256,2048]{2,1,0:T(8,128)} custom-call(f32[1,1]{1,0:T(1,128)} %bitcast.15.base_ref, bf16[1,2,256,2048]{3,2,1,0:T(8,128)(2,1)} %wave_ref.1, bf16[2,256,2048]{2,1,0:T(8,128)(2,1)} %copy-done, bf16[1,2,256,2048]{3,2,1,0:T(8,128)(2,1)} %src_ref.3, f32[1,256,2048]{2,1,0:T(8,128)} %slow_ref.1, f32[1,256,2048]{2,1,0:T(8,128)} %refl_ref.1, ...), custom_call_target="tpu_custom_call" | custom-call | tf_op jit(solution)/shard_map/pallas_call | solution.py:279
  69.0 7.3 %copy.11 = f32[2,256,2048]{1,0,2:T(2,128)} copy(f32[2,256,2048]{2,1,0:T(8,128)} %shard_map.77) | data formatting | bytes 8388608 | tf_op jit(solution)/shard_map/pallas_call | solution.py:279
  76.3 5.1 %all-to-all-start = ((f32[2,256,2048]{1,0,2:T(2,128)}), f32[2,256,2048]{1,0,2:T(2,128)}, u32[]{:S(2)}, u32[]{:S(2)}) async-start(f32[2,256,2048]{1,0,2:T(2,128)} %copy.11), calls=%async_computation | async-start | bytes 8388608 | tf_op jit(solution)/shard_map/all_to_all | solution.py:372
  81.4 2.0 copy.13.tw_ref
  83.4 8.4 %fusion.2 = (f32[1,2048,256]{2,1,0:T(8,128)S(1)}, f32[1,2048,256]{2,1,0:T(8,128)S(1)}) fusion(f32[256]{0:T(256)S(1)} %fusion.43, f32[2048]{0:T(1024)S(1)} %fusion.33), kind=kLoop, calls=%fused_computation.6 | loop fusion | flops 4718592 | bytes 4203520 | tf_op jit(solution)/shard_map/mul | solution.py:338
  91.8 2.2 pad_maximum_fusion.p_ref
  94.1 81.5 %all-to-all-done = f32[2,256,2048]{1,0,2:T(2,128)} async-done(((f32[2,256,2048]{1,0,2:T(2,128)}), f32[2,256,2048]{1,0,2:T(2,128)}, u32[]{:S(2)}, u32[]{:S(2)}) %all-to-all-start) | async-done | bytes 4194336 | tf_op jit(solution)/shard_map/all_to_all | solution.py:372
  175.5 7.2 %copy.12 = f32[2,256,8,256]{3,1,2,0:T(8,128)} copy(f32[2,256,8,256]{1,0,3,2:T(2,128)} %bitcast.2) | data formatting | bytes 8388608 | tf_op jit(solution)/shard_map/all_to_all | solution.py:372
  182.7 13.6 %shard_map.78 = f32[2,2048,256]{2,1,0:T(8,128)} custom-call(f32[2,2048,256]{2,1,0:T(8,128)} %bitcast.16, f32[2,2048,256]{2,1,0:T(8,128)} %pad_maximum_fusion.p_ref, f32[2,128,128]{2,1,0:T(8,128)} %pad_maximum_fusion.1.w_ref, f32[2,16,128,1]{3,2,1,0:T(8,128)} %copy.13.tw_ref), custom_call_target="tpu_custom_call" | custom-call | tf_op jit(solution)/shard_map/pallas_call | solution.py:181
  196.3 7.8 %copy.14 = f32[2,2048,256]{2,0,1:T(2,128)S(1)} copy(f32[2,2048,256]{2,1,0:T(8,128)} %shard_map.78) | data formatting | bytes 8388608 | tf_op jit(solution)/shard_map/pallas_call | solution.py:181
  204.1 96.5 %all_to_all.36 = f32[2,2048,256]{2,0,1:T(2,128)S(1)} all-to-all(f32[2,2048,256]{2,0,1:T(2,128)S(1)} %copy.14), channel_id=1, replica_groups=mesh['slab'=4,'gx'=8] {'gx'}, dimensions={1} | all-to-all | bytes 8388608 | tf_op jit(solution)/shard_map/all_to_all | solution.py:383
  300.6 4.4 %copy.17 = f32[2,8,256,256]{3,1,2,0:T(8,128)} copy(f32[2,8,256,256]{3,0,2,1:T(2,128)S(1)} %bitcast.17) | data formatting | bytes 8388608 | tf_op jit(solution)/shard_map/all_to_all | solution.py:383
  305.0 4.9 %all_to_all.33.x_ref = f32[2,256,2048]{2,1,0:T(8,128)} reshape(f32[2,256,8,256]{3,2,1,0:T(8,128)} %bitcast.18) | data formatting | bytes 8388608 | tf_op jit(solution)/shard_map/all_to_all | solution.py:383
  309.9 9.7 %shard_map.79 = (bf16[1,2,256,2048]{3,2,1,0:T(8,128)(2,1)}, f32[1,256,2048]{2,1,0:T(8,128)}) custom-call(f32[2,256,2048]{2,1,0:T(8,128)} %all_to_all.33.x_ref, bf16[1,2,256,2048]{3,2,1,0:T(8,128)(2,1)} %src_ref.3, f32[2,128,128]{2,1,0:T(8,128)} %pad_maximum_fusion.1.w_ref, f32[2,16,128]{2,1,0:T(8,128)} %get-tuple-element.3.tw_ref), custom_call_target="tpu_custom_call" | custom-call | tf_op jit(solution)/shard_map/pallas_call | solution.py:301
  (2 shorter events, 0.0 us)
Async XLA Ops:
  0.6 50.7 %collective-permute-start = (bf16[2,256,2048]{2,1,0:T(8,128)(2,1)}, bf16[2,256,2048]{2,1,0:T(8,128)(2,1)S(1)}, u32[]{:S(2)}, u32[]{:S(2)}) collective-permute-start(bf16[2,256,2048]{2,1,0:T(8,128)(2,1)} %bitcast.19), channel_id=1, source_target_pairs={{8,0},{16,8},{24,16},{9,1},{17,9},{25,17},{10,2},{18,10},{26,18},{... | collective-permute-start | bytes 6291464 | tf_op jit(solution)/shard_map/ppermute | solution.py:19
  51.3 1.3 copy-start
  76.3 99.2 %all-to-all-start = ((f32[2,256,2048]{1,0,2:T(2,128)}), f32[2,256,2048]{1,0,2:T(2,128)}, u32[]{:S(2)}, u32[]{:S(2)}) async-start(f32[2,256,2048]{1,0,2:T(2,128)} %copy.11), calls=%async_computation | async-start | bytes 8388608 | tf_op jit(solution)/shard_map/all_to_all | solution.py:372
where the time goes:
time: 321 us; the launch traced here: 320 us
  waiting for transfers between devices  129 us (40%)
  blocking collectives  96.5 us (30%)
  Pallas kernels  39.7 us (12%)
  local copies, waits for them, and re-layouts  34.8 us (11%)
  other arithmetic  12.3 us (4%)
  starting transfers between devices  6.42 us (2%)
    all_to_all x1, blocking collectives, body(): back = lax.all_to_all(part, 'gx', split_axis=1, concat_axis=2, tiled=True)  96.5 us
    all_to_all x1, waiting for transfers between devices, body(): sent = lax.all_to_all(field, 'gx', split_axis=2, concat_axis=1, tiled=True)  81.5 us
    ppermute x1, waiting for transfers between devices, shifted(): return lax.ppermute(block, axis, route)  47.1 us
    pallas_call x1, Pallas kernels, lanes_forward(): pl.pallas_call(lanes_forward_kernel, grid=(step // block,), in_specs=[pl....  16.4 us
    pallas_call x1, Pallas kernels, rows_shift(): pl.pallas_call(rows_kernel, grid=(width // block,), in_specs=[field_spec,...  13.6 us
    pallas_call x1, Pallas kernels, lanes_inverse(): pl.pallas_call(lanes_inverse_kernel, grid=(step // block,), in_specs=[pl....  9.74 us
    all_to_all x2, local copies, waits for them, and re-layouts, body(): back = lax.all_to_all(part, 'gx', split_axis=1, concat_axis=2, tiled=True)  9.29 us
    mul x1, other arithmetic, propagator(): return (real_part * scale, imag_part * scale)  8.44 us
  transfers between devices with their start and end apart: 2, of which 2 were waited for; matrix products, arithmetic and copies ran while one was open for 4% of the time, Pallas kernels for 0%

commit v1 on v0

--- a/solution.py
+++ b/solution.py
@@ -142,10 +142,15 @@
 def rows_kernel(x_ref, p_ref, w_ref, tw_ref, o_ref):
     outer = tw_ref.shape[1]
     inner = tw_ref.shape[2]
-    slabs = [
-        (x_ref[0, a * inner:(a + 1) * inner, :], x_ref[1, a * inner:(a + 1) * inner, :])
-        for a in range(outer)
-    ]
+    count = x_ref.shape[2]
+
+    def place(a):
+        return (a * inner) // count, slice((a * inner) % count, (a * inner) % count + inner)
+
+    slabs = []
+    for a in range(outer):
+        origin, rows = place(a)
+        slabs.append((x_ref[origin, 0, rows, :], x_ref[origin, 1, rows, :]))
     spec = fft_slabs(slabs, -1)
     wr = w_ref[0]
     wi = w_ref[1]
@@ -165,25 +170,27 @@
         outs.append((sr * tr + si * ti, si * tr - sr * ti))
     res = fft_slabs(outs, 1)
     for a in range(outer):
-        o_ref[0, a * inner:(a + 1) * inner, :] = res[a][0]
-        o_ref[1, a * inner:(a + 1) * inner, :] = res[a][1]
+        origin, rows = place(a)
+        o_ref[origin, 0, rows, :] = res[a][0]
+        o_ref[origin, 1, rows, :] = res[a][1]
 
 
 def rows_shift(turned, factor):
-    _, length, width = turned.shape
+    groups, _, count, width = turned.shape
+    length = groups * count
     outer, inner = factor_pair(length)
     block = min(width, 128)
     table = dft_table(inner, -1.0)
     turn = twiddle_table(outer, inner, length, -1.0)
     table = jnp.stack(table)
     turn = jnp.stack(turn)[..., None]
-    field_spec = pl.BlockSpec((2, length, block), lambda j: (0, 0, j))
+    field_spec = pl.BlockSpec((groups, 2, count, block), lambda j: (0, 0, 0, j))
     return pl.pallas_call(
         rows_kernel,
         grid=(width // block,),
         in_specs=[
             field_spec,
-            field_spec,
+            pl.BlockSpec((2, length, block), lambda j: (0, 0, j)),
             pl.BlockSpec((2, inner, inner), lambda j: (0, 0, 0)),
             pl.BlockSpec((2, outer, inner, 1), lambda j: (0, 0, 0, 0)),
         ],
@@ -228,19 +235,25 @@
             jnp.concatenate([zr, zi], axis=0), both,
             precision=lax.Precision.HIGH, preferred_element_type=jnp.float32,
         )
-        o_ref[0, :, k * inner:(k + 1) * inner] = prod[:count, :inner] - prod[count:, inner:]
-        o_ref[1, :, k * inner:(k + 1) * inner] = prod[:count, inner:] + prod[count:, :inner]
+        width = o_ref.shape[3]
+        dest = (k * inner) // width
+        lanes = slice((k * inner) % width, (k * inner) % width + inner)
+        o_ref[dest, 0, :, lanes] = prod[:count, :inner] - prod[count:, inner:]
+        o_ref[dest, 1, :, lanes] = prod[:count, inner:] + prod[count:, :inner]
 
 
 def lanes_inverse_kernel(x_ref, src_ref, w_ref, tw_ref, ext_ref, img_ref):
     outer = tw_ref.shape[1]
     inner = tw_ref.shape[2]
-    count = x_ref.shape[1]
+    count = x_ref.shape[2]
     both = jnp.concatenate([w_ref[0], -w_ref[1]], axis=1)
     outs = []
     for k in range(outer):
-        yr = x_ref[0, :, k * inner:(k + 1) * inner]
-        yi = x_ref[1, :, k * inner:(k + 1) * inner]
+        width = x_ref.shape[3]
+        origin = (k * inner) // width
+        lanes = slice((k * inner) % width, (k * inner) % width + inner)
+        yr = x_ref[origin, 0, :, lanes]
+        yi = x_ref[origin, 1, :, lanes]
         prod = jnp.dot(
             jnp.concatenate([yr, yi], axis=0), both,
             precision=lax.Precision.HIGH, preferred_element_type=jnp.float32,
@@ -269,7 +282,7 @@
     return outer, inner, table, turn
 
 
-def lanes_forward(wavefield, handed, source, slowness, reflectivity, base, first, step):
+def lanes_forward(wavefield, handed, source, slowness, reflectivity, base, first, step, groups):
     length = wavefield.shape[3]
     outer, inner, table, turn = lane_tables(length)
     block = min(step, 32)
@@ -289,20 +302,21 @@
             pl.BlockSpec((2, inner, inner), lambda i: (0, 0, 0)),
             pl.BlockSpec((2, outer, inner), lambda i: (0, 0, 0)),
         ],
-        out_specs=pl.BlockSpec((2, block, length), lambda i: (0, i, 0)),
-        out_shape=jax.ShapeDtypeStruct((2, step, length), jnp.float32),
+        out_specs=pl.BlockSpec((groups, 2, block, length // groups), lambda i: (0, 0, i, 0)),
+        out_shape=jax.ShapeDtypeStruct((groups, 2, step, length // groups), jnp.float32),
     )(base.reshape(1, 1), wavefield, handed, source, slowness, reflectivity, table, turn)
 
 
 def lanes_inverse(back, source):
-    _, step, length = back.shape
+    groups, _, step, width = back.shape
+    length = groups * width
     outer, inner, table, turn = lane_tables(length)
     block = min(step, 32)
     return pl.pallas_call(
         lanes_inverse_kernel,
         grid=(step // block,),
         in_specs=[
-            pl.BlockSpec((2, block, length), lambda i: (0, i, 0)),
+            pl.BlockSpec((groups, 2, block, width), lambda i: (0, 0, i, 0)),
             pl.BlockSpec((1, 2, block, length), lambda i: (0, 0, i, 0)),
             pl.BlockSpec((2, inner, inner), lambda i: (0, 0, 0)),
             pl.BlockSpec((2, outer, inner), lambda i: (0, 0, 0)),
@@ -368,19 +382,18 @@
     for c in range(chunks):
         rows = slice(c * step, (c + 1) * step)
         handed = shifted(boundary[0, :, rows], "slab", -1)
-        field = lanes_forward(wavefield, handed, source, slowness, reflectivity, base, c * step, step)
-        sent = lax.all_to_all(field, "gx", split_axis=2, concat_axis=1, tiled=True)
-        pieces.append(sent.reshape(2, groups, step, width))
-    turned = jnp.stack(pieces, axis=2).reshape(2, total_rows, width)
+        field = lanes_forward(wavefield, handed, source, slowness, reflectivity, base, c * step, step, groups)
+        pieces.append(lax.all_to_all(field, "gx", split_axis=0, concat_axis=0, tiled=True))
+    turned = pieces[0] if chunks == 1 else jnp.concatenate(pieces, axis=2)
     freq_row = permuted_freq(jnp.arange(total_rows, dtype=jnp.int32), total_rows)
     freq_col = permuted_freq(device * width + jnp.arange(width, dtype=jnp.int32), columns)
     factor = propagator(freq_row[:, None], freq_col[None, :], base, scale)
-    spatial = rows_shift(turned, jnp.stack(factor)).reshape(2, groups, chunks, step, width)
+    spatial = rows_shift(turned, jnp.stack(factor))
     extrapolated = []
     images = []
     for c in range(chunks):
-        part = spatial[:, :, c].reshape(2, groups * step, width)
-        back = lax.all_to_all(part, "gx", split_axis=1, concat_axis=2, tiled=True)
+        part = spatial[:, :, c * step:(c + 1) * step]
+        back = lax.all_to_all(part, "gx", split_axis=0, concat_axis=0, tiled=True)
         ext, img = lanes_inverse(back, source[:, :, c * step:(c + 1) * step])
         extrapolated.append(ext)
         images.append(img)

time: 321 us -> 291 us (0.907)
  local copies, waits for them, and re-layouts: 34.8 us -> 3.29 us
    all_to_all x3 -> x0, local copies, waits for them, and re-layouts: 16.5 us -> none  [the longest x2 9.29 us: body(): back = lax.all_to_all(part, 'gx', split_axis=1, concat_axis=2, tiled=True)]
    pallas_call x2 -> x0, local copies, waits for them, and re-layouts: 15 us -> none  [the longest x1 7.78 us: rows_shift(): pl.pallas_call(rows_kernel, grid=(width // block,), in_specs=[field_spec,...]
  transfers between devices with their start and end apart: 2 -> 2, of which waited for: 2 -> 2; matrix products, arithmetic and copies ran while one was open for 4% -> 5% of each run, Pallas kernels for 0% -> 0%
where the time goes in v1:
time: 291 us; the launch traced here: 290 us
  waiting for transfers between devices  129 us (44%)
  blocking collectives  98.5 us (34%)
  Pallas kernels  39.7 us (14%)
  other arithmetic  12.3 us (4%)
  starting transfers between devices  6.42 us (2%)
  local copies, waits for them, and re-layouts  3.29 us (1%)
    all_to_all x1, blocking collectives, body(): back = lax.all_to_all(part, 'gx', split_axis=0, concat_axis=0, tiled=True)  98.5 us
    all_to_all x1, waiting for transfers between devices, body(): lax.all_to_all(field, 'gx', split_axis=0, concat_axis=0, tiled=True)  81.4 us
    ppermute x1, waiting for transfers between devices, shifted(): return lax.ppermute(block, axis, route)  47.1 us
    pallas_call x1, Pallas kernels, lanes_forward(): pl.pallas_call(lanes_forward_kernel, grid=(step // block,), in_specs=[pl....  16.4 us
    pallas_call x1, Pallas kernels, rows_shift(): pl.pallas_call(rows_kernel, grid=(width // block,), in_specs=[field_spec,...  13.5 us
    pallas_call x1, Pallas kernels, lanes_inverse(): pl.pallas_call(lanes_inverse_kernel, grid=(step // block,), in_specs=[pl....  9.75 us
    mul x1, other arithmetic, propagator(): return (real_part * scale, imag_part * scale)  8.44 us
  transfers between devices with their start and end apart: 2, of which 2 were waited for; matrix products, arithmetic and copies ran while one was open for 5% of the time, Pallas kernels for 0%

profile of v1, /device:TPU:0, one launch (start us, length us, event | category | flops | bytes accessed | tf_op | source)
XLA Modules:
  0.0 290.1 jit_solution(2314752763829353436)
XLA Ops:
  0.6 1.3 collective-permute-start
  2.6 0.1 fusion.37
  2.6 0.6 fusion.44
  3.2 0.3 fusion.16
  3.5 0.7 pad_maximum_fusion.1.w_ref
  4.2 47.1 %collective-permute-done.hand_ref = bf16[2,256,2048]{2,1,0:T(8,128)(2,1)S(1)} collective-permute-done((bf16[2,256,2048]{2,1,0:T(8,128)(2,1)}, bf16[2,256,2048]{2,1,0:T(8,128)(2,1)S(1)}, u32[]{:S(2)}, u32[]{:S(2)}) %collective-permute-start) | collective-permute-done | bytes 2097184 | tf_op jit(solution)/shard_map/ppermute | solution.py:19
  51.3 0.0 copy-start
  51.3 1.3 copy-done
  52.6 16.4 %shard_map.77 = f32[8,2,256,256]{3,2,1,0:T(8,128)} custom-call(f32[1,1]{1,0:T(1,128)} %bitcast.5.base_ref, bf16[1,2,256,2048]{3,2,1,0:T(8,128)(2,1)} %wave_ref.1, bf16[2,256,2048]{2,1,0:T(8,128)(2,1)} %copy-done, bf16[1,2,256,2048]{3,2,1,0:T(8,128)(2,1)} %src_ref.3, f32[1,256,2048]{2,1,0:T(8,128)} %slow_ref.1, f32[1,256,2048]{2,1,0:T(8,128)} %refl_ref.1, ...), custom_call_target="tpu_custom_call" | custom-call | tf_op jit(solution)/shard_map/pallas_call | solution.py:292
  69.0 5.1 %all-to-all-start = ((f32[8,2,256,256]{3,2,1,0:T(8,128)}), f32[8,2,256,256]{3,2,1,0:T(8,128)}, u32[]{:S(2)}, u32[]{:S(2)}) async-start(f32[8,2,256,256]{3,2,1,0:T(8,128)} %shard_map.77), calls=%async_computation | async-start | bytes 8388608 | tf_op jit(solution)/shard_map/all_to_all | solution.py:386
  74.2 2.0 copy.8.tw_ref
  76.2 8.4 %fusion.2 = (f32[1,2048,256]{2,1,0:T(8,128)S(1)}, f32[1,2048,256]{2,1,0:T(8,128)S(1)}) fusion(f32[256]{0:T(256)S(1)} %fusion.43, f32[2048]{0:T(1024)S(1)} %fusion.33), kind=kLoop, calls=%fused_computation.5 | loop fusion | flops 4718592 | bytes 4203520 | tf_op jit(solution)/shard_map/mul | solution.py:352
  84.6 2.3 pad_maximum_fusion.p_ref
  86.9 81.4 %all-to-all-done.x_ref = f32[8,2,256,256]{3,2,1,0:T(8,128)} async-done(((f32[8,2,256,256]{3,2,1,0:T(8,128)}), f32[8,2,256,256]{3,2,1,0:T(8,128)}, u32[]{:S(2)}, u32[]{:S(2)}) %all-to-all-start) | async-done | bytes 4194336 | tf_op jit(solution)/shard_map/all_to_all | solution.py:386
  168.3 13.5 %shard_map.78 = f32[8,2,256,256]{3,2,1,0:T(8,128)} custom-call(f32[8,2,256,256]{3,2,1,0:T(8,128)} %all-to-all-done.x_ref, f32[2,2048,256]{2,1,0:T(8,128)} %pad_maximum_fusion.p_ref, f32[2,128,128]{2,1,0:T(8,128)} %pad_maximum_fusion.1.w_ref, f32[2,16,128,1]{3,2,1,0:T(8,128)} %copy.8.tw_ref), custom_call_target="tpu_custom_call" | custom-call | tf_op jit(solution)/shard_map/pallas_call | solution.py:188
  181.8 98.5 %all_to_all.10.x_ref = f32[8,2,256,256]{3,2,1,0:T(8,128)} all-to-all(f32[8,2,256,256]{3,2,1,0:T(8,128)} %shard_map.78), channel_id=1, replica_groups=mesh['slab'=4,'gx'=8] {'gx'}, dimensions={0} | all-to-all | bytes 8388608 | tf_op jit(solution)/shard_map/all_to_all | solution.py:396
  280.3 9.7 %shard_map.79 = (bf16[1,2,256,2048]{3,2,1,0:T(8,128)(2,1)}, f32[1,256,2048]{2,1,0:T(8,128)}) custom-call(f32[8,2,256,256]{3,2,1,0:T(8,128)} %all_to_all.10.x_ref, bf16[1,2,256,2048]{3,2,1,0:T(8,128)(2,1)} %src_ref.3, f32[2,128,128]{2,1,0:T(8,128)} %pad_maximum_fusion.1.w_ref, f32[2,16,128]{2,1,0:T(8,128)} %get-tuple-element.3.tw_ref), custom_call_target="tpu_custom_call" | custom-call | tf_op jit(solution)/shard_map/pallas_call | solution.py:315
  (2 shorter events, 0.0 us)
Async XLA Ops:
  0.6 50.7 %collective-permute-start = (bf16[2,256,2048]{2,1,0:T(8,128)(2,1)}, bf16[2,256,2048]{2,1,0:T(8,128)(2,1)S(1)}, u32[]{:S(2)}, u32[]{:S(2)}) collective-permute-start(bf16[2,256,2048]{2,1,0:T(8,128)(2,1)} %bitcast.6), channel_id=1, source_target_pairs={{8,0},{16,8},{24,16},{9,1},{17,9},{25,17},{10,2},{18,10},{26,18},{... | collective-permute-start | bytes 6291464 | tf_op jit(solution)/shard_map/ppermute | solution.py:19
  51.3 1.3 copy-start
  69.0 99.2 %all-to-all-start = ((f32[8,2,256,256]{3,2,1,0:T(8,128)}), f32[8,2,256,256]{3,2,1,0:T(8,128)}, u32[]{:S(2)}, u32[]{:S(2)}) async-start(f32[8,2,256,256]{3,2,1,0:T(8,128)} %shard_map.77), calls=%async_computation | async-start | bytes 8388608 | tf_op jit(solution)/shard_map/all_to_all | solution.py:386

commit v2 on v1

--- a/solution.py
+++ b/solution.py
@@ -139,18 +139,23 @@
     )
 
 
-def rows_kernel(x_ref, p_ref, w_ref, tw_ref, o_ref):
+def rows_kernel(*refs):
+    x_refs = refs[:-4]
+    p_ref, w_ref, tw_ref, o_ref = refs[-4:]
     outer = tw_ref.shape[1]
     inner = tw_ref.shape[2]
-    count = x_ref.shape[2]
+    step = x_refs[0].shape[2]
+    count = step * len(x_refs)
 
     def place(a):
         return (a * inner) // count, slice((a * inner) % count, (a * inner) % count + inner)
 
     slabs = []
     for a in range(outer):
-        origin, rows = place(a)
-        slabs.append((x_ref[origin, 0, rows, :], x_ref[origin, 1, rows, :]))
+        origin = (a * inner) // count
+        part = x_refs[((a * inner) % count) // step]
+        first = (a * inner) % step
+        slabs.append((part[origin, 0, first:first + inner, :], part[origin, 1, first:first + inner, :]))
     spec = fft_slabs(slabs, -1)
     wr = w_ref[0]
     wi = w_ref[1]
@@ -176,27 +181,26 @@
 
 
 def rows_shift(turned, factor):
-    groups, _, count, width = turned.shape
-    length = groups * count
+    groups, _, step, width = turned[0].shape
+    length = groups * step * len(turned)
     outer, inner = factor_pair(length)
     block = min(width, 128)
     table = dft_table(inner, -1.0)
     turn = twiddle_table(outer, inner, length, -1.0)
     table = jnp.stack(table)
     turn = jnp.stack(turn)[..., None]
-    field_spec = pl.BlockSpec((groups, 2, count, block), lambda j: (0, 0, 0, j))
+    field_spec = pl.BlockSpec((groups, 2, step, block), lambda j: (0, 0, 0, j))
     return pl.pallas_call(
         rows_kernel,
         grid=(width // block,),
-        in_specs=[
-            field_spec,
+        in_specs=[field_spec] * len(turned) + [
             pl.BlockSpec((2, length, block), lambda j: (0, 0, j)),
             pl.BlockSpec((2, inner, inner), lambda j: (0, 0, 0)),
             pl.BlockSpec((2, outer, inner, 1), lambda j: (0, 0, 0, 0)),
         ],
-        out_specs=field_spec,
-        out_shape=jax.ShapeDtypeStruct(turned.shape, jnp.float32),
-    )(turned, factor, table, turn)
+        out_specs=pl.BlockSpec((groups, 2, step * len(turned), block), lambda j: (0, 0, 0, j)),
+        out_shape=jax.ShapeDtypeStruct((groups, 2, step * len(turned), width), jnp.float32),
+    )(*turned, factor, table, turn)
 
 
 def lanes_forward_kernel(base_ref, wave_ref, hand_ref, src_ref, slow_ref, refl_ref, w_ref, tw_ref, o_ref):
@@ -352,7 +356,7 @@
     return (real_part * scale, imag_part * scale)
 
 
-CHUNKS = 1
+CHUNKS = 2
 
 
 def lens_rows(wave, handed, source, slow, refl, base):
@@ -384,20 +388,14 @@
         handed = shifted(boundary[0, :, rows], "slab", -1)
         field = lanes_forward(wavefield, handed, source, slowness, reflectivity, base, c * step, step, groups)
         pieces.append(lax.all_to_all(field, "gx", split_axis=0, concat_axis=0, tiled=True))
-    turned = pieces[0] if chunks == 1 else jnp.concatenate(pieces, axis=2)
+    if (step % factor_pair(total_rows)[1]) != 0:
+        pieces = [jnp.concatenate(pieces, axis=2)]
     freq_row = permuted_freq(jnp.arange(total_rows, dtype=jnp.int32), total_rows)
     freq_col = permuted_freq(device * width + jnp.arange(width, dtype=jnp.int32), columns)
     factor = propagator(freq_row[:, None], freq_col[None, :], base, scale)
-    spatial = rows_shift(turned, jnp.stack(factor))
-    extrapolated = []
-    images = []
-    for c in range(chunks):
-        part = spatial[:, :, c * step:(c + 1) * step]
-        back = lax.all_to_all(part, "gx", split_axis=0, concat_axis=0, tiled=True)
-        ext, img = lanes_inverse(back, source[:, :, c * step:(c + 1) * step])
-        extrapolated.append(ext)
-        images.append(img)
-    return (jnp.concatenate(extrapolated, axis=2), jnp.concatenate(images, axis=1))
+    spatial = rows_shift(pieces, jnp.stack(factor))
+    back = lax.all_to_all(spatial, "gx", split_axis=0, concat_axis=0, tiled=True)
+    return lanes_inverse(back, source)
 
 
 def solution(mesh):

time: 291 us -> 273 us (0.938)
  waiting for transfers between devices: 129 us -> 98.2 us
  starting transfers between devices: 6.42 us -> 12.2 us
  local copies, waits for them, and re-layouts: 3.29 us -> 7.95 us
    all_to_all x1 -> x2, waiting for transfers between devices: 81.4 us -> 46.7 us  [body(): lax.all_to_all(field, 'gx', split_axis=0, concat_axis=0, tiled=True)]
    all_to_all x1 -> x2, starting transfers between devices: 5.13 us -> 9.67 us  [body(): lax.all_to_all(field, 'gx', split_axis=0, concat_axis=0, tiled=True)]
    ppermute x1 -> x2, waiting for transfers between devices: 47.1 us -> 51.5 us  [shifted(): return lax.ppermute(block, axis, route)]
    pallas_call x1 -> x2, Pallas kernels: 16.4 us -> 18.5 us  [lanes_forward(): pl.pallas_call(lanes_forward_kernel, grid=(step // block,), in_specs=[pl....]
  transfers between devices with their start and end apart: 2 -> 4, of which waited for: 2 -> 4; matrix products, arithmetic and copies ran while one was open for 5% -> 5% of each run, Pallas kernels for 0% -> 3%
where the time goes in v2:
time: 273 us
  blocking collectives  98.5 us (36%)
  waiting for transfers between devices  98.2 us (36%)
  Pallas kernels  42.2 us (15%)
  other arithmetic  12.3 us (5%)
  starting transfers between devices  12.2 us (4%)
  local copies, waits for them, and re-layouts  7.95 us (3%)
    all_to_all x1, blocking collectives, body(): lax.all_to_all(spatial, 'gx', split_axis=0, concat_axis=0, tiled=True)  98.5 us
    ppermute x2, waiting for transfers between devices, shifted(): return lax.ppermute(block, axis, route)  51.5 us
    all_to_all x2, waiting for transfers between devices, body(): lax.all_to_all(field, 'gx', split_axis=0, concat_axis=0, tiled=True)  46.7 us
    pallas_call x2, Pallas kernels, lanes_forward(): pl.pallas_call(lanes_forward_kernel, grid=(step // block,), in_specs=[pl....  18.5 us
    pallas_call x1, Pallas kernels, rows_shift(): pl.pallas_call(rows_kernel, grid=(width // block,), in_specs=[field_spec]...  13.9 us
    pallas_call x1, Pallas kernels, lanes_inverse(): pl.pallas_call(lanes_inverse_kernel, grid=(step // block,), in_specs=[pl....  9.75 us
    all_to_all x2, starting transfers between devices, body(): lax.all_to_all(field, 'gx', split_axis=0, concat_axis=0, tiled=True)  9.67 us
    mul x1, other arithmetic, propagator(): return (real_part * scale, imag_part * scale)  8.44 us
  transfers between devices with their start and end apart: 4, of which 4 were waited for; matrix products, arithmetic and copies ran while one was open for 5% of the time, Pallas kernels for 3%

profile of v2, /device:TPU:0, one launch (start us, length us, event | category | flops | bytes accessed | tf_op | source)
XLA Modules:
  0.0 272.7 jit_solution(6872563174200258758)
XLA Ops:
  0.6 2.7 slice_bitcast_fusion
  3.3 1.3 collective-permute-start.1
  5.3 0.1 fusion.37
  5.3 0.6 fusion.44
  5.9 0.3 fusion.16
  6.2 0.7 pad_maximum_fusion.1.w_ref.refs_3_
  6.9 24.4 %collective-permute-done.1.hand_ref = bf16[2,128,2048]{2,1,0:T(8,128)(2,1)S(1)} collective-permute-done((bf16[2,128,2048]{2,1,0:T(8,128)(2,1)S(1)}, bf16[2,128,2048]{2,1,0:T(8,128)(2,1)S(1)}, u32[]{:S(2)}, u32[]{:S(2)}) %collective-permute-start.1) | collective-permute-done | bytes 1048608 | tf_op jit(solution)/shard_map/ppermute | solution.py:19
  31.3 0.0 copy-start.1
  31.3 1.0 copy-done.1
  32.3 9.3 %shard_map.78 = f32[8,2,128,256]{3,2,1,0:T(8,128)} custom-call(f32[1,1]{1,0:T(1,128)} %bitcast.9.base_ref, bf16[1,2,256,2048]{3,2,1,0:T(8,128)(2,1)} %wave_ref.3, bf16[2,128,2048]{2,1,0:T(8,128)(2,1)} %copy-done.1, bf16[1,2,256,2048]{3,2,1,0:T(8,128)(2,1)} %src_ref.5, f32[1,256,2048]{2,1,0:T(8,128)} %slow_ref.3, f32[1,256,2048]{2,1,0:T(8,128)} %refl_ref.3, ...), custom_call_target="tpu_custom_call" | custom-call | tf_op jit(solution)/shard_map/pallas_call | solution.py:296
  41.6 5.1 %all-to-all-start.1 = ((f32[8,2,128,256]{3,2,1,0:T(8,128)}), f32[8,2,128,256]{3,2,1,0:T(8,128)S(1)}, u32[]{:S(2)}, u32[]{:S(2)}) async-start(f32[8,2,128,256]{3,2,1,0:T(8,128)} %shard_map.78), calls=%async_computation.1 | async-start | bytes 4194304 | tf_op jit(solution)/shard_map/all_to_all | solution.py:390
  46.7 1.3 collective-permute-start
  48.0 27.0 %collective-permute-done.hand_ref = bf16[2,128,2048]{2,1,0:T(8,128)(2,1)S(1)} collective-permute-done((bf16[2,128,2048]{2,1,0:T(8,128)(2,1)}, bf16[2,128,2048]{2,1,0:T(8,128)(2,1)S(1)}, u32[]{:S(2)}, u32[]{:S(2)}) %collective-permute-start) | collective-permute-done | bytes 1048608 | tf_op jit(solution)/shard_map/ppermute | solution.py:19
  75.0 0.0 copy-start.2
  75.0 1.0 copy-done.2
  76.0 9.2 %shard_map.77 = f32[8,2,128,256]{3,2,1,0:T(8,128)} custom-call(f32[1,1]{1,0:T(1,128)} %bitcast.8.base_ref, bf16[1,2,256,2048]{3,2,1,0:T(8,128)(2,1)} %wave_ref.3, bf16[2,128,2048]{2,1,0:T(8,128)(2,1)} %copy-done.2, bf16[1,2,256,2048]{3,2,1,0:T(8,128)(2,1)} %src_ref.5, f32[1,256,2048]{2,1,0:T(8,128)} %slow_ref.3, f32[1,256,2048]{2,1,0:T(8,128)} %refl_ref.3, ...), custom_call_target="tpu_custom_call" | custom-call | tf_op jit(solution)/shard_map/pallas_call | solution.py:296
  85.2 10.6 %all-to-all-done.1.refs_1_ = f32[8,2,128,256]{3,2,1,0:T(8,128)S(1)} async-done(((f32[8,2,128,256]{3,2,1,0:T(8,128)}), f32[8,2,128,256]{3,2,1,0:T(8,128)S(1)}, u32[]{:S(2)}, u32[]{:S(2)}) %all-to-all-start.1) | async-done | bytes 2097184 | tf_op jit(solution)/shard_map/all_to_all | solution.py:390
  95.7 0.0 copy-start
  95.7 1.3 copy-done
  97.1 4.6 %all-to-all-start = ((f32[8,2,128,256]{3,2,1,0:T(8,128)}), f32[8,2,128,256]{3,2,1,0:T(8,128)}, u32[]{:S(2)}, u32[]{:S(2)}) async-start(f32[8,2,128,256]{3,2,1,0:T(8,128)} %shard_map.77), calls=%async_computation | async-start | bytes 4194304 | tf_op jit(solution)/shard_map/all_to_all | solution.py:390
  101.6 2.0 copy.8.refs_4_
  103.6 8.4 %fusion.2 = (f32[1,2048,256]{2,1,0:T(8,128)S(1)}, f32[1,2048,256]{2,1,0:T(8,128)S(1)}) fusion(f32[256]{0:T(256)S(1)} %fusion.43, f32[2048]{0:T(1024)S(1)} %fusion.33), kind=kLoop, calls=%fused_computation.5 | loop fusion | flops 4718592 | bytes 4203520 | tf_op jit(solution)/shard_map/mul | solution.py:356
  112.1 2.2 pad_maximum_fusion.refs_2_
  114.3 36.2 %all-to-all-done.refs_0_ = f32[8,2,128,256]{3,2,1,0:T(8,128)} async-done(((f32[8,2,128,256]{3,2,1,0:T(8,128)}), f32[8,2,128,256]{3,2,1,0:T(8,128)}, u32[]{:S(2)}, u32[]{:S(2)}) %all-to-all-start) | async-done | bytes 2097184 | tf_op jit(solution)/shard_map/all_to_all | solution.py:390
  150.5 13.9 %shard_map.79 = f32[8,2,256,256]{3,2,1,0:T(8,128)} custom-call(f32[8,2,128,256]{3,2,1,0:T(8,128)} %all-to-all-done.refs_0_, f32[8,2,128,256]{3,2,1,0:T(8,128)} %copy-done, f32[2,2048,256]{2,1,0:T(8,128)} %pad_maximum_fusion.refs_2_, f32[2,128,128]{2,1,0:T(8,128)} %pad_maximum_fusion.1.w_ref.refs_3_, f32[2,16,128,1]{3,2,1,0:T(8,128)} %copy.8.refs_4_), custom_call_target="tpu_custom_call" | custom-call | tf_op jit(solution)/shard_map/pallas_call | solution.py:193
  164.4 98.5 %all_to_all.15.x_ref = f32[8,2,256,256]{3,2,1,0:T(8,128)} all-to-all(f32[8,2,256,256]{3,2,1,0:T(8,128)} %shard_map.79), channel_id=1, replica_groups=mesh['slab'=4,'gx'=8] {'gx'}, dimensions={0} | all-to-all | bytes 8388608 | tf_op jit(solution)/shard_map/all_to_all | solution.py:397
  262.9 9.7 %shard_map.80 = (bf16[1,2,256,2048]{3,2,1,0:T(8,128)(2,1)}, f32[1,256,2048]{2,1,0:T(8,128)}) custom-call(f32[8,2,256,256]{3,2,1,0:T(8,128)} %all_to_all.15.x_ref, bf16[1,2,256,2048]{3,2,1,0:T(8,128)(2,1)} %src_ref.5, f32[2,128,128]{2,1,0:T(8,128)} %pad_maximum_fusion.1.w_ref.refs_3_, f32[2,16,128]{2,1,0:T(8,128)} %get-tuple-element.5.tw_ref), custom_call_target="tpu_custom_call" | custom-call | tf_op jit(solution)/shard_map/pallas_call | solution.py:319
  (2 shorter events, 0.0 us)
Async XLA Ops:
  3.3 28.0 %collective-permute-start.1 = (bf16[2,128,2048]{2,1,0:T(8,128)(2,1)S(1)}, bf16[2,128,2048]{2,1,0:T(8,128)(2,1)S(1)}, u32[]{:S(2)}, u32[]{:S(2)}) collective-permute-start(bf16[2,128,2048]{2,1,0:T(8,128)(2,1)S(1)} %get-tuple-element.2), channel_id=1, source_target_pairs={{8,0},{16,8},{24,16},{9,1},{17,9},{25,17},{10,2},{18,10},{26,18},{... | collective-permute-start | bytes 3145736 | tf_op jit(solution)/shard_map/ppermute | solution.py:19
  31.3 1.0 copy-start.1
  41.6 54.2 %all-to-all-start.1 = ((f32[8,2,128,256]{3,2,1,0:T(8,128)}), f32[8,2,128,256]{3,2,1,0:T(8,128)S(1)}, u32[]{:S(2)}, u32[]{:S(2)}) async-start(f32[8,2,128,256]{3,2,1,0:T(8,128)} %shard_map.78), calls=%async_computation.1 | async-start | bytes 4194304 | tf_op jit(solution)/shard_map/all_to_all | solution.py:390
  46.7 28.3 %collective-permute-start = (bf16[2,128,2048]{2,1,0:T(8,128)(2,1)}, bf16[2,128,2048]{2,1,0:T(8,128)(2,1)S(1)}, u32[]{:S(2)}, u32[]{:S(2)}) collective-permute-start(bf16[2,128,2048]{2,1,0:T(8,128)(2,1)} %get-tuple-element.3), channel_id=1, source_target_pairs={{8,0},{16,8},{24,16},{9,1},{17,9},{25,17},{10,2},{18,10},{26,18},{... | collective-permute-start | bytes 3145736 | tf_op jit(solution)/shard_map/ppermute | solution.py:19
  75.0 1.0 copy-start.2
  95.7 1.3 copy-start
  97.1 53.4 %all-to-all-start = ((f32[8,2,128,256]{3,2,1,0:T(8,128)}), f32[8,2,128,256]{3,2,1,0:T(8,128)}, u32[]{:S(2)}, u32[]{:S(2)}) async-start(f32[8,2,128,256]{3,2,1,0:T(8,128)} %shard_map.77), calls=%async_computation | async-start | bytes 4194304 | tf_op jit(solution)/shard_map/all_to_all | solution.py:390

commit v3 on v2

--- a/solution.py
+++ b/solution.py
@@ -395,7 +395,7 @@
     factor = propagator(freq_row[:, None], freq_col[None, :], base, scale)
     spatial = rows_shift(pieces, jnp.stack(factor))
     back = lax.all_to_all(spatial, "gx", split_axis=0, concat_axis=0, tiled=True)
-    return lanes_inverse(back, source)
+    return lanes_inverse(back, source.astype(jnp.float32))
 
 
 def solution(mesh):

time: 273 us -> 274 us (level)
  blocking collectives: 98.5 us -> 0 us
  waiting for transfers between devices: 98.2 us -> 190 us
  starting transfers between devices: 12.2 us -> 16.9 us
    all_to_all x1 -> x0, blocking collectives: 98.5 us -> none  [body(): lax.all_to_all(spatial, 'gx', split_axis=0, concat_axis=0, tiled=True)]
    all_to_all x0 -> x1, waiting for transfers between devices: none -> 91.5 us  [body(): lax.all_to_all(spatial, 'gx', split_axis=0, concat_axis=0, tiled=True)]
    all_to_all x0 -> x1, starting transfers between devices: none -> 4.69 us  [body(): lax.all_to_all(spatial, 'gx', split_axis=0, concat_axis=0, tiled=True)]
  transfers between devices with their start and end apart: 4 -> 5, of which waited for: 4 -> 5; matrix products, arithmetic and copies ran while one was open for 5% -> 6% of each run, Pallas kernels for 3% -> 3%
where the time goes in v3:
time: 274 us; the launch traced here: 273 us
  waiting for transfers between devices  190 us (69%)
  Pallas kernels  42.6 us (16%)
  starting transfers between devices  16.9 us (6%)
  other arithmetic  14.8 us (5%)
  local copies, waits for them, and re-layouts  7.96 us (3%)
    all_to_all x1, waiting for transfers between devices, body(): lax.all_to_all(spatial, 'gx', split_axis=0, concat_axis=0, tiled=True)  91.5 us
    ppermute x2, waiting for transfers between devices, shifted(): return lax.ppermute(block, axis, route)  51.5 us
    all_to_all x2, waiting for transfers between devices, body(): lax.all_to_all(field, 'gx', split_axis=0, concat_axis=0, tiled=True)  46.7 us
    pallas_call x2, Pallas kernels, lanes_forward(): pl.pallas_call(lanes_forward_kernel, grid=(step // block,), in_specs=[pl....  18.5 us
    pallas_call x1, Pallas kernels, rows_shift(): pl.pallas_call(rows_kernel, grid=(width // block,), in_specs=[field_spec]...  13.9 us
    pallas_call x1, Pallas kernels, lanes_inverse(): pl.pallas_call(lanes_inverse_kernel, grid=(step // block,), in_specs=[pl....  10.1 us
    all_to_all x2, starting transfers between devices, body(): lax.all_to_all(field, 'gx', split_axis=0, concat_axis=0, tiled=True)  9.66 us
    mul x1, other arithmetic, propagator(): return (real_part * scale, imag_part * scale)  8.44 us
  transfers between devices with their start and end apart: 5, of which 5 were waited for; matrix products, arithmetic and copies ran while one was open for 6% of the time, Pallas kernels for 3%

profile of v3, /device:TPU:0, one launch (start us, length us, event | category | flops | bytes accessed | tf_op | source)
XLA Modules:
  0.0 273.3 jit_solution(725093128013623188)
XLA Ops:
  0.6 2.7 slice_bitcast_fusion
  3.3 1.3 collective-permute-start.1
  5.3 0.1 fusion.37
  5.3 0.6 fusion.44
  5.9 0.3 fusion.16
  6.2 0.7 pad_maximum_fusion.1.w_ref.refs_3_
  6.9 24.4 %collective-permute-done.1.hand_ref = bf16[2,128,2048]{2,1,0:T(8,128)(2,1)S(1)} collective-permute-done((bf16[2,128,2048]{2,1,0:T(8,128)(2,1)S(1)}, bf16[2,128,2048]{2,1,0:T(8,128)(2,1)S(1)}, u32[]{:S(2)}, u32[]{:S(2)}) %collective-permute-start.1) | collective-permute-done | bytes 1048608 | tf_op jit(solution)/shard_map/ppermute | solution.py:19
  31.3 0.0 copy-start.2
  31.3 1.0 copy-done.2
  32.3 9.3 %shard_map.78 = f32[8,2,128,256]{3,2,1,0:T(8,128)} custom-call(f32[1,1]{1,0:T(1,128)} %bitcast.9.base_ref, bf16[1,2,256,2048]{3,2,1,0:T(8,128)(2,1)} %wave_ref.3, bf16[2,128,2048]{2,1,0:T(8,128)(2,1)} %copy-done.2, bf16[1,2,256,2048]{3,2,1,0:T(8,128)(2,1)} %src_ref.3, f32[1,256,2048]{2,1,0:T(8,128)} %slow_ref.3, f32[1,256,2048]{2,1,0:T(8,128)} %refl_ref.3, ...), custom_call_target="tpu_custom_call" | custom-call | tf_op jit(solution)/shard_map/pallas_call | solution.py:296
  41.6 5.1 %all-to-all-start.1 = ((f32[8,2,128,256]{3,2,1,0:T(8,128)}), f32[8,2,128,256]{3,2,1,0:T(8,128)S(1)}, u32[]{:S(2)}, u32[]{:S(2)}) async-start(f32[8,2,128,256]{3,2,1,0:T(8,128)} %shard_map.78), calls=%async_computation.1 | async-start | bytes 4194304 | tf_op jit(solution)/shard_map/all_to_all | solution.py:390
  46.7 1.3 collective-permute-start
  48.0 27.0 %collective-permute-done.hand_ref = bf16[2,128,2048]{2,1,0:T(8,128)(2,1)S(1)} collective-permute-done((bf16[2,128,2048]{2,1,0:T(8,128)(2,1)}, bf16[2,128,2048]{2,1,0:T(8,128)(2,1)S(1)}, u32[]{:S(2)}, u32[]{:S(2)}) %collective-permute-start) | collective-permute-done | bytes 1048608 | tf_op jit(solution)/shard_map/ppermute | solution.py:19
  75.0 0.0 copy-start.3
  75.0 1.0 copy-done.3
  76.0 9.2 %shard_map.77 = f32[8,2,128,256]{3,2,1,0:T(8,128)} custom-call(f32[1,1]{1,0:T(1,128)} %bitcast.8.base_ref, bf16[1,2,256,2048]{3,2,1,0:T(8,128)(2,1)} %wave_ref.3, bf16[2,128,2048]{2,1,0:T(8,128)(2,1)} %copy-done.3, bf16[1,2,256,2048]{3,2,1,0:T(8,128)(2,1)} %src_ref.3, f32[1,256,2048]{2,1,0:T(8,128)} %slow_ref.3, f32[1,256,2048]{2,1,0:T(8,128)} %refl_ref.3, ...), custom_call_target="tpu_custom_call" | custom-call | tf_op jit(solution)/shard_map/pallas_call | solution.py:296
  85.2 10.6 %all-to-all-done.1.refs_1_ = f32[8,2,128,256]{3,2,1,0:T(8,128)S(1)} async-done(((f32[8,2,128,256]{3,2,1,0:T(8,128)}), f32[8,2,128,256]{3,2,1,0:T(8,128)S(1)}, u32[]{:S(2)}, u32[]{:S(2)}) %all-to-all-start.1) | async-done | bytes 2097184 | tf_op jit(solution)/shard_map/all_to_all | solution.py:390
  95.7 0.0 copy-start.1
  95.7 1.3 copy-done.1
  97.1 4.5 %all-to-all-start = ((f32[8,2,128,256]{3,2,1,0:T(8,128)}), f32[8,2,128,256]{3,2,1,0:T(8,128)}, u32[]{:S(2)}, u32[]{:S(2)}) async-start(f32[8,2,128,256]{3,2,1,0:T(8,128)} %shard_map.77), calls=%async_computation | async-start | bytes 4194304 | tf_op jit(solution)/shard_map/all_to_all | solution.py:390
  101.6 2.0 copy.8.refs_4_
  103.6 8.4 %fusion.2 = (f32[1,2048,256]{2,1,0:T(8,128)S(1)}, f32[1,2048,256]{2,1,0:T(8,128)S(1)}) fusion(f32[256]{0:T(256)S(1)} %fusion.43, f32[2048]{0:T(1024)S(1)} %fusion.33), kind=kLoop, calls=%fused_computation.5 | loop fusion | flops 4718592 | bytes 4203520 | tf_op jit(solution)/shard_map/mul | solution.py:356
  112.1 2.3 pad_maximum_fusion.refs_2_
  114.3 36.2 %all-to-all-done.refs_0_ = f32[8,2,128,256]{3,2,1,0:T(8,128)} async-done(((f32[8,2,128,256]{3,2,1,0:T(8,128)}), f32[8,2,128,256]{3,2,1,0:T(8,128)}, u32[]{:S(2)}, u32[]{:S(2)}) %all-to-all-start) | async-done | bytes 2097184 | tf_op jit(solution)/shard_map/all_to_all | solution.py:390
  150.5 13.9 %shard_map.79 = f32[8,2,256,256]{3,2,1,0:T(8,128)} custom-call(f32[8,2,128,256]{3,2,1,0:T(8,128)} %all-to-all-done.refs_0_, f32[8,2,128,256]{3,2,1,0:T(8,128)} %copy-done.1, f32[2,2048,256]{2,1,0:T(8,128)} %pad_maximum_fusion.refs_2_, f32[2,128,128]{2,1,0:T(8,128)} %pad_maximum_fusion.1.w_ref.refs_3_, f32[2,16,128,1]{3,2,1,0:T(8,128)} %copy.8.refs_4_), custom_call_target="tpu_custom_call" | custom-call | tf_op jit(solution)/shard_map/pallas_call | solution.py:193
  164.4 0.0 copy-start
  164.4 4.7 %all-to-all-start.2 = ((f32[8,2,256,256]{3,2,1,0:T(8,128)}), f32[8,2,256,256]{3,2,1,0:T(8,128)}, u32[]{:S(2)}, u32[]{:S(2)}) async-start(f32[8,2,256,256]{3,2,1,0:T(8,128)} %shard_map.79), calls=%async_computation.2 | async-start | bytes 8388608 | tf_op jit(solution)/shard_map/all_to_all | solution.py:397
  169.1 0.0 copy-done
  169.2 2.5 convert_element_type.59.src_ref
  171.7 91.5 %all-to-all-done.2.x_ref = f32[8,2,256,256]{3,2,1,0:T(8,128)} async-done(((f32[8,2,256,256]{3,2,1,0:T(8,128)}), f32[8,2,256,256]{3,2,1,0:T(8,128)}, u32[]{:S(2)}, u32[]{:S(2)}) %all-to-all-start.2) | async-done | bytes 4194336 | tf_op jit(solution)/shard_map/all_to_all | solution.py:397
  263.1 10.1 %shard_map.80 = (bf16[1,2,256,2048]{3,2,1,0:T(8,128)(2,1)}, f32[1,256,2048]{2,1,0:T(8,128)}) custom-call(f32[8,2,256,256]{3,2,1,0:T(8,128)} %all-to-all-done.2.x_ref, f32[1,2,256,2048]{3,2,1,0:T(8,128)} %convert_element_type.59.src_ref, f32[2,128,128]{2,1,0:T(8,128)} %pad_maximum_fusion.1.w_ref.refs_3_, f32[2,16,128]{2,1,0:T(8,128)} %get-tuple-element.5.tw_ref), custom_call_target="tpu_custom_call" | custom-call | tf_op jit(solution)/shard_map/pallas_call | solution.py:319
  (2 shorter events, 0.0 us)
Async XLA Ops:
  3.3 28.0 %collective-permute-start.1 = (bf16[2,128,2048]{2,1,0:T(8,128)(2,1)S(1)}, bf16[2,128,2048]{2,1,0:T(8,128)(2,1)S(1)}, u32[]{:S(2)}, u32[]{:S(2)}) collective-permute-start(bf16[2,128,2048]{2,1,0:T(8,128)(2,1)S(1)} %get-tuple-element.2), channel_id=1, source_target_pairs={{8,0},{16,8},{24,16},{9,1},{17,9},{25,17},{10,2},{18,10},{26,18},{... | collective-permute-start | bytes 3145736 | tf_op jit(solution)/shard_map/ppermute | solution.py:19
  31.3 1.0 copy-start.2
  41.6 54.2 %all-to-all-start.1 = ((f32[8,2,128,256]{3,2,1,0:T(8,128)}), f32[8,2,128,256]{3,2,1,0:T(8,128)S(1)}, u32[]{:S(2)}, u32[]{:S(2)}) async-start(f32[8,2,128,256]{3,2,1,0:T(8,128)} %shard_map.78), calls=%async_computation.1 | async-start | bytes 4194304 | tf_op jit(solution)/shard_map/all_to_all | solution.py:390
  46.7 28.3 %collective-permute-start = (bf16[2,128,2048]{2,1,0:T(8,128)(2,1)}, bf16[2,128,2048]{2,1,0:T(8,128)(2,1)S(1)}, u32[]{:S(2)}, u32[]{:S(2)}) collective-permute-start(bf16[2,128,2048]{2,1,0:T(8,128)(2,1)} %get-tuple-element.3), channel_id=1, source_target_pairs={{8,0},{16,8},{24,16},{9,1},{17,9},{25,17},{10,2},{18,10},{26,18},{... | collective-permute-start | bytes 3145736 | tf_op jit(solution)/shard_map/ppermute | solution.py:19
  75.0 1.0 copy-start.3
  95.7 1.3 copy-start.1
  97.1 53.4 %all-to-all-start = ((f32[8,2,128,256]{3,2,1,0:T(8,128)}), f32[8,2,128,256]{3,2,1,0:T(8,128)}, u32[]{:S(2)}, u32[]{:S(2)}) async-start(f32[8,2,128,256]{3,2,1,0:T(8,128)} %shard_map.77), calls=%async_computation | async-start | bytes 4194304 | tf_op jit(solution)/shard_map/all_to_all | solution.py:390
  164.4 4.7 %copy-start = (bf16[1,2,256,2048]{3,2,1,0:T(8,128)(2,1)S(1)}, bf16[1,2,256,2048]{3,2,1,0:T(8,128)(2,1)}, u32[]{:S(2)}) copy-start(bf16[1,2,256,2048]{3,2,1,0:T(8,128)(2,1)} %src_ref.3) | copy-start | bytes 6291460
  164.4 98.7 %all-to-all-start.2 = ((f32[8,2,256,256]{3,2,1,0:T(8,128)}), f32[8,2,256,256]{3,2,1,0:T(8,128)}, u32[]{:S(2)}, u32[]{:S(2)}) async-start(f32[8,2,256,256]{3,2,1,0:T(8,128)} %shard_map.79), calls=%async_computation.2 | async-start | bytes 8388608 | tf_op jit(solution)/shard_map/all_to_all | solution.py:397

commit v4 on v2

--- a/solution.py
+++ b/solution.py
@@ -144,18 +144,30 @@
     p_ref, w_ref, tw_ref, o_ref = refs[-4:]
     outer = tw_ref.shape[1]
     inner = tw_ref.shape[2]
-    step = x_refs[0].shape[2]
-    count = step * len(x_refs)
+    count = sum(ref.shape[2] for ref in x_refs)
 
     def place(a):
         return (a * inner) // count, slice((a * inner) % count, (a * inner) % count + inner)
 
+    sizes = [ref.shape[2] for ref in x_refs]
+    starts = [sum(sizes[:i]) for i in range(len(sizes))]
     slabs = []
     for a in range(outer):
         origin = (a * inner) // count
-        part = x_refs[((a * inner) % count) // step]
-        first = (a * inner) % step
-        slabs.append((part[origin, 0, first:first + inner, :], part[origin, 1, first:first + inner, :]))
+        low = (a * inner) % count
+        pieces = []
+        for ref, start, size in zip(x_refs, starts, sizes):
+            top = min(low + inner, start + size)
+            bottom = max(low, start)
+            if top > bottom:
+                pieces.append((ref[origin, 0, bottom - start:top - start, :], ref[origin, 1, bottom - start:top - start, :]))
+        if len(pieces) == 1:
+            slabs.append(pieces[0])
+        else:
+            slabs.append((
+                jnp.concatenate([p[0] for p in pieces], axis=0),
+                jnp.concatenate([p[1] for p in pieces], axis=0),
+            ))
     spec = fft_slabs(slabs, -1)
     wr = w_ref[0]
     wi = w_ref[1]
@@ -181,25 +193,25 @@
 
 
 def rows_shift(turned, factor):
-    groups, _, step, width = turned[0].shape
-    length = groups * step * len(turned)
+    groups, _, _, width = turned[0].shape
+    count = sum(piece.shape[2] for piece in turned)
+    length = groups * count
     outer, inner = factor_pair(length)
     block = min(width, 128)
     table = dft_table(inner, -1.0)
     turn = twiddle_table(outer, inner, length, -1.0)
     table = jnp.stack(table)
     turn = jnp.stack(turn)[..., None]
-    field_spec = pl.BlockSpec((groups, 2, step, block), lambda j: (0, 0, 0, j))
     return pl.pallas_call(
         rows_kernel,
         grid=(width // block,),
-        in_specs=[field_spec] * len(turned) + [
+        in_specs=[pl.BlockSpec((groups, 2, piece.shape[2], block), lambda j: (0, 0, 0, j)) for piece in turned] + [
             pl.BlockSpec((2, length, block), lambda j: (0, 0, j)),
             pl.BlockSpec((2, inner, inner), lambda j: (0, 0, 0)),
             pl.BlockSpec((2, outer, inner, 1), lambda j: (0, 0, 0, 0)),
         ],
-        out_specs=pl.BlockSpec((groups, 2, step * len(turned), block), lambda j: (0, 0, 0, j)),
-        out_shape=jax.ShapeDtypeStruct((groups, 2, step * len(turned), width), jnp.float32),
+        out_specs=pl.BlockSpec((groups, 2, count, block), lambda j: (0, 0, 0, j)),
+        out_shape=jax.ShapeDtypeStruct((groups, 2, count, width), jnp.float32),
     )(*turned, factor, table, turn)
 
 
@@ -356,9 +368,6 @@
     return (real_part * scale, imag_part * scale)
 
 
-CHUNKS = 2
-
-
 def lens_rows(wave, handed, source, slow, refl, base):
     wave = wave.astype(jnp.float32)
     handed = handed.astype(jnp.float32)
@@ -374,8 +383,11 @@
 def body(wavefield, boundary, source, slowness, reflectivity, ref_slowness):
     count = wavefield.shape[2]
     columns = wavefield.shape[3]
-    chunks = CHUNKS if count % CHUNKS == 0 else 1
-    step = count // chunks
+    eighth = count // 8
+    if count % 8 == 0 and eighth % 8 == 0:
+        bounds = [0, eighth, 3 * eighth, count]
+    else:
+        bounds = [0, count]
     groups = lax.axis_size("gx")
     device = lax.axis_index("gx")
     total_rows = count * groups
@@ -383,13 +395,10 @@
     scale = 1.0 / (total_rows * columns)
     base = ref_slowness[0]
     pieces = []
-    for c in range(chunks):
-        rows = slice(c * step, (c + 1) * step)
-        handed = shifted(boundary[0, :, rows], "slab", -1)
-        field = lanes_forward(wavefield, handed, source, slowness, reflectivity, base, c * step, step, groups)
+    for first, last in zip(bounds[:-1], bounds[1:]):
+        handed = shifted(boundary[0, :, first:last], "slab", -1)
+        field = lanes_forward(wavefield, handed, source, slowness, reflectivity, base, first, last - first, groups)
         pieces.append(lax.all_to_all(field, "gx", split_axis=0, concat_axis=0, tiled=True))
-    if (step % factor_pair(total_rows)[1]) != 0:
-        pieces = [jnp.concatenate(pieces, axis=2)]
     freq_row = permuted_freq(jnp.arange(total_rows, dtype=jnp.int32), total_rows)
     freq_col = permuted_freq(device * width + jnp.arange(width, dtype=jnp.int32), columns)
     factor = propagator(freq_row[:, None], freq_col[None, :], base, scale)

time: 273 us -> 290 us (1.062)
  starting transfers between devices: 12.2 us -> 18.5 us
  waiting for transfers between devices: 98.2 us -> 103 us
    all_to_all x2 -> x3, starting transfers between devices: 9.67 us -> 14.6 us  [body(): lax.all_to_all(field, 'gx', split_axis=0, concat_axis=0, tiled=True)]
    ppermute x2 -> x3, waiting for transfers between devices: 51.5 us -> 55.8 us  [shifted(): return lax.ppermute(block, axis, route)]
    pallas_call x2 -> x3, Pallas kernels: 18.5 us -> 20.6 us  [lanes_forward(): pl.pallas_call(lanes_forward_kernel, grid=(step // block,), in_specs=[pl....]
    all_to_all x2 -> x3, waiting for transfers between devices: 46.7 us -> 47.6 us  [body(): lax.all_to_all(field, 'gx', split_axis=0, concat_axis=0, tiled=True)]
  transfers between devices with their start and end apart: 4 -> 6, of which waited for: 4 -> 4; matrix products, arithmetic and copies ran while one was open for 5% -> 6% of each run, Pallas kernels for 3% -> 6%
where the time goes in v4:
time: 290 us; the launch traced here: 289 us
  waiting for transfers between devices  103 us (36%)
  blocking collectives  98.5 us (34%)
  Pallas kernels  44.2 us (15%)
  starting transfers between devices  18.5 us (6%)
  other arithmetic  12.3 us (4%)
  local copies, waits for them, and re-layouts  10.6 us (4%)
    all_to_all x1, blocking collectives, body(): lax.all_to_all(spatial, 'gx', split_axis=0, concat_axis=0, tiled=True)  98.5 us
    ppermute x3, waiting for transfers between devices, shifted(): return lax.ppermute(block, axis, route)  55.8 us
    all_to_all x3, waiting for transfers between devices, body(): lax.all_to_all(field, 'gx', split_axis=0, concat_axis=0, tiled=True)  47.6 us
    pallas_call x3, Pallas kernels, lanes_forward(): pl.pallas_call(lanes_forward_kernel, grid=(step // block,), in_specs=[pl....  20.6 us
    all_to_all x3, starting transfers between devices, body(): lax.all_to_all(field, 'gx', split_axis=0, concat_axis=0, tiled=True)  14.6 us
    pallas_call x1, Pallas kernels, rows_shift(): pl.pallas_call(rows_kernel, grid=(width // block,), in_specs=[pl.BlockSpe...  13.9 us
    pallas_call x1, Pallas kernels, lanes_inverse(): pl.pallas_call(lanes_inverse_kernel, grid=(step // block,), in_specs=[pl....  9.75 us
    mul x1, other arithmetic, propagator(): return (real_part * scale, imag_part * scale)  8.44 us
  transfers between devices with their start and end apart: 6, of which 4 were waited for; matrix products, arithmetic and copies ran while one was open for 6% of the time, Pallas kernels for 6%

profile of v4, /device:TPU:0, one launch (start us, length us, event | category | flops | bytes accessed | tf_op | source)
XLA Modules:
  0.0 288.9 jit_solution(2888403104044156554)
XLA Ops:
  0.6 1.0 slice_bitcast_fusion.2
  1.6 1.3 collective-permute-start
  2.9 0.1 fusion.37
  3.0 0.6 fusion.44
  4.2 0.3 fusion.16
  4.5 0.7 pad_maximum_fusion.1.w_ref.refs_4_
  5.2 7.6 %collective-permute-done.hand_ref = bf16[2,32,2048]{2,1,0:T(8,128)(2,1)S(1)} collective-permute-done((bf16[2,32,2048]{2,1,0:T(8,128)(2,1)S(1)}, bf16[2,32,2048]{2,1,0:T(8,128)(2,1)S(1)}, u32[]{:S(2)}, u32[]{:S(2)}) %collective-permute-start) | collective-permute-done | bytes 262176 | tf_op jit(solution)/shard_map/ppermute | solution.py:19
  12.7 0.0 copy-start.5
  12.8 0.7 copy-done.5
  13.5 3.9 %shard_map.77 = f32[8,2,32,256]{3,2,1,0:T(8,128)} custom-call(f32[1,1]{1,0:T(1,128)} %bitcast.10.base_ref, bf16[1,2,256,2048]{3,2,1,0:T(8,128)(2,1)} %wave_ref.5, bf16[2,32,2048]{2,1,0:T(8,128)(2,1)} %copy-done.5, bf16[1,2,256,2048]{3,2,1,0:T(8,128)(2,1)} %src_ref.7, f32[1,256,2048]{2,1,0:T(8,128)} %slow_ref.5, f32[1,256,2048]{2,1,0:T(8,128)} %refl_ref.5, ...), custom_call_target="tpu_custom_call" | custom-call | tf_op jit(solution)/shard_map/pallas_call | solution.py:308
  17.3 5.1 %all-to-all-start = ((f32[8,2,32,256]{3,2,1,0:T(8,128)}), f32[8,2,32,256]{3,2,1,0:T(8,128)S(1)}, u32[]{:S(2)}, u32[]{:S(2)}) async-start(f32[8,2,32,256]{3,2,1,0:T(8,128)} %shard_map.77), calls=%async_computation | async-start | bytes 1048576 | tf_op jit(solution)/shard_map/all_to_all | solution.py:401
  22.4 1.1 slice_bitcast_fusion.1
  23.5 1.3 collective-permute-start.1
  24.8 15.6 %collective-permute-done.1.hand_ref = bf16[2,64,2048]{2,1,0:T(8,128)(2,1)S(1)} collective-permute-done((bf16[2,64,2048]{2,1,0:T(8,128)(2,1)S(1)}, bf16[2,64,2048]{2,1,0:T(8,128)(2,1)S(1)}, u32[]{:S(2)}, u32[]{:S(2)}) %collective-permute-start.1) | collective-permute-done | bytes 524320 | tf_op jit(solution)/shard_map/ppermute | solution.py:19
  40.4 0.0 copy-start.4
  40.4 0.8 copy-done.4
  41.2 5.6 %shard_map.78 = f32[8,2,64,256]{3,2,1,0:T(8,128)} custom-call(f32[1,1]{1,0:T(1,128)} %bitcast.11.base_ref, bf16[1,2,256,2048]{3,2,1,0:T(8,128)(2,1)} %wave_ref.5, bf16[2,64,2048]{2,1,0:T(8,128)(2,1)} %copy-done.4, bf16[1,2,256,2048]{3,2,1,0:T(8,128)(2,1)} %src_ref.7, f32[1,256,2048]{2,1,0:T(8,128)} %slow_ref.5, f32[1,256,2048]{2,1,0:T(8,128)} %refl_ref.5, ...), custom_call_target="tpu_custom_call" | custom-call | tf_op jit(solution)/shard_map/pallas_call | solution.py:308
  46.8 0.0 all-to-all-done.refs_0_
  46.8 0.0 copy-start.2
  46.8 4.8 %all-to-all-start.1 = ((f32[8,2,64,256]{3,2,1,0:T(8,128)}), f32[8,2,64,256]{3,2,1,0:T(8,128)S(1)}, u32[]{:S(2)}, u32[]{:S(2)}) async-start(f32[8,2,64,256]{3,2,1,0:T(8,128)} %shard_map.78), calls=%async_computation.1 | async-start | bytes 2097152 | tf_op jit(solution)/shard_map/all_to_all | solution.py:401
  51.6 1.4 slice_bitcast_fusion
  53.1 0.0 copy-done.2
  53.1 1.3 collective-permute-start.2
  54.4 32.7 %collective-permute-done.2.hand_ref = bf16[2,160,2048]{2,1,0:T(8,128)(2,1)S(1)} collective-permute-done((bf16[2,160,2048]{2,1,0:T(8,128)(2,1)S(1)}, bf16[2,160,2048]{2,1,0:T(8,128)(2,1)S(1)}, u32[]{:S(2)}, u32[]{:S(2)}) %collective-permute-start.2) | collective-permute-done | bytes 1310752 | tf_op jit(solution)/shard_map/ppermute | solution.py:19
  87.0 0.0 copy-start.3
  87.0 1.1 copy-done.3
  88.1 11.1 %shard_map.79 = f32[8,2,160,256]{3,2,1,0:T(8,128)} custom-call(f32[1,1]{1,0:T(1,128)} %bitcast.12.base_ref, bf16[1,2,256,2048]{3,2,1,0:T(8,128)(2,1)} %wave_ref.5, bf16[2,160,2048]{2,1,0:T(8,128)(2,1)} %copy-done.3, bf16[1,2,256,2048]{3,2,1,0:T(8,128)(2,1)} %src_ref.7, f32[1,256,2048]{2,1,0:T(8,128)} %slow_ref.5, f32[1,256,2048]{2,1,0:T(8,128)} %refl_ref.5, ...), custom_call_target="tpu_custom_call" | custom-call | tf_op jit(solution)/shard_map/pallas_call | solution.py:308
  99.2 0.0 all-to-all-done.1.refs_1_
  99.2 0.0 copy-start.1
  99.2 1.0 copy-done.1
  100.2 4.7 %all-to-all-start.2 = ((f32[8,2,160,256]{3,2,1,0:T(8,128)}), f32[8,2,160,256]{3,2,1,0:T(8,128)S(1)}, u32[]{:S(2)}, u32[]{:S(2)}) async-start(f32[8,2,160,256]{3,2,1,0:T(8,128)} %shard_map.79), calls=%async_computation.2 | async-start | bytes 5242880 | tf_op jit(solution)/shard_map/all_to_all | solution.py:401
  104.9 2.0 copy.8.refs_5_
  106.9 8.4 %fusion.2 = (f32[1,2048,256]{2,1,0:T(8,128)S(1)}, f32[1,2048,256]{2,1,0:T(8,128)S(1)}) fusion(f32[256]{0:T(256)S(1)} %fusion.43, f32[2048]{0:T(1024)S(1)} %fusion.33), kind=kLoop, calls=%fused_computation.5 | loop fusion | flops 4718592 | bytes 4203520 | tf_op jit(solution)/shard_map/mul | solution.py:368
  115.4 2.2 pad_maximum_fusion.refs_3_
  117.6 47.6 %all-to-all-done.2.refs_2_ = f32[8,2,160,256]{3,2,1,0:T(8,128)S(1)} async-done(((f32[8,2,160,256]{3,2,1,0:T(8,128)}), f32[8,2,160,256]{3,2,1,0:T(8,128)S(1)}, u32[]{:S(2)}, u32[]{:S(2)}) %all-to-all-start.2) | async-done | bytes 2621472 | tf_op jit(solution)/shard_map/all_to_all | solution.py:401
  165.2 0.0 copy-start
  165.2 1.6 copy-done
  166.8 13.9 %shard_map.80 = f32[8,2,256,256]{3,2,1,0:T(8,128)} custom-call(f32[8,2,32,256]{3,2,1,0:T(8,128)} %copy-done.2, f32[8,2,64,256]{3,2,1,0:T(8,128)} %copy-done.1, f32[8,2,160,256]{3,2,1,0:T(8,128)} %copy-done, f32[2,2048,256]{2,1,0:T(8,128)} %pad_maximum_fusion.refs_3_, f32[2,128,128]{2,1,0:T(8,128)} %pad_maximum_fusion.1.w_ref.refs_4_, ...), custom_call_target="tpu_custom_call" | custom-call | tf_op jit(solution)/shard_map/pallas_call | solution.py:205
  180.7 98.5 %all_to_all.20.x_ref = f32[8,2,256,256]{3,2,1,0:T(8,128)} all-to-all(f32[8,2,256,256]{3,2,1,0:T(8,128)} %shard_map.80), channel_id=1, replica_groups=mesh['slab'=4,'gx'=8] {'gx'}, dimensions={0} | all-to-all | bytes 8388608 | tf_op jit(solution)/shard_map/all_to_all | solution.py:406
  279.2 9.7 %shard_map.81 = (bf16[1,2,256,2048]{3,2,1,0:T(8,128)(2,1)}, f32[1,256,2048]{2,1,0:T(8,128)}) custom-call(f32[8,2,256,256]{3,2,1,0:T(8,128)} %all_to_all.20.x_ref, bf16[1,2,256,2048]{3,2,1,0:T(8,128)(2,1)} %src_ref.7, f32[2,128,128]{2,1,0:T(8,128)} %pad_maximum_fusion.1.w_ref.refs_4_, f32[2,16,128]{2,1,0:T(8,128)} %get-tuple-element.3.tw_ref), custom_call_target="tpu_custom_call" | custom-call | tf_op jit(solution)/shard_map/pallas_call | solution.py:331
  (2 shorter events, 0.0 us)
Async XLA Ops:
  1.6 11.1 %collective-permute-start = (bf16[2,32,2048]{2,1,0:T(8,128)(2,1)S(1)}, bf16[2,32,2048]{2,1,0:T(8,128)(2,1)S(1)}, u32[]{:S(2)}, u32[]{:S(2)}) collective-permute-start(bf16[2,32,2048]{2,1,0:T(8,128)(2,1)S(1)} %slice_bitcast_fusion.2), channel_id=1, source_target_pairs={{8,0},{16,8},{24,16},{9,1},{17,9},{25,17},{10,2},{18,10},{26,18},{... | collective-permute-start | bytes 786440 | tf_op jit(solution)/shard_map/ppermute | solution.py:19
  12.7 0.7 copy-start.5
  17.3 29.5 %all-to-all-start = ((f32[8,2,32,256]{3,2,1,0:T(8,128)}), f32[8,2,32,256]{3,2,1,0:T(8,128)S(1)}, u32[]{:S(2)}, u32[]{:S(2)}) async-start(f32[8,2,32,256]{3,2,1,0:T(8,128)} %shard_map.77), calls=%async_computation | async-start | bytes 1048576 | tf_op jit(solution)/shard_map/all_to_all | solution.py:401
  23.5 16.9 %collective-permute-start.1 = (bf16[2,64,2048]{2,1,0:T(8,128)(2,1)S(1)}, bf16[2,64,2048]{2,1,0:T(8,128)(2,1)S(1)}, u32[]{:S(2)}, u32[]{:S(2)}) collective-permute-start(bf16[2,64,2048]{2,1,0:T(8,128)(2,1)S(1)} %slice_bitcast_fusion.1), channel_id=1, source_target_pairs={{8,0},{16,8},{24,16},{9,1},{17,9},{25,17},{10,2},{18,10},{26,18},{... | collective-permute-start | bytes 1572872 | tf_op jit(solution)/shard_map/ppermute | solution.py:19
  40.4 0.8 copy-start.4
  46.8 6.2 %copy-start.2 = (f32[8,2,32,256]{3,2,1,0:T(8,128)}, f32[8,2,32,256]{3,2,1,0:T(8,128)S(1)}, u32[]{:S(2)}) copy-start(f32[8,2,32,256]{3,2,1,0:T(8,128)S(1)} %all-to-all-done.refs_0_) | copy-start | bytes 1572868
  46.8 52.4 %all-to-all-start.1 = ((f32[8,2,64,256]{3,2,1,0:T(8,128)}), f32[8,2,64,256]{3,2,1,0:T(8,128)S(1)}, u32[]{:S(2)}, u32[]{:S(2)}) async-start(f32[8,2,64,256]{3,2,1,0:T(8,128)} %shard_map.78), calls=%async_computation.1 | async-start | bytes 2097152 | tf_op jit(solution)/shard_map/all_to_all | solution.py:401
  53.1 34.0 %collective-permute-start.2 = (bf16[2,160,2048]{2,1,0:T(8,128)(2,1)S(1)}, bf16[2,160,2048]{2,1,0:T(8,128)(2,1)S(1)}, u32[]{:S(2)}, u32[]{:S(2)}) collective-permute-start(bf16[2,160,2048]{2,1,0:T(8,128)(2,1)S(1)} %slice_bitcast_fusion), channel_id=1, source_target_pairs={{8,0},{16,8},{24,16},{9,1},{17,9},{25,17},{10,2},{18,10},{26,18},{... | collective-permute-start | bytes 3932168 | tf_op jit(solution)/shard_map/ppermute | solution.py:19
  87.0 1.1 copy-start.3
  99.2 1.0 copy-start.1
  100.2 65.0 %all-to-all-start.2 = ((f32[8,2,160,256]{3,2,1,0:T(8,128)}), f32[8,2,160,256]{3,2,1,0:T(8,128)S(1)}, u32[]{:S(2)}, u32[]{:S(2)}) async-start(f32[8,2,160,256]{3,2,1,0:T(8,128)} %shard_map.79), calls=%async_computation.2 | async-start | bytes 5242880 | tf_op jit(solution)/shard_map/all_to_all | solution.py:401
  165.2 1.6 copy-start

commit v5 on v4

--- a/solution.py
+++ b/solution.py
@@ -385,7 +385,7 @@
     columns = wavefield.shape[3]
     eighth = count // 8
     if count % 8 == 0 and eighth % 8 == 0:
-        bounds = [0, eighth, 3 * eighth, count]
+        bounds = [0, 3 * eighth, count]
     else:
         bounds = [0, count]
     groups = lax.axis_size("gx")

time: 290 us -> 276 us (0.952)
  starting transfers between devices: 18.5 us -> 12.4 us
  waiting for transfers between devices: 103 us -> 98.9 us
    all_to_all x3 -> x2, starting transfers between devices: 14.6 us -> 9.86 us  [body(): lax.all_to_all(field, 'gx', split_axis=0, concat_axis=0, tiled=True)]
    ppermute x3 -> x2, waiting for transfers between devices: 55.8 us -> 51.3 us  [shifted(): return lax.ppermute(block, axis, route)]
    pallas_call x3 -> x2, Pallas kernels: 20.6 us -> 18.5 us  [lanes_forward(): pl.pallas_call(lanes_forward_kernel, grid=(step // block,), in_specs=[pl....]
    all_to_all x3 -> x2, waiting for transfers between devices: 47.6 us -> 47.6 us  [body(): lax.all_to_all(field, 'gx', split_axis=0, concat_axis=0, tiled=True)]
  transfers between devices with their start and end apart: 6 -> 4, of which waited for: 4 -> 3; matrix products, arithmetic and copies ran while one was open for 6% -> 6% of each run, Pallas kernels for 6% -> 4%
where the time goes in v5:
time: 276 us; the launch traced here: 275 us
  waiting for transfers between devices  98.9 us (36%)
  blocking collectives  98.5 us (36%)
  Pallas kernels  42.3 us (15%)
  starting transfers between devices  12.4 us (4%)
  other arithmetic  12.3 us (4%)
  local copies, waits for them, and re-layouts  9.26 us (3%)
    all_to_all x1, blocking collectives, body(): lax.all_to_all(spatial, 'gx', split_axis=0, concat_axis=0, tiled=True)  98.5 us
    ppermute x2, waiting for transfers between devices, shifted(): return lax.ppermute(block, axis, route)  51.3 us
    all_to_all x2, waiting for transfers between devices, body(): lax.all_to_all(field, 'gx', split_axis=0, concat_axis=0, tiled=True)  47.6 us
    pallas_call x2, Pallas kernels, lanes_forward(): pl.pallas_call(lanes_forward_kernel, grid=(step // block,), in_specs=[pl....  18.5 us
    pallas_call x1, Pallas kernels, rows_shift(): pl.pallas_call(rows_kernel, grid=(width // block,), in_specs=[pl.BlockSpe...  14 us
    all_to_all x2, starting transfers between devices, body(): lax.all_to_all(field, 'gx', split_axis=0, concat_axis=0, tiled=True)  9.86 us
    pallas_call x1, Pallas kernels, lanes_inverse(): pl.pallas_call(lanes_inverse_kernel, grid=(step // block,), in_specs=[pl....  9.75 us
    mul x1, other arithmetic, propagator(): return (real_part * scale, imag_part * scale)  8.44 us
  transfers between devices with their start and end apart: 4, of which 3 were waited for; matrix products, arithmetic and copies ran while one was open for 6% of the time, Pallas kernels for 4%

profile of v5, /device:TPU:0, one launch (start us, length us, event | category | flops | bytes accessed | tf_op | source)
XLA Modules:
  0.0 275.0 jit_solution(18137774374108853028)
XLA Ops:
  0.6 1.2 slice_bitcast_fusion.1
  1.8 1.3 collective-permute-start
  3.8 0.1 fusion.37
  3.9 0.6 fusion.44
  4.5 0.3 fusion.16
  4.7 0.6 pad_maximum_fusion.1.w_ref.refs_3_
  5.4 18.8 %collective-permute-done.hand_ref = bf16[2,96,2048]{2,1,0:T(8,128)(2,1)S(1)} collective-permute-done((bf16[2,96,2048]{2,1,0:T(8,128)(2,1)S(1)}, bf16[2,96,2048]{2,1,0:T(8,128)(2,1)S(1)}, u32[]{:S(2)}, u32[]{:S(2)}) %collective-permute-start) | collective-permute-done | bytes 786464 | tf_op jit(solution)/shard_map/ppermute | solution.py:19
  24.2 0.0 copy-start.3
  24.2 0.9 copy-done.3
  25.1 7.4 %shard_map.77 = f32[8,2,96,256]{3,2,1,0:T(8,128)} custom-call(f32[1,1]{1,0:T(1,128)} %bitcast.8.base_ref, bf16[1,2,256,2048]{3,2,1,0:T(8,128)(2,1)} %wave_ref.3, bf16[2,96,2048]{2,1,0:T(8,128)(2,1)} %copy-done.3, bf16[1,2,256,2048]{3,2,1,0:T(8,128)(2,1)} %src_ref.5, f32[1,256,2048]{2,1,0:T(8,128)} %slow_ref.3, f32[1,256,2048]{2,1,0:T(8,128)} %refl_ref.3, ...), custom_call_target="tpu_custom_call" | custom-call | tf_op jit(solution)/shard_map/pallas_call | solution.py:308
  32.5 5.1 %all-to-all-start = ((f32[8,2,96,256]{3,2,1,0:T(8,128)}), f32[8,2,96,256]{3,2,1,0:T(8,128)S(1)}, u32[]{:S(2)}, u32[]{:S(2)}) async-start(f32[8,2,96,256]{3,2,1,0:T(8,128)} %shard_map.77), calls=%async_computation | async-start | bytes 3145728 | tf_op jit(solution)/shard_map/all_to_all | solution.py:401
  37.6 1.4 slice_bitcast_fusion
  39.1 1.3 collective-permute-start.1
  40.4 32.4 %collective-permute-done.1.hand_ref = bf16[2,160,2048]{2,1,0:T(8,128)(2,1)S(1)} collective-permute-done((bf16[2,160,2048]{2,1,0:T(8,128)(2,1)S(1)}, bf16[2,160,2048]{2,1,0:T(8,128)(2,1)S(1)}, u32[]{:S(2)}, u32[]{:S(2)}) %collective-permute-start.1) | collective-permute-done | bytes 1310752 | tf_op jit(solution)/shard_map/ppermute | solution.py:19
  72.8 0.0 copy-start.2
  72.8 1.1 copy-done.2
  73.9 11.1 %shard_map.78 = f32[8,2,160,256]{3,2,1,0:T(8,128)} custom-call(f32[1,1]{1,0:T(1,128)} %bitcast.9.base_ref, bf16[1,2,256,2048]{3,2,1,0:T(8,128)(2,1)} %wave_ref.3, bf16[2,160,2048]{2,1,0:T(8,128)(2,1)} %copy-done.2, bf16[1,2,256,2048]{3,2,1,0:T(8,128)(2,1)} %src_ref.5, f32[1,256,2048]{2,1,0:T(8,128)} %slow_ref.3, f32[1,256,2048]{2,1,0:T(8,128)} %refl_ref.3, ...), custom_call_target="tpu_custom_call" | custom-call | tf_op jit(solution)/shard_map/pallas_call | solution.py:308
  85.0 0.0 all-to-all-done.refs_0_
  85.0 0.0 copy-start.1
  85.0 1.1 copy-done.1
  86.1 4.7 %all-to-all-start.1 = ((f32[8,2,160,256]{3,2,1,0:T(8,128)}), f32[8,2,160,256]{3,2,1,0:T(8,128)S(1)}, u32[]{:S(2)}, u32[]{:S(2)}) async-start(f32[8,2,160,256]{3,2,1,0:T(8,128)} %shard_map.78), calls=%async_computation.1 | async-start | bytes 5242880 | tf_op jit(solution)/shard_map/all_to_all | solution.py:401
  90.9 2.0 copy.8.refs_4_
  92.9 8.4 %fusion.2 = (f32[1,2048,256]{2,1,0:T(8,128)S(1)}, f32[1,2048,256]{2,1,0:T(8,128)S(1)}) fusion(f32[256]{0:T(256)S(1)} %fusion.43, f32[2048]{0:T(1024)S(1)} %fusion.33), kind=kLoop, calls=%fused_computation.5 | loop fusion | flops 4718592 | bytes 4203520 | tf_op jit(solution)/shard_map/mul | solution.py:368
  101.3 2.2 pad_maximum_fusion.refs_2_
  103.5 47.6 %all-to-all-done.1.refs_1_ = f32[8,2,160,256]{3,2,1,0:T(8,128)S(1)} async-done(((f32[8,2,160,256]{3,2,1,0:T(8,128)}), f32[8,2,160,256]{3,2,1,0:T(8,128)S(1)}, u32[]{:S(2)}, u32[]{:S(2)}) %all-to-all-start.1) | async-done | bytes 2621472 | tf_op jit(solution)/shard_map/all_to_all | solution.py:401
  151.2 0.0 copy-start
  151.2 1.6 copy-done
  152.7 14.0 %shard_map.79 = f32[8,2,256,256]{3,2,1,0:T(8,128)} custom-call(f32[8,2,96,256]{3,2,1,0:T(8,128)} %copy-done.1, f32[8,2,160,256]{3,2,1,0:T(8,128)} %copy-done, f32[2,2048,256]{2,1,0:T(8,128)} %pad_maximum_fusion.refs_2_, f32[2,128,128]{2,1,0:T(8,128)} %pad_maximum_fusion.1.w_ref.refs_3_, f32[2,16,128,1]{3,2,1,0:T(8,128)} %copy.8.refs_4_), custom_call_target="tpu_custom_call" | custom-call | tf_op jit(solution)/shard_map/pallas_call | solution.py:205
  166.7 98.5 %all_to_all.15.x_ref = f32[8,2,256,256]{3,2,1,0:T(8,128)} all-to-all(f32[8,2,256,256]{3,2,1,0:T(8,128)} %shard_map.79), channel_id=1, replica_groups=mesh['slab'=4,'gx'=8] {'gx'}, dimensions={0} | all-to-all | bytes 8388608 | tf_op jit(solution)/shard_map/all_to_all | solution.py:406
  265.2 9.7 %shard_map.80 = (bf16[1,2,256,2048]{3,2,1,0:T(8,128)(2,1)}, f32[1,256,2048]{2,1,0:T(8,128)}) custom-call(f32[8,2,256,256]{3,2,1,0:T(8,128)} %all_to_all.15.x_ref, bf16[1,2,256,2048]{3,2,1,0:T(8,128)(2,1)} %src_ref.5, f32[2,128,128]{2,1,0:T(8,128)} %pad_maximum_fusion.1.w_ref.refs_3_, f32[2,16,128]{2,1,0:T(8,128)} %get-tuple-element.3.tw_ref), custom_call_target="tpu_custom_call" | custom-call | tf_op jit(solution)/shard_map/pallas_call | solution.py:331
  (2 shorter events, 0.0 us)
Async XLA Ops:
  1.8 22.4 %collective-permute-start = (bf16[2,96,2048]{2,1,0:T(8,128)(2,1)S(1)}, bf16[2,96,2048]{2,1,0:T(8,128)(2,1)S(1)}, u32[]{:S(2)}, u32[]{:S(2)}) collective-permute-start(bf16[2,96,2048]{2,1,0:T(8,128)(2,1)S(1)} %slice_bitcast_fusion.1), channel_id=1, source_target_pairs={{8,0},{16,8},{24,16},{9,1},{17,9},{25,17},{10,2},{18,10},{26,18},{... | collective-permute-start | bytes 2359304 | tf_op jit(solution)/shard_map/ppermute | solution.py:19
  24.2 0.9 copy-start.3
  32.5 52.5 %all-to-all-start = ((f32[8,2,96,256]{3,2,1,0:T(8,128)}), f32[8,2,96,256]{3,2,1,0:T(8,128)S(1)}, u32[]{:S(2)}, u32[]{:S(2)}) async-start(f32[8,2,96,256]{3,2,1,0:T(8,128)} %shard_map.77), calls=%async_computation | async-start | bytes 3145728 | tf_op jit(solution)/shard_map/all_to_all | solution.py:401
  39.1 33.7 %collective-permute-start.1 = (bf16[2,160,2048]{2,1,0:T(8,128)(2,1)S(1)}, bf16[2,160,2048]{2,1,0:T(8,128)(2,1)S(1)}, u32[]{:S(2)}, u32[]{:S(2)}) collective-permute-start(bf16[2,160,2048]{2,1,0:T(8,128)(2,1)S(1)} %slice_bitcast_fusion), channel_id=1, source_target_pairs={{8,0},{16,8},{24,16},{9,1},{17,9},{25,17},{10,2},{18,10},{26,18},{... | collective-permute-start | bytes 3932168 | tf_op jit(solution)/shard_map/ppermute | solution.py:19
  72.8 1.1 copy-start.2
  85.0 1.1 copy-start.1
  86.1 65.0 %all-to-all-start.1 = ((f32[8,2,160,256]{3,2,1,0:T(8,128)}), f32[8,2,160,256]{3,2,1,0:T(8,128)S(1)}, u32[]{:S(2)}, u32[]{:S(2)}) async-start(f32[8,2,160,256]{3,2,1,0:T(8,128)} %shard_map.78), calls=%async_computation.1 | async-start | bytes 5242880 | tf_op jit(solution)/shard_map/all_to_all | solution.py:401
  151.2 1.6 copy-start

commit v6 on v5

--- a/solution.py
+++ b/solution.py
@@ -215,26 +215,49 @@
     )(*turned, factor, table, turn)
 
 
-def lanes_forward_kernel(base_ref, wave_ref, hand_ref, src_ref, slow_ref, refl_ref, w_ref, tw_ref, o_ref):
-    outer = tw_ref.shape[1]
-    inner = tw_ref.shape[2]
+def prelens_kernel(base_ref, wave_ref, src_ref, slow_ref, refl_ref, o_ref):
     base = base_ref[0, 0]
     gain = OMEGA * OMEGA * refl_ref[0]
-    real_in = (
-        wave_ref[0, 0].astype(jnp.float32)
-        + hand_ref[0].astype(jnp.float32)
-        + gain * src_ref[0, 0].astype(jnp.float32)
-    )
-    imag_in = (
-        wave_ref[0, 1].astype(jnp.float32)
-        + hand_ref[1].astype(jnp.float32)
-        + gain * src_ref[0, 1].astype(jnp.float32)
-    )
+    real_in = wave_ref[0, 0].astype(jnp.float32) + gain * src_ref[0, 0].astype(jnp.float32)
+    imag_in = wave_ref[0, 1].astype(jnp.float32) + gain * src_ref[0, 1].astype(jnp.float32)
     angle = -OMEGA * (slow_ref[0] - base) * DEPTH_STEP
     cosine = jnp.cos(angle)
     sine = jnp.sin(angle)
-    lensed_real = real_in * cosine - imag_in * sine
-    lensed_imag = real_in * sine + imag_in * cosine
+    o_ref[0] = real_in * cosine - imag_in * sine
+    o_ref[1] = real_in * sine + imag_in * cosine
+    o_ref[2] = cosine
+    o_ref[3] = sine
+
+
+def prelens(wavefield, source, slowness, reflectivity, base):
+    _, _, count, length = wavefield.shape
+    block = min(count, 32)
+    quad = lambda i: (0, 0, i, 0)
+    flat = lambda i: (0, i, 0)
+    return pl.pallas_call(
+        prelens_kernel,
+        grid=(count // block,),
+        in_specs=[
+            pl.BlockSpec(memory_space=pltpu.SMEM),
+            pl.BlockSpec((1, 2, block, length), quad),
+            pl.BlockSpec((1, 2, block, length), quad),
+            pl.BlockSpec((1, block, length), flat),
+            pl.BlockSpec((1, block, length), flat),
+        ],
+        out_specs=pl.BlockSpec((4, block, length), flat),
+        out_shape=jax.ShapeDtypeStruct((4, count, length), jnp.float32),
+    )(base.reshape(1, 1), wavefield, source, slowness, reflectivity)
+
+
+def lanes_forward_kernel(pre_ref, hand_ref, w_ref, tw_ref, o_ref):
+    outer = tw_ref.shape[1]
+    inner = tw_ref.shape[2]
+    hand_real = hand_ref[0].astype(jnp.float32)
+    hand_imag = hand_ref[1].astype(jnp.float32)
+    cosine = pre_ref[2]
+    sine = pre_ref[3]
+    lensed_real = pre_ref[0] + (hand_real * cosine - hand_imag * sine)
+    lensed_imag = pre_ref[1] + (hand_real * sine + hand_imag * cosine)
     slabs = [
         (lensed_real[:, a * inner:(a + 1) * inner], lensed_imag[:, a * inner:(a + 1) * inner])
         for a in range(outer)
@@ -298,29 +321,23 @@
     return outer, inner, table, turn
 
 
-def lanes_forward(wavefield, handed, source, slowness, reflectivity, base, first, step, groups):
-    length = wavefield.shape[3]
+def lanes_forward(lensed, handed, first, step, groups):
+    length = lensed.shape[2]
     outer, inner, table, turn = lane_tables(length)
     block = min(step, 32)
     offset = first // block
-    quad = lambda i: (0, 0, offset + i, 0)
-    flat = lambda i: (0, offset + i, 0)
     return pl.pallas_call(
         lanes_forward_kernel,
         grid=(step // block,),
         in_specs=[
-            pl.BlockSpec(memory_space=pltpu.SMEM),
-            pl.BlockSpec((1, 2, block, length), quad),
+            pl.BlockSpec((4, block, length), lambda i: (0, offset + i, 0)),
             pl.BlockSpec((2, block, length), lambda i: (0, i, 0)),
-            pl.BlockSpec((1, 2, block, length), quad),
-            pl.BlockSpec((1, block, length), flat),
-            pl.BlockSpec((1, block, length), flat),
             pl.BlockSpec((2, inner, inner), lambda i: (0, 0, 0)),
             pl.BlockSpec((2, outer, inner), lambda i: (0, 0, 0)),
         ],
         out_specs=pl.BlockSpec((groups, 2, block, length // groups), lambda i: (0, 0, i, 0)),
         out_shape=jax.ShapeDtypeStruct((groups, 2, step, length // groups), jnp.float32),
-    )(base.reshape(1, 1), wavefield, handed, source, slowness, reflectivity, table, turn)
+    )(lensed, handed, table, turn)
 
 
 def lanes_inverse(back, source):
@@ -395,9 +412,10 @@
     scale = 1.0 / (total_rows * columns)
     base = ref_slowness[0]
     pieces = []
+    lensed = prelens(wavefield, source, slowness, reflectivity, base)
     for first, last in zip(bounds[:-1], bounds[1:]):
         handed = shifted(boundary[0, :, first:last], "slab", -1)
-        field = lanes_forward(wavefield, handed, source, slowness, reflectivity, base, first, last - first, groups)
+        field = lanes_forward(lensed, handed, first, last - first, groups)
         pieces.append(lax.all_to_all(field, "gx", split_axis=0, concat_axis=0, tiled=True))
     freq_row = permuted_freq(jnp.arange(total_rows, dtype=jnp.int32), total_rows)
     freq_col = permuted_freq(device * width + jnp.arange(width, dtype=jnp.int32), columns)

time: 276 us -> 270 us (0.978)
  waiting for transfers between devices: 98.9 us -> 86.4 us
  Pallas kernels: 42.3 us -> 48.5 us
    pallas_call x0 -> x1, Pallas kernels: none -> 12.5 us  [prelens(): pl.pallas_call(prelens_kernel, grid=(count // block,), in_specs=[pl.Block...]
    ppermute x2, waiting for transfers between devices: 51.3 us -> 38.8 us  [shifted(): return lax.ppermute(block, axis, route)]
    pallas_call x2, Pallas kernels: 18.5 us -> 12.3 us  [lanes_forward(): pl.pallas_call(lanes_forward_kernel, grid=(step // block,), in_specs=[pl....]
  transfers between devices with their start and end apart: 4 -> 4, of which waited for: 3 -> 3; matrix products, arithmetic and copies ran while one was open for 6% -> 6% of each run, Pallas kernels for 4% -> 7%
where the time goes in v6:
time: 270 us; the launch traced here: 269 us
  blocking collectives  98.5 us (36%)
  waiting for transfers between devices  86.4 us (32%)
  Pallas kernels  48.5 us (18%)
  starting transfers between devices  12.4 us (5%)
  other arithmetic  12.3 us (5%)
  local copies, waits for them, and re-layouts  9.24 us (3%)
    all_to_all x1, blocking collectives, body(): lax.all_to_all(spatial, 'gx', split_axis=0, concat_axis=0, tiled=True)  98.5 us
    all_to_all x2, waiting for transfers between devices, body(): lax.all_to_all(field, 'gx', split_axis=0, concat_axis=0, tiled=True)  47.6 us
    ppermute x2, waiting for transfers between devices, shifted(): return lax.ppermute(block, axis, route)  38.8 us
    pallas_call x1, Pallas kernels, rows_shift(): pl.pallas_call(rows_kernel, grid=(width // block,), in_specs=[pl.BlockSpe...  14 us
    pallas_call x1, Pallas kernels, prelens(): pl.pallas_call(prelens_kernel, grid=(count // block,), in_specs=[pl.Block...  12.5 us
    pallas_call x2, Pallas kernels, lanes_forward(): pl.pallas_call(lanes_forward_kernel, grid=(step // block,), in_specs=[pl....  12.3 us
    all_to_all x2, starting transfers between devices, body(): lax.all_to_all(field, 'gx', split_axis=0, concat_axis=0, tiled=True)  9.86 us
    pallas_call x1, Pallas kernels, lanes_inverse(): pl.pallas_call(lanes_inverse_kernel, grid=(step // block,), in_specs=[pl....  9.75 us
  transfers between devices with their start and end apart: 4, of which 3 were waited for; matrix products, arithmetic and copies ran while one was open for 6% of the time, Pallas kernels for 7%

profile of v6, /device:TPU:0, one launch (start us, length us, event | category | flops | bytes accessed | tf_op | source)
XLA Modules:
  0.0 268.8 jit_solution(1100852309374030975)
XLA Ops:
  0.6 1.2 slice_bitcast_fusion.1
  1.8 1.3 collective-permute-start
  3.8 12.5 %shard_map.77.pre_ref = f32[4,256,2048]{2,1,0:T(8,128)} custom-call(f32[1,1]{1,0:T(1,128)} %bitcast.8.base_ref, bf16[1,2,256,2048]{3,2,1,0:T(8,128)(2,1)} %wave_ref.1, bf16[1,2,256,2048]{3,2,1,0:T(8,128)(2,1)} %src_ref.3, f32[1,256,2048]{2,1,0:T(8,128)} %slow_ref.1, f32[1,256,2048]{2,1,0:T(8,128)} %refl_ref.1), custom_call_target="tpu_custom_call" | custom-call | tf_op jit(solution)/shard_map/pallas_call | solution.py:237
  16.2 0.1 fusion.37
  16.3 0.6 fusion.44
  16.9 0.3 fusion.16
  17.2 0.6 pad_maximum_fusion.1.w_ref.refs_3_
  17.8 6.4 %collective-permute-done.hand_ref = bf16[2,96,2048]{2,1,0:T(8,128)(2,1)S(1)} collective-permute-done((bf16[2,96,2048]{2,1,0:T(8,128)(2,1)S(1)}, bf16[2,96,2048]{2,1,0:T(8,128)(2,1)S(1)}, u32[]{:S(2)}, u32[]{:S(2)}) %collective-permute-start) | collective-permute-done | bytes 786464 | tf_op jit(solution)/shard_map/ppermute | solution.py:19
  24.2 0.0 copy-start.3
  24.2 0.9 copy-done.3
  25.1 5.0 %shard_map.78 = f32[8,2,96,256]{3,2,1,0:T(8,128)} custom-call(f32[4,256,2048]{2,1,0:T(8,128)} %shard_map.77.pre_ref, bf16[2,96,2048]{2,1,0:T(8,128)(2,1)} %copy-done.3, f32[2,128,128]{2,1,0:T(8,128)} %pad_maximum_fusion.1.w_ref.refs_3_, f32[2,16,128]{2,1,0:T(8,128)} %get-tuple-element.3.tw_ref), custom_call_target="tpu_custom_call" | custom-call | tf_op jit(solution)/shard_map/pallas_call | solution.py:329
  30.1 5.1 %all-to-all-start = ((f32[8,2,96,256]{3,2,1,0:T(8,128)}), f32[8,2,96,256]{3,2,1,0:T(8,128)S(1)}, u32[]{:S(2)}, u32[]{:S(2)}) async-start(f32[8,2,96,256]{3,2,1,0:T(8,128)} %shard_map.78), calls=%async_computation | async-start | bytes 3145728 | tf_op jit(solution)/shard_map/all_to_all | solution.py:419
  35.2 1.4 slice_bitcast_fusion
  36.7 1.3 collective-permute-start.1
  38.0 32.4 %collective-permute-done.1.hand_ref = bf16[2,160,2048]{2,1,0:T(8,128)(2,1)S(1)} collective-permute-done((bf16[2,160,2048]{2,1,0:T(8,128)(2,1)S(1)}, bf16[2,160,2048]{2,1,0:T(8,128)(2,1)S(1)}, u32[]{:S(2)}, u32[]{:S(2)}) %collective-permute-start.1) | collective-permute-done | bytes 1310752 | tf_op jit(solution)/shard_map/ppermute | solution.py:19
  70.4 0.0 copy-start.2
  70.4 1.1 copy-done.2
  71.5 7.3 %shard_map.79 = f32[8,2,160,256]{3,2,1,0:T(8,128)} custom-call(f32[4,256,2048]{2,1,0:T(8,128)} %shard_map.77.pre_ref, bf16[2,160,2048]{2,1,0:T(8,128)(2,1)} %copy-done.2, f32[2,128,128]{2,1,0:T(8,128)} %pad_maximum_fusion.1.w_ref.refs_3_, f32[2,16,128]{2,1,0:T(8,128)} %get-tuple-element.3.tw_ref), custom_call_target="tpu_custom_call" | custom-call | tf_op jit(solution)/shard_map/pallas_call | solution.py:329
  78.8 0.0 all-to-all-done.refs_0_
  78.8 0.0 copy-start.1
  78.8 1.1 copy-done.1
  79.9 4.7 %all-to-all-start.1 = ((f32[8,2,160,256]{3,2,1,0:T(8,128)}), f32[8,2,160,256]{3,2,1,0:T(8,128)S(1)}, u32[]{:S(2)}, u32[]{:S(2)}) async-start(f32[8,2,160,256]{3,2,1,0:T(8,128)} %shard_map.79), calls=%async_computation.1 | async-start | bytes 5242880 | tf_op jit(solution)/shard_map/all_to_all | solution.py:419
  84.7 2.0 copy.8.refs_4_
  86.7 8.4 %fusion.2 = (f32[1,2048,256]{2,1,0:T(8,128)S(1)}, f32[1,2048,256]{2,1,0:T(8,128)S(1)}) fusion(f32[256]{0:T(256)S(1)} %fusion.43, f32[2048]{0:T(1024)S(1)} %fusion.33), kind=kLoop, calls=%fused_computation.5 | loop fusion | flops 4718592 | bytes 4203520 | tf_op jit(solution)/shard_map/mul | solution.py:385
  95.1 2.2 pad_maximum_fusion.refs_2_
  97.3 47.6 %all-to-all-done.1.refs_1_ = f32[8,2,160,256]{3,2,1,0:T(8,128)S(1)} async-done(((f32[8,2,160,256]{3,2,1,0:T(8,128)}), f32[8,2,160,256]{3,2,1,0:T(8,128)S(1)}, u32[]{:S(2)}, u32[]{:S(2)}) %all-to-all-start.1) | async-done | bytes 2621472 | tf_op jit(solution)/shard_map/all_to_all | solution.py:419
  145.0 0.0 copy-start
  145.0 1.6 copy-done
  146.5 14.0 %shard_map.80 = f32[8,2,256,256]{3,2,1,0:T(8,128)} custom-call(f32[8,2,96,256]{3,2,1,0:T(8,128)} %copy-done.1, f32[8,2,160,256]{3,2,1,0:T(8,128)} %copy-done, f32[2,2048,256]{2,1,0:T(8,128)} %pad_maximum_fusion.refs_2_, f32[2,128,128]{2,1,0:T(8,128)} %pad_maximum_fusion.1.w_ref.refs_3_, f32[2,16,128,1]{3,2,1,0:T(8,128)} %copy.8.refs_4_), custom_call_target="tpu_custom_call" | custom-call | tf_op jit(solution)/shard_map/pallas_call | solution.py:205
  160.5 98.5 %all_to_all.15.x_ref = f32[8,2,256,256]{3,2,1,0:T(8,128)} all-to-all(f32[8,2,256,256]{3,2,1,0:T(8,128)} %shard_map.80), channel_id=1, replica_groups=mesh['slab'=4,'gx'=8] {'gx'}, dimensions={0} | all-to-all | bytes 8388608 | tf_op jit(solution)/shard_map/all_to_all | solution.py:424
  259.0 9.7 %shard_map.81 = (bf16[1,2,256,2048]{3,2,1,0:T(8,128)(2,1)}, f32[1,256,2048]{2,1,0:T(8,128)}) custom-call(f32[8,2,256,256]{3,2,1,0:T(8,128)} %all_to_all.15.x_ref, bf16[1,2,256,2048]{3,2,1,0:T(8,128)(2,1)} %src_ref.3, f32[2,128,128]{2,1,0:T(8,128)} %pad_maximum_fusion.1.w_ref.refs_3_, f32[2,16,128]{2,1,0:T(8,128)} %get-tuple-element.3.tw_ref), custom_call_target="tpu_custom_call" | custom-call | tf_op jit(solution)/shard_map/pallas_call | solution.py:348
  (2 shorter events, 0.0 us)
Async XLA Ops:
  1.8 22.4 %collective-permute-start = (bf16[2,96,2048]{2,1,0:T(8,128)(2,1)S(1)}, bf16[2,96,2048]{2,1,0:T(8,128)(2,1)S(1)}, u32[]{:S(2)}, u32[]{:S(2)}) collective-permute-start(bf16[2,96,2048]{2,1,0:T(8,128)(2,1)S(1)} %slice_bitcast_fusion.1), channel_id=1, source_target_pairs={{8,0},{16,8},{24,16},{9,1},{17,9},{25,17},{10,2},{18,10},{26,18},{... | collective-permute-start | bytes 2359304 | tf_op jit(solution)/shard_map/ppermute | solution.py:19
  24.2 0.9 copy-start.3
  30.1 48.7 %all-to-all-start = ((f32[8,2,96,256]{3,2,1,0:T(8,128)}), f32[8,2,96,256]{3,2,1,0:T(8,128)S(1)}, u32[]{:S(2)}, u32[]{:S(2)}) async-start(f32[8,2,96,256]{3,2,1,0:T(8,128)} %shard_map.78), calls=%async_computation | async-start | bytes 3145728 | tf_op jit(solution)/shard_map/all_to_all | solution.py:419
  36.7 33.7 %collective-permute-start.1 = (bf16[2,160,2048]{2,1,0:T(8,128)(2,1)S(1)}, bf16[2,160,2048]{2,1,0:T(8,128)(2,1)S(1)}, u32[]{:S(2)}, u32[]{:S(2)}) collective-permute-start(bf16[2,160,2048]{2,1,0:T(8,128)(2,1)S(1)} %slice_bitcast_fusion), channel_id=1, source_target_pairs={{8,0},{16,8},{24,16},{9,1},{17,9},{25,17},{10,2},{18,10},{26,18},{... | collective-permute-start | bytes 3932168 | tf_op jit(solution)/shard_map/ppermute | solution.py:19
  70.4 1.1 copy-start.2
  78.8 1.1 copy-start.1
  79.9 65.0 %all-to-all-start.1 = ((f32[8,2,160,256]{3,2,1,0:T(8,128)}), f32[8,2,160,256]{3,2,1,0:T(8,128)S(1)}, u32[]{:S(2)}, u32[]{:S(2)}) async-start(f32[8,2,160,256]{3,2,1,0:T(8,128)} %shard_map.79), calls=%async_computation.1 | async-start | bytes 5242880 | tf_op jit(solution)/shard_map/all_to_all | solution.py:419
  145.0 1.6 copy-start

commit v7 on v6

--- a/solution.py
+++ b/solution.py
@@ -2,6 +2,8 @@
 import math
 
 import jax
+import ml_dtypes
+import numpy as np
 import jax.numpy as jnp
 from jax import lax
 from jax.sharding import PartitionSpec as P
@@ -128,11 +130,31 @@
     return out
 
 
+def split_bf16(value):
+    spread = value * 65537.0
+    high = spread - (spread - value)
+    return high.astype(jnp.bfloat16), (value - high).astype(jnp.bfloat16)
+
+
+def split_table(table):
+    table = np.asarray(table, np.float32)
+    high = table.astype(ml_dtypes.bfloat16)
+    low = (table - high.astype(np.float32)).astype(ml_dtypes.bfloat16)
+    return high, low
+
+
+def dft_numpy(length, orient):
+    position = np.arange(length)
+    angle = orient * 2.0 * np.pi * (position[:, None] * position[None, :] % length) / length
+    return np.cos(angle), np.sin(angle)
+
+
 def stacked_matmul(stacked, real, imag):
     size = real.shape[1]
     rows = stacked.shape[0] // 2
-    both = jnp.concatenate([real, imag], axis=1)
-    prod = jnp.dot(stacked, both, precision=lax.Precision.HIGH, preferred_element_type=jnp.float32)
+    high, low = split_bf16(jnp.concatenate([real, imag], axis=1))
+    both = jnp.concatenate([high, low, high], axis=0)
+    prod = jnp.dot(stacked, both, preferred_element_type=jnp.float32)
     return (
         prod[:rows, :size] - prod[rows:, size:],
         prod[:rows, size:] + prod[rows:, :size],
@@ -169,10 +191,8 @@
                 jnp.concatenate([p[1] for p in pieces], axis=0),
             ))
     spec = fft_slabs(slabs, -1)
-    wr = w_ref[0]
-    wi = w_ref[1]
-    forward = jnp.concatenate([wr, wi], axis=0)
-    backward = jnp.concatenate([wr, -wi], axis=0)
+    forward = w_ref[0]
+    backward = w_ref[1]
     outs = []
     for k in range(outer):
         zr, zi = spec[k]
@@ -198,16 +218,17 @@
     length = groups * count
     outer, inner = factor_pair(length)
     block = min(width, 128)
-    table = dft_table(inner, -1.0)
+    real, imag = dft_numpy(inner, -1.0)
     turn = twiddle_table(outer, inner, length, -1.0)
-    table = jnp.stack(table)
     turn = jnp.stack(turn)[..., None]
+    parts = [split_table(np.concatenate([real, sign * imag], axis=0)) for sign in (1.0, -1.0)]
+    table = jnp.asarray(np.stack([np.concatenate([hi, hi, lo], axis=1) for hi, lo in parts]))
     return pl.pallas_call(
         rows_kernel,
         grid=(width // block,),
         in_specs=[pl.BlockSpec((groups, 2, piece.shape[2], block), lambda j: (0, 0, 0, j)) for piece in turned] + [
             pl.BlockSpec((2, length, block), lambda j: (0, 0, j)),
-            pl.BlockSpec((2, inner, inner), lambda j: (0, 0, 0)),
+            pl.BlockSpec((2, 2 * inner, 3 * inner), lambda j: (0, 0, 0)),
             pl.BlockSpec((2, outer, inner, 1), lambda j: (0, 0, 0, 0)),
         ],
         out_specs=pl.BlockSpec((groups, 2, count, block), lambda j: (0, 0, 0, j)),
@@ -263,17 +284,15 @@
         for a in range(outer)
     ]
     spec = fft_slabs(slabs, -1)
-    both = jnp.concatenate([w_ref[0], w_ref[1]], axis=1)
+    both = w_ref[0]
     count = lensed_real.shape[0]
     for k in range(outer):
         zr, zi = spec[k]
         tr = tw_ref[0, k:k + 1, :]
         ti = tw_ref[1, k:k + 1, :]
         zr, zi = zr * tr - zi * ti, zr * ti + zi * tr
-        prod = jnp.dot(
-            jnp.concatenate([zr, zi], axis=0), both,
-            precision=lax.Precision.HIGH, preferred_element_type=jnp.float32,
-        )
+        high, low = split_bf16(jnp.concatenate([zr, zi], axis=0))
+        prod = jnp.dot(jnp.concatenate([high, low, high], axis=1), both, preferred_element_type=jnp.float32)
         width = o_ref.shape[3]
         dest = (k * inner) // width
         lanes = slice((k * inner) % width, (k * inner) % width + inner)
@@ -285,7 +304,7 @@
     outer = tw_ref.shape[1]
     inner = tw_ref.shape[2]
     count = x_ref.shape[2]
-    both = jnp.concatenate([w_ref[0], -w_ref[1]], axis=1)
+    both = w_ref[1]
     outs = []
     for k in range(outer):
         width = x_ref.shape[3]
@@ -293,10 +312,8 @@
         lanes = slice((k * inner) % width, (k * inner) % width + inner)
         yr = x_ref[origin, 0, :, lanes]
         yi = x_ref[origin, 1, :, lanes]
-        prod = jnp.dot(
-            jnp.concatenate([yr, yi], axis=0), both,
-            precision=lax.Precision.HIGH, preferred_element_type=jnp.float32,
-        )
+        high, low = split_bf16(jnp.concatenate([yr, yi], axis=0))
+        prod = jnp.dot(jnp.concatenate([high, low, high], axis=1), both, preferred_element_type=jnp.float32)
         sr = prod[:count, :inner] - prod[count:, inner:]
         si = prod[:count, inner:] + prod[count:, :inner]
         tr = tw_ref[0, k:k + 1, :]
@@ -316,7 +333,9 @@
 
 def lane_tables(length):
     outer, inner = factor_pair(length)
-    table = jnp.stack(dft_table(inner, -1.0))
+    real, imag = dft_numpy(inner, -1.0)
+    parts = [split_table(np.concatenate([real, sign * imag], axis=1)) for sign in (1.0, -1.0)]
+    table = jnp.asarray(np.stack([np.concatenate([hi, hi, lo], axis=0) for hi, lo in parts]))
     turn = jnp.stack(twiddle_table(outer, inner, length, -1.0))
     return outer, inner, table, turn
 
@@ -332,7 +351,7 @@
         in_specs=[
             pl.BlockSpec((4, block, length), lambda i: (0, offset + i, 0)),
             pl.BlockSpec((2, block, length), lambda i: (0, i, 0)),
-            pl.BlockSpec((2, inner, inner), lambda i: (0, 0, 0)),
+            pl.BlockSpec((2, 3 * inner, 2 * inner), lambda i: (0, 0, 0)),
             pl.BlockSpec((2, outer, inner), lambda i: (0, 0, 0)),
         ],
         out_specs=pl.BlockSpec((groups, 2, block, length // groups), lambda i: (0, 0, i, 0)),
@@ -344,14 +363,14 @@
     groups, _, step, width = back.shape
     length = groups * width
     outer, inner, table, turn = lane_tables(length)
-    block = min(step, 32)
+    block = min(step, 64)
     return pl.pallas_call(
         lanes_inverse_kernel,
         grid=(step // block,),
         in_specs=[
             pl.BlockSpec((groups, 2, block, width), lambda i: (0, 0, i, 0)),
             pl.BlockSpec((1, 2, block, length), lambda i: (0, 0, i, 0)),
-            pl.BlockSpec((2, inner, inner), lambda i: (0, 0, 0)),
+            pl.BlockSpec((2, 3 * inner, 2 * inner), lambda i: (0, 0, 0)),
             pl.BlockSpec((2, outer, inner), lambda i: (0, 0, 0)),
         ],
         out_specs=[

time: 270 us -> 266 us (0.985)
  Pallas kernels: 48.5 us -> 44.7 us
  transfers between devices with their start and end apart: 4 -> 4, of which waited for: 3 -> 3; matrix products, arithmetic and copies ran while one was open for 6% -> 6% of each run, Pallas kernels for 7% -> 8%
where the time goes in v7:
time: 266 us; the launch traced here: 265 us
  blocking collectives  98.5 us (37%)
  waiting for transfers between devices  87.4 us (33%)
  Pallas kernels  44.7 us (17%)
  starting transfers between devices  12.4 us (5%)
  other arithmetic  11.4 us (4%)
  local copies, waits for them, and re-layouts  9.25 us (3%)
    all_to_all x1, blocking collectives, body(): lax.all_to_all(spatial, 'gx', split_axis=0, concat_axis=0, tiled=True)  98.5 us
    all_to_all x2, waiting for transfers between devices, body(): lax.all_to_all(field, 'gx', split_axis=0, concat_axis=0, tiled=True)  47.6 us
    ppermute x2, waiting for transfers between devices, shifted(): return lax.ppermute(block, axis, route)  39.7 us
    pallas_call x2, Pallas kernels, lanes_forward(): pl.pallas_call(lanes_forward_kernel, grid=(step // block,), in_specs=[pl....  13 us
    pallas_call x1, Pallas kernels, prelens(): pl.pallas_call(prelens_kernel, grid=(count // block,), in_specs=[pl.Block...  12.5 us
    pallas_call x1, Pallas kernels, rows_shift(): pl.pallas_call(rows_kernel, grid=(width // block,), in_specs=[pl.BlockSpe...  11.8 us
    all_to_all x2, starting transfers between devices, body(): lax.all_to_all(field, 'gx', split_axis=0, concat_axis=0, tiled=True)  9.86 us
    mul x1, other arithmetic, propagator(): return (real_part * scale, imag_part * scale)  8.44 us
  transfers between devices with their start and end apart: 4, of which 3 were waited for; matrix products, arithmetic and copies ran while one was open for 6% of the time, Pallas kernels for 8%

profile of v7, /device:TPU:0, one launch (start us, length us, event | category | flops | bytes accessed | tf_op | source)
XLA Modules:
  0.0 264.9 jit_solution(16980135860103101820)
XLA Ops:
  0.6 1.2 slice_bitcast_fusion.1
  1.8 1.3 collective-permute-start
  3.8 12.5 %shard_map.113.pre_ref = f32[4,256,2048]{2,1,0:T(8,128)} custom-call(f32[1,1]{1,0:T(1,128)} %bitcast.8.base_ref, bf16[1,2,256,2048]{3,2,1,0:T(8,128)(2,1)} %wave_ref.1, bf16[1,2,256,2048]{3,2,1,0:T(8,128)(2,1)} %src_ref.3, f32[1,256,2048]{2,1,0:T(8,128)} %slow_ref.1, f32[1,256,2048]{2,1,0:T(8,128)} %refl_ref.1), custom_call_target="tpu_custom_call" | custom-call | tf_op jit(solution)/shard_map/pallas_call | solution.py:258
  16.3 0.1 fusion.29
  16.3 0.6 fusion.36
  16.9 7.3 %collective-permute-done.hand_ref = bf16[2,96,2048]{2,1,0:T(8,128)(2,1)S(1)} collective-permute-done((bf16[2,96,2048]{2,1,0:T(8,128)(2,1)S(1)}, bf16[2,96,2048]{2,1,0:T(8,128)(2,1)S(1)}, u32[]{:S(2)}, u32[]{:S(2)}) %collective-permute-start) | collective-permute-done | bytes 786464 | tf_op jit(solution)/shard_map/ppermute | solution.py:21
  24.2 0.0 copy-start.3
  24.2 0.9 copy-done.3
  25.1 5.3 %shard_map.114 = f32[8,2,96,256]{3,2,1,0:T(8,128)} custom-call(f32[4,256,2048]{2,1,0:T(8,128)} %shard_map.113.pre_ref, bf16[2,96,2048]{2,1,0:T(8,128)(2,1)} %copy-done.3, bf16[2,384,256]{2,1,0:T(8,128)(2,1)} %constant.108.clone.w_ref, f32[2,16,128]{2,1,0:T(8,128)} %get-tuple-element.3.tw_ref), custom_call_target="tpu_custom_call" | custom-call | tf_op jit(solution)/shard_map/pallas_call | solution.py:348
  30.4 5.1 %all-to-all-start = ((f32[8,2,96,256]{3,2,1,0:T(8,128)}), f32[8,2,96,256]{3,2,1,0:T(8,128)S(1)}, u32[]{:S(2)}, u32[]{:S(2)}) async-start(f32[8,2,96,256]{3,2,1,0:T(8,128)} %shard_map.114), calls=%async_computation | async-start | bytes 3145728 | tf_op jit(solution)/shard_map/all_to_all | solution.py:438
  35.5 1.4 slice_bitcast_fusion
  37.0 1.3 collective-permute-start.1
  38.3 32.4 %collective-permute-done.1.hand_ref = bf16[2,160,2048]{2,1,0:T(8,128)(2,1)S(1)} collective-permute-done((bf16[2,160,2048]{2,1,0:T(8,128)(2,1)S(1)}, bf16[2,160,2048]{2,1,0:T(8,128)(2,1)S(1)}, u32[]{:S(2)}, u32[]{:S(2)}) %collective-permute-start.1) | collective-permute-done | bytes 1310752 | tf_op jit(solution)/shard_map/ppermute | solution.py:21
  70.7 0.0 copy-start.2
  70.7 1.1 copy-done.2
  71.8 7.7 %shard_map.115 = f32[8,2,160,256]{3,2,1,0:T(8,128)} custom-call(f32[4,256,2048]{2,1,0:T(8,128)} %shard_map.113.pre_ref, bf16[2,160,2048]{2,1,0:T(8,128)(2,1)} %copy-done.2, bf16[2,384,256]{2,1,0:T(8,128)(2,1)} %constant.108.clone.w_ref, f32[2,16,128]{2,1,0:T(8,128)} %get-tuple-element.3.tw_ref), custom_call_target="tpu_custom_call" | custom-call | tf_op jit(solution)/shard_map/pallas_call | solution.py:348
  79.4 0.0 all-to-all-done.refs_0_
  79.4 0.0 copy-start.1
  79.4 1.1 copy-done.1
  80.6 4.7 %all-to-all-start.1 = ((f32[8,2,160,256]{3,2,1,0:T(8,128)}), f32[8,2,160,256]{3,2,1,0:T(8,128)S(1)}, u32[]{:S(2)}, u32[]{:S(2)}) async-start(f32[8,2,160,256]{3,2,1,0:T(8,128)} %shard_map.115), calls=%async_computation.1 | async-start | bytes 5242880 | tf_op jit(solution)/shard_map/all_to_all | solution.py:438
  85.3 2.0 copy.12.refs_4_
  87.3 8.4 %fusion.2 = (f32[1,2048,256]{2,1,0:T(8,128)S(1)}, f32[1,2048,256]{2,1,0:T(8,128)S(1)}) fusion(f32[256]{0:T(256)S(1)} %fusion.35, f32[2048]{0:T(1024)S(1)} %fusion.25), kind=kLoop, calls=%fused_computation.5 | loop fusion | flops 4718592 | bytes 4203520 | tf_op jit(solution)/shard_map/mul | solution.py:404
  95.7 2.2 pad_maximum_fusion.refs_2_
  98.0 47.6 %all-to-all-done.1.refs_1_ = f32[8,2,160,256]{3,2,1,0:T(8,128)S(1)} async-done(((f32[8,2,160,256]{3,2,1,0:T(8,128)}), f32[8,2,160,256]{3,2,1,0:T(8,128)S(1)}, u32[]{:S(2)}, u32[]{:S(2)}) %all-to-all-start.1) | async-done | bytes 2621472 | tf_op jit(solution)/shard_map/all_to_all | solution.py:438
  145.6 0.0 copy-start
  145.6 1.6 copy-done
  147.2 11.8 %shard_map.116 = f32[8,2,256,256]{3,2,1,0:T(8,128)} custom-call(f32[8,2,96,256]{3,2,1,0:T(8,128)} %copy-done.1, f32[8,2,160,256]{3,2,1,0:T(8,128)} %copy-done, f32[2,2048,256]{2,1,0:T(8,128)} %pad_maximum_fusion.refs_2_, bf16[2,256,384]{2,1,0:T(8,128)(2,1)} %constant.109.clone.refs_3_, f32[2,16,128,1]{3,2,1,0:T(8,128)} %copy.12.refs_4_), custom_call_target="tpu_custom_call" | custom-call | tf_op jit(solution)/shard_map/pallas_call | solution.py:226
  159.0 98.5 %all_to_all.15.x_ref = f32[8,2,256,256]{3,2,1,0:T(8,128)} all-to-all(f32[8,2,256,256]{3,2,1,0:T(8,128)} %shard_map.116), channel_id=1, replica_groups=mesh['slab'=4,'gx'=8] {'gx'}, dimensions={0} | all-to-all | bytes 8388608 | tf_op jit(solution)/shard_map/all_to_all | solution.py:443
  257.5 7.4 %shard_map.117 = (bf16[1,2,256,2048]{3,2,1,0:T(8,128)(2,1)}, f32[1,256,2048]{2,1,0:T(8,128)}) custom-call(f32[8,2,256,256]{3,2,1,0:T(8,128)} %all_to_all.15.x_ref, bf16[1,2,256,2048]{3,2,1,0:T(8,128)(2,1)} %src_ref.3, bf16[2,384,256]{2,1,0:T(8,128)(2,1)} %constant.108.clone.w_ref, f32[2,16,128]{2,1,0:T(8,128)} %get-tuple-element.3.tw_ref), custom_call_target="tpu_custom_call" | custom-call | tf_op jit(solution)/shard_map/pallas_call | solution.py:367
  (2 shorter events, 0.0 us)
Async XLA Ops:
  1.8 22.4 %collective-permute-start = (bf16[2,96,2048]{2,1,0:T(8,128)(2,1)S(1)}, bf16[2,96,2048]{2,1,0:T(8,128)(2,1)S(1)}, u32[]{:S(2)}, u32[]{:S(2)}) collective-permute-start(bf16[2,96,2048]{2,1,0:T(8,128)(2,1)S(1)} %slice_bitcast_fusion.1), channel_id=1, source_target_pairs={{8,0},{16,8},{24,16},{9,1},{17,9},{25,17},{10,2},{18,10},{26,18},{... | collective-permute-start | bytes 2359304 | tf_op jit(solution)/shard_map/ppermute | solution.py:21
  24.2 0.9 copy-start.3
  30.4 49.0 %all-to-all-start = ((f32[8,2,96,256]{3,2,1,0:T(8,128)}), f32[8,2,96,256]{3,2,1,0:T(8,128)S(1)}, u32[]{:S(2)}, u32[]{:S(2)}) async-start(f32[8,2,96,256]{3,2,1,0:T(8,128)} %shard_map.114), calls=%async_computation | async-start | bytes 3145728 | tf_op jit(solution)/shard_map/all_to_all | solution.py:438
  37.0 33.7 %collective-permute-start.1 = (bf16[2,160,2048]{2,1,0:T(8,128)(2,1)S(1)}, bf16[2,160,2048]{2,1,0:T(8,128)(2,1)S(1)}, u32[]{:S(2)}, u32[]{:S(2)}) collective-permute-start(bf16[2,160,2048]{2,1,0:T(8,128)(2,1)S(1)} %slice_bitcast_fusion), channel_id=1, source_target_pairs={{8,0},{16,8},{24,16},{9,1},{17,9},{25,17},{10,2},{18,10},{26,18},{... | collective-permute-start | bytes 3932168 | tf_op jit(solution)/shard_map/ppermute | solution.py:21
  70.7 1.1 copy-start.2
  79.4 1.1 copy-start.1
  80.6 65.0 %all-to-all-start.1 = ((f32[8,2,160,256]{3,2,1,0:T(8,128)}), f32[8,2,160,256]{3,2,1,0:T(8,128)S(1)}, u32[]{:S(2)}, u32[]{:S(2)}) async-start(f32[8,2,160,256]{3,2,1,0:T(8,128)} %shard_map.115), calls=%async_computation.1 | async-start | bytes 5242880 | tf_op jit(solution)/shard_map/all_to_all | solution.py:438
  145.6 1.6 copy-start

commit v8 on v7

--- a/solution.py
+++ b/solution.py
@@ -343,7 +343,7 @@
 def lanes_forward(lensed, handed, first, step, groups):
     length = lensed.shape[2]
     outer, inner, table, turn = lane_tables(length)
-    block = min(step, 32)
+    block = 64 if step % 64 == 0 and first % 64 == 0 else min(step, 32)
     offset = first // block
     return pl.pallas_call(
         lanes_forward_kernel,
@@ -421,7 +421,7 @@
     columns = wavefield.shape[3]
     eighth = count // 8
     if count % 8 == 0 and eighth % 8 == 0:
-        bounds = [0, 3 * eighth, count]
+        bounds = [0, 4 * eighth, count]
     else:
         bounds = [0, count]
     groups = lax.axis_size("gx")

time: 266 us -> 265 us (level)
  waiting for transfers between devices: 87.4 us -> 90.8 us
  Pallas kernels: 44.7 us -> 41.8 us
    all_to_all x2, waiting for transfers between devices: 47.6 us -> 50.8 us  [body(): lax.all_to_all(field, 'gx', split_axis=0, concat_axis=0, tiled=True)]
    pallas_call x2, Pallas kernels: 13 us -> 10.1 us  [lanes_forward(): pl.pallas_call(lanes_forward_kernel, grid=(step // block,), in_specs=[pl....]
  transfers between devices with their start and end apart: 4 -> 4, of which waited for: 3 -> 4; matrix products, arithmetic and copies ran while one was open for 6% -> 5% of each run, Pallas kernels for 8% -> 7%
where the time goes in v8:
time: 265 us; the launch traced here: 264 us
  blocking collectives  98.5 us (37%)
  waiting for transfers between devices  90.8 us (34%)
  Pallas kernels  41.8 us (16%)
  starting transfers between devices  12.2 us (5%)
  other arithmetic  11.4 us (4%)
  local copies, waits for them, and re-layouts  8.12 us (3%)
    all_to_all x1, blocking collectives, body(): lax.all_to_all(spatial, 'gx', split_axis=0, concat_axis=0, tiled=True)  98.5 us
    all_to_all x2, waiting for transfers between devices, body(): lax.all_to_all(field, 'gx', split_axis=0, concat_axis=0, tiled=True)  50.8 us
    ppermute x2, waiting for transfers between devices, shifted(): return lax.ppermute(block, axis, route)  39.9 us
    pallas_call x1, Pallas kernels, prelens(): pl.pallas_call(prelens_kernel, grid=(count // block,), in_specs=[pl.Block...  12.5 us
    pallas_call x1, Pallas kernels, rows_shift(): pl.pallas_call(rows_kernel, grid=(width // block,), in_specs=[pl.BlockSpe...  11.8 us
    pallas_call x2, Pallas kernels, lanes_forward(): pl.pallas_call(lanes_forward_kernel, grid=(step // block,), in_specs=[pl....  10.1 us
    all_to_all x2, starting transfers between devices, body(): lax.all_to_all(field, 'gx', split_axis=0, concat_axis=0, tiled=True)  9.68 us
    mul x1, other arithmetic, propagator(): return (real_part * scale, imag_part * scale)  8.44 us
  transfers between devices with their start and end apart: 4, of which 4 were waited for; matrix products, arithmetic and copies ran while one was open for 5% of the time, Pallas kernels for 7%

profile of v8, /device:TPU:0, one launch (start us, length us, event | category | flops | bytes accessed | tf_op | source)
XLA Modules:
  0.0 264.1 jit_solution(13097585264698885543)
XLA Ops:
  0.6 2.7 %slice_bitcast_fusion = (bf16[2,128,2048]{2,1,0:T(8,128)(2,1)S(1)}, bf16[2,128,2048]{2,1,0:T(8,128)(2,1)}) fusion(bf16[1,2,256,2048]{3,2,1,0:T(8,128)(2,1)} %param.11), kind=kLoop, calls=%fused_computation.13 | loop fusion | bytes 4194304 | tf_op jit(solution)/shard_map/squeeze | solution.py:436
  3.3 1.3 collective-permute-start.1
  5.3 12.5 %shard_map.113.pre_ref = f32[4,256,2048]{2,1,0:T(8,128)} custom-call(f32[1,1]{1,0:T(1,128)} %bitcast.8.base_ref, bf16[1,2,256,2048]{3,2,1,0:T(8,128)(2,1)} %wave_ref.1, bf16[1,2,256,2048]{3,2,1,0:T(8,128)(2,1)} %src_ref.3, f32[1,256,2048]{2,1,0:T(8,128)} %slow_ref.1, f32[1,256,2048]{2,1,0:T(8,128)} %refl_ref.1), custom_call_target="tpu_custom_call" | custom-call | tf_op jit(solution)/shard_map/pallas_call | solution.py:258
  17.8 0.1 fusion.29
  17.8 0.6 fusion.36
  18.4 12.9 %collective-permute-done.1.hand_ref = bf16[2,128,2048]{2,1,0:T(8,128)(2,1)S(1)} collective-permute-done((bf16[2,128,2048]{2,1,0:T(8,128)(2,1)S(1)}, bf16[2,128,2048]{2,1,0:T(8,128)(2,1)S(1)}, u32[]{:S(2)}, u32[]{:S(2)}) %collective-permute-start.1) | collective-permute-done | bytes 1048608 | tf_op jit(solution)/shard_map/ppermute | solution.py:21
  31.3 0.0 copy-start.1
  31.3 1.1 copy-done.1
  32.4 5.1 %shard_map.115 = f32[8,2,128,256]{3,2,1,0:T(8,128)} custom-call(f32[4,256,2048]{2,1,0:T(8,128)} %shard_map.113.pre_ref, bf16[2,128,2048]{2,1,0:T(8,128)(2,1)} %copy-done.1, bf16[2,384,256]{2,1,0:T(8,128)(2,1)} %constant.108.clone.w_ref, f32[2,16,128]{2,1,0:T(8,128)} %get-tuple-element.5.tw_ref), custom_call_target="tpu_custom_call" | custom-call | tf_op jit(solution)/shard_map/pallas_call | solution.py:348
  37.5 5.1 %all-to-all-start.1 = ((f32[8,2,128,256]{3,2,1,0:T(8,128)}), f32[8,2,128,256]{3,2,1,0:T(8,128)S(1)}, u32[]{:S(2)}, u32[]{:S(2)}) async-start(f32[8,2,128,256]{3,2,1,0:T(8,128)} %shard_map.115), calls=%async_computation.1 | async-start | bytes 4194304 | tf_op jit(solution)/shard_map/all_to_all | solution.py:438
  42.6 1.3 collective-permute-start
  43.9 27.0 %collective-permute-done.hand_ref = bf16[2,128,2048]{2,1,0:T(8,128)(2,1)S(1)} collective-permute-done((bf16[2,128,2048]{2,1,0:T(8,128)(2,1)}, bf16[2,128,2048]{2,1,0:T(8,128)(2,1)S(1)}, u32[]{:S(2)}, u32[]{:S(2)}) %collective-permute-start) | collective-permute-done | bytes 1048608 | tf_op jit(solution)/shard_map/ppermute | solution.py:21
  70.9 0.0 copy-start.2
  70.9 1.1 copy-done.2
  71.9 5.1 %shard_map.114 = f32[8,2,128,256]{3,2,1,0:T(8,128)} custom-call(f32[4,256,2048]{2,1,0:T(8,128)} %shard_map.113.pre_ref, bf16[2,128,2048]{2,1,0:T(8,128)(2,1)} %copy-done.2, bf16[2,384,256]{2,1,0:T(8,128)(2,1)} %constant.108.clone.w_ref, f32[2,16,128]{2,1,0:T(8,128)} %get-tuple-element.5.tw_ref), custom_call_target="tpu_custom_call" | custom-call | tf_op jit(solution)/shard_map/pallas_call | solution.py:348
  77.0 14.6 %all-to-all-done.1.refs_1_ = f32[8,2,128,256]{3,2,1,0:T(8,128)S(1)} async-done(((f32[8,2,128,256]{3,2,1,0:T(8,128)}), f32[8,2,128,256]{3,2,1,0:T(8,128)S(1)}, u32[]{:S(2)}, u32[]{:S(2)}) %all-to-all-start.1) | async-done | bytes 2097184 | tf_op jit(solution)/shard_map/all_to_all | solution.py:438
  91.6 0.0 copy-start
  91.6 1.3 copy-done
  93.0 4.6 %all-to-all-start = ((f32[8,2,128,256]{3,2,1,0:T(8,128)}), f32[8,2,128,256]{3,2,1,0:T(8,128)}, u32[]{:S(2)}, u32[]{:S(2)}) async-start(f32[8,2,128,256]{3,2,1,0:T(8,128)} %shard_map.114), calls=%async_computation | async-start | bytes 4194304 | tf_op jit(solution)/shard_map/all_to_all | solution.py:438
  97.5 2.0 copy.12.refs_4_
  99.5 8.4 %fusion.2 = (f32[1,2048,256]{2,1,0:T(8,128)S(1)}, f32[1,2048,256]{2,1,0:T(8,128)S(1)}) fusion(f32[256]{0:T(256)S(1)} %fusion.35, f32[2048]{0:T(1024)S(1)} %fusion.25), kind=kLoop, calls=%fused_computation.5 | loop fusion | flops 4718592 | bytes 4203520 | tf_op jit(solution)/shard_map/mul | solution.py:404
  108.0 2.2 pad_maximum_fusion.refs_2_
  110.2 36.2 %all-to-all-done.refs_0_ = f32[8,2,128,256]{3,2,1,0:T(8,128)} async-done(((f32[8,2,128,256]{3,2,1,0:T(8,128)}), f32[8,2,128,256]{3,2,1,0:T(8,128)}, u32[]{:S(2)}, u32[]{:S(2)}) %all-to-all-start) | async-done | bytes 2097184 | tf_op jit(solution)/shard_map/all_to_all | solution.py:438
  146.4 11.8 %shard_map.116 = f32[8,2,256,256]{3,2,1,0:T(8,128)} custom-call(f32[8,2,128,256]{3,2,1,0:T(8,128)} %all-to-all-done.refs_0_, f32[8,2,128,256]{3,2,1,0:T(8,128)} %copy-done, f32[2,2048,256]{2,1,0:T(8,128)} %pad_maximum_fusion.refs_2_, bf16[2,256,384]{2,1,0:T(8,128)(2,1)} %constant.109.clone.refs_3_, f32[2,16,128,1]{3,2,1,0:T(8,128)} %copy.12.refs_4_), custom_call_target="tpu_custom_call" | custom-call | tf_op jit(solution)/shard_map/pallas_call | solution.py:226
  158.2 98.5 %all_to_all.15.x_ref = f32[8,2,256,256]{3,2,1,0:T(8,128)} all-to-all(f32[8,2,256,256]{3,2,1,0:T(8,128)} %shard_map.116), channel_id=1, replica_groups=mesh['slab'=4,'gx'=8] {'gx'}, dimensions={0} | all-to-all | bytes 8388608 | tf_op jit(solution)/shard_map/all_to_all | solution.py:443
  256.7 7.4 %shard_map.117 = (bf16[1,2,256,2048]{3,2,1,0:T(8,128)(2,1)}, f32[1,256,2048]{2,1,0:T(8,128)}) custom-call(f32[8,2,256,256]{3,2,1,0:T(8,128)} %all_to_all.15.x_ref, bf16[1,2,256,2048]{3,2,1,0:T(8,128)(2,1)} %src_ref.3, bf16[2,384,256]{2,1,0:T(8,128)(2,1)} %constant.108.clone.w_ref, f32[2,16,128]{2,1,0:T(8,128)} %get-tuple-element.5.tw_ref), custom_call_target="tpu_custom_call" | custom-call | tf_op jit(solution)/shard_map/pallas_call | solution.py:367
  (2 shorter events, 0.0 us)
Async XLA Ops:
  3.3 28.0 %collective-permute-start.1 = (bf16[2,128,2048]{2,1,0:T(8,128)(2,1)S(1)}, bf16[2,128,2048]{2,1,0:T(8,128)(2,1)S(1)}, u32[]{:S(2)}, u32[]{:S(2)}) collective-permute-start(bf16[2,128,2048]{2,1,0:T(8,128)(2,1)S(1)} %get-tuple-element.2), channel_id=1, source_target_pairs={{8,0},{16,8},{24,16},{9,1},{17,9},{25,17},{10,2},{18,10},{26,18},{... | collective-permute-start | bytes 3145736 | tf_op jit(solution)/shard_map/ppermute | solution.py:21
  31.3 1.1 copy-start.1
  37.5 54.2 %all-to-all-start.1 = ((f32[8,2,128,256]{3,2,1,0:T(8,128)}), f32[8,2,128,256]{3,2,1,0:T(8,128)S(1)}, u32[]{:S(2)}, u32[]{:S(2)}) async-start(f32[8,2,128,256]{3,2,1,0:T(8,128)} %shard_map.115), calls=%async_computation.1 | async-start | bytes 4194304 | tf_op jit(solution)/shard_map/all_to_all | solution.py:438
  42.6 28.3 %collective-permute-start = (bf16[2,128,2048]{2,1,0:T(8,128)(2,1)}, bf16[2,128,2048]{2,1,0:T(8,128)(2,1)S(1)}, u32[]{:S(2)}, u32[]{:S(2)}) collective-permute-start(bf16[2,128,2048]{2,1,0:T(8,128)(2,1)} %get-tuple-element.3), channel_id=1, source_target_pairs={{8,0},{16,8},{24,16},{9,1},{17,9},{25,17},{10,2},{18,10},{26,18},{... | collective-permute-start | bytes 3145736 | tf_op jit(solution)/shard_map/ppermute | solution.py:21
  70.9 1.1 copy-start.2
  91.6 1.3 copy-start
  93.0 53.5 %all-to-all-start = ((f32[8,2,128,256]{3,2,1,0:T(8,128)}), f32[8,2,128,256]{3,2,1,0:T(8,128)}, u32[]{:S(2)}, u32[]{:S(2)}) async-start(f32[8,2,128,256]{3,2,1,0:T(8,128)} %shard_map.114), calls=%async_computation | async-start | bytes 4194304 | tf_op jit(solution)/shard_map/all_to_all | solution.py:438

commit v9 on v8

--- a/solution.py
+++ b/solution.py
@@ -270,11 +270,11 @@
     )(base.reshape(1, 1), wavefield, source, slowness, reflectivity)
 
 
-def lanes_forward_kernel(pre_ref, hand_ref, w_ref, tw_ref, o_ref):
+def lanes_forward_kernel(pre_ref, real_ref, imag_ref, w_ref, tw_ref, o_ref):
     outer = tw_ref.shape[1]
     inner = tw_ref.shape[2]
-    hand_real = hand_ref[0].astype(jnp.float32)
-    hand_imag = hand_ref[1].astype(jnp.float32)
+    hand_real = real_ref[...].astype(jnp.float32)
+    hand_imag = imag_ref[...].astype(jnp.float32)
     cosine = pre_ref[2]
     sine = pre_ref[3]
     lensed_real = pre_ref[0] + (hand_real * cosine - hand_imag * sine)
@@ -350,13 +350,14 @@
         grid=(step // block,),
         in_specs=[
             pl.BlockSpec((4, block, length), lambda i: (0, offset + i, 0)),
-            pl.BlockSpec((2, block, length), lambda i: (0, i, 0)),
+            pl.BlockSpec((block, length), lambda i: (i, 0)),
+            pl.BlockSpec((block, length), lambda i: (i, 0)),
             pl.BlockSpec((2, 3 * inner, 2 * inner), lambda i: (0, 0, 0)),
             pl.BlockSpec((2, outer, inner), lambda i: (0, 0, 0)),
         ],
         out_specs=pl.BlockSpec((groups, 2, block, length // groups), lambda i: (0, 0, i, 0)),
         out_shape=jax.ShapeDtypeStruct((groups, 2, step, length // groups), jnp.float32),
-    )(lensed, handed, table, turn)
+    )(lensed, handed[0], handed[1], table, turn)
 
 
 def lanes_inverse(back, source):
@@ -433,7 +434,7 @@
     pieces = []
     lensed = prelens(wavefield, source, slowness, reflectivity, base)
     for first, last in zip(bounds[:-1], bounds[1:]):
-        handed = shifted(boundary[0, :, first:last], "slab", -1)
+        handed = shifted((boundary[0, 0, first:last], boundary[0, 1, first:last]), "slab", -1)
         field = lanes_forward(lensed, handed, first, last - first, groups)
         pieces.append(lax.all_to_all(field, "gx", split_axis=0, concat_axis=0, tiled=True))
     freq_row = permuted_freq(jnp.arange(total_rows, dtype=jnp.int32), total_rows)

time: 265 us -> 265 us (level)
    ppermute x2 -> x4, waiting for transfers between devices: 39.9 us -> 37.3 us  [shifted(): return lax.ppermute(block, axis, route)]
  transfers between devices with their start and end apart: 4 -> 6, of which waited for: 4 -> 6; matrix products, arithmetic and copies ran while one was open for 5% -> 5% of each run, Pallas kernels for 7% -> 7%
where the time goes in v9:
time: 265 us; the launch traced here: 264 us
  blocking collectives  98.5 us (37%)
  waiting for transfers between devices  88.3 us (33%)
  Pallas kernels  41.8 us (16%)
  starting transfers between devices  14.8 us (6%)
  other arithmetic  11.4 us (4%)
  local copies, waits for them, and re-layouts  7.65 us (3%)
    all_to_all x1, blocking collectives, body(): lax.all_to_all(spatial, 'gx', split_axis=0, concat_axis=0, tiled=True)  98.5 us
    all_to_all x2, waiting for transfers between devices, body(): lax.all_to_all(field, 'gx', split_axis=0, concat_axis=0, tiled=True)  51 us
    ppermute x4, waiting for transfers between devices, shifted(): return lax.ppermute(block, axis, route)  37.3 us
    pallas_call x1, Pallas kernels, prelens(): pl.pallas_call(prelens_kernel, grid=(count // block,), in_specs=[pl.Block...  12.5 us
    pallas_call x1, Pallas kernels, rows_shift(): pl.pallas_call(rows_kernel, grid=(width // block,), in_specs=[pl.BlockSpe...  11.8 us
    pallas_call x2, Pallas kernels, lanes_forward(): pl.pallas_call(lanes_forward_kernel, grid=(step // block,), in_specs=[pl....  10.1 us
    all_to_all x2, starting transfers between devices, body(): lax.all_to_all(field, 'gx', split_axis=0, concat_axis=0, tiled=True)  9.66 us
    mul x1, other arithmetic, propagator(): return (real_part * scale, imag_part * scale)  8.44 us
  transfers between devices with their start and end apart: 6, of which 6 were waited for; matrix products, arithmetic and copies ran while one was open for 5% of the time, Pallas kernels for 7%

profile of v9, /device:TPU:0, one launch (start us, length us, event | category | flops | bytes accessed | tf_op | source)
XLA Modules:
  0.0 263.9 jit_solution(16915556680253840814)
XLA Ops:
  0.6 2.7 %slice_bitcast_fusion = (bf16[128,2048]{1,0:T(8,128)(2,1)S(1)}, bf16[128,2048]{1,0:T(8,128)(2,1)}, bf16[128,2048]{1,0:T(8,128)(2,1)}, bf16[128,2048]{1,0:T(8,128)(2,1)S(1)}) fusion(bf16[1,2,256,2048]{3,2,1,0:T(8,128)(2,1)} %param.11), kind=kLoop, calls=%fused_computation.13 | loop fusion | bytes 4194304 | tf_op jit(solution)/shard_map/squeeze | solution.py:437
  3.3 1.3 collective-permute-start.2
  4.6 1.3 collective-permute-start.3
  6.6 12.5 %shard_map.113.pre_ref = f32[4,256,2048]{2,1,0:T(8,128)} custom-call(f32[1,1]{1,0:T(1,128)} %bitcast.12.base_ref, bf16[1,2,256,2048]{3,2,1,0:T(8,128)(2,1)} %wave_ref.1, bf16[1,2,256,2048]{3,2,1,0:T(8,128)(2,1)} %src_ref.3, f32[1,256,2048]{2,1,0:T(8,128)} %slow_ref.1, f32[1,256,2048]{2,1,0:T(8,128)} %refl_ref.1), custom_call_target="tpu_custom_call" | custom-call | tf_op jit(solution)/shard_map/pallas_call | solution.py:258
  19.1 0.1 fusion.29
  19.1 0.6 fusion.36
  19.7 1.2 collective-permute-done.2.real_ref
  20.9 0.0 copy-start.1
  20.9 10.4 %collective-permute-done.3.imag_ref = bf16[128,2048]{1,0:T(8,128)(2,1)S(1)} collective-permute-done((bf16[128,2048]{1,0:T(8,128)(2,1)S(1)}, bf16[128,2048]{1,0:T(8,128)(2,1)S(1)}, u32[]{:S(2)}, u32[]{:S(2)}) %collective-permute-start.3) | collective-permute-done | bytes 524320 | tf_op jit(solution)/shard_map/ppermute | solution.py:21
  31.3 0.0 copy-start.2
  31.3 0.0 copy-done.1
  31.3 0.8 copy-done.2
  32.1 5.1 %shard_map.115 = f32[8,2,128,256]{3,2,1,0:T(8,128)} custom-call(f32[4,256,2048]{2,1,0:T(8,128)} %shard_map.113.pre_ref, bf16[128,2048]{1,0:T(8,128)(2,1)} %copy-done.1, bf16[128,2048]{1,0:T(8,128)(2,1)} %copy-done.2, bf16[2,384,256]{2,1,0:T(8,128)(2,1)} %constant.108.clone.w_ref, f32[2,16,128]{2,1,0:T(8,128)} %get-tuple-element.7.tw_ref), custom_call_target="tpu_custom_call" | custom-call | tf_op jit(solution)/shard_map/pallas_call | solution.py:348
  37.2 5.1 %all-to-all-start.1 = ((f32[8,2,128,256]{3,2,1,0:T(8,128)}), f32[8,2,128,256]{3,2,1,0:T(8,128)S(1)}, u32[]{:S(2)}, u32[]{:S(2)}) async-start(f32[8,2,128,256]{3,2,1,0:T(8,128)} %shard_map.115), calls=%async_computation.1 | async-start | bytes 4194304 | tf_op jit(solution)/shard_map/all_to_all | solution.py:439
  42.3 1.3 collective-permute-start
  43.6 1.3 collective-permute-start.1
  44.9 14.7 %collective-permute-done.real_ref = bf16[128,2048]{1,0:T(8,128)(2,1)S(1)} collective-permute-done((bf16[128,2048]{1,0:T(8,128)(2,1)}, bf16[128,2048]{1,0:T(8,128)(2,1)S(1)}, u32[]{:S(2)}, u32[]{:S(2)}) %collective-permute-start) | collective-permute-done | bytes 524320 | tf_op jit(solution)/shard_map/ppermute | solution.py:21
  59.6 0.0 copy-start.3
  59.6 11.1 %collective-permute-done.1.imag_ref = bf16[128,2048]{1,0:T(8,128)(2,1)S(1)} collective-permute-done((bf16[128,2048]{1,0:T(8,128)(2,1)}, bf16[128,2048]{1,0:T(8,128)(2,1)S(1)}, u32[]{:S(2)}, u32[]{:S(2)}) %collective-permute-start.1) | collective-permute-done | bytes 524320 | tf_op jit(solution)/shard_map/ppermute | solution.py:21
  70.6 0.0 copy-done.3
  70.6 0.0 copy-start.4
  70.6 0.8 copy-done.4
  71.5 5.1 %shard_map.114 = f32[8,2,128,256]{3,2,1,0:T(8,128)} custom-call(f32[4,256,2048]{2,1,0:T(8,128)} %shard_map.113.pre_ref, bf16[128,2048]{1,0:T(8,128)(2,1)} %copy-done.3, bf16[128,2048]{1,0:T(8,128)(2,1)} %copy-done.4, bf16[2,384,256]{2,1,0:T(8,128)(2,1)} %constant.108.clone.w_ref, f32[2,16,128]{2,1,0:T(8,128)} %get-tuple-element.7.tw_ref), custom_call_target="tpu_custom_call" | custom-call | tf_op jit(solution)/shard_map/pallas_call | solution.py:348
  76.5 14.9 %all-to-all-done.1.refs_1_ = f32[8,2,128,256]{3,2,1,0:T(8,128)S(1)} async-done(((f32[8,2,128,256]{3,2,1,0:T(8,128)}), f32[8,2,128,256]{3,2,1,0:T(8,128)S(1)}, u32[]{:S(2)}, u32[]{:S(2)}) %all-to-all-start.1) | async-done | bytes 2097184 | tf_op jit(solution)/shard_map/all_to_all | solution.py:439
  91.4 0.0 copy-start
  91.4 1.3 copy-done
  92.7 4.5 %all-to-all-start = ((f32[8,2,128,256]{3,2,1,0:T(8,128)}), f32[8,2,128,256]{3,2,1,0:T(8,128)}, u32[]{:S(2)}, u32[]{:S(2)}) async-start(f32[8,2,128,256]{3,2,1,0:T(8,128)} %shard_map.114), calls=%async_computation | async-start | bytes 4194304 | tf_op jit(solution)/shard_map/all_to_all | solution.py:439
  97.3 2.0 copy.12.refs_4_
  99.3 8.4 %fusion.2 = (f32[1,2048,256]{2,1,0:T(8,128)S(1)}, f32[1,2048,256]{2,1,0:T(8,128)S(1)}) fusion(f32[256]{0:T(256)S(1)} %fusion.35, f32[2048]{0:T(1024)S(1)} %fusion.25), kind=kLoop, calls=%fused_computation.5 | loop fusion | flops 4718592 | bytes 4203520 | tf_op jit(solution)/shard_map/mul | solution.py:405
  107.7 2.3 pad_maximum_fusion.refs_2_
  110.0 36.2 %all-to-all-done.refs_0_ = f32[8,2,128,256]{3,2,1,0:T(8,128)} async-done(((f32[8,2,128,256]{3,2,1,0:T(8,128)}), f32[8,2,128,256]{3,2,1,0:T(8,128)}, u32[]{:S(2)}, u32[]{:S(2)}) %all-to-all-start) | async-done | bytes 2097184 | tf_op jit(solution)/shard_map/all_to_all | solution.py:439
  146.1 11.8 %shard_map.116 = f32[8,2,256,256]{3,2,1,0:T(8,128)} custom-call(f32[8,2,128,256]{3,2,1,0:T(8,128)} %all-to-all-done.refs_0_, f32[8,2,128,256]{3,2,1,0:T(8,128)} %copy-done, f32[2,2048,256]{2,1,0:T(8,128)} %pad_maximum_fusion.refs_2_, bf16[2,256,384]{2,1,0:T(8,128)(2,1)} %constant.109.clone.refs_3_, f32[2,16,128,1]{3,2,1,0:T(8,128)} %copy.12.refs_4_), custom_call_target="tpu_custom_call" | custom-call | tf_op jit(solution)/shard_map/pallas_call | solution.py:226
  157.9 98.5 %all_to_all.15.x_ref = f32[8,2,256,256]{3,2,1,0:T(8,128)} all-to-all(f32[8,2,256,256]{3,2,1,0:T(8,128)} %shard_map.116), channel_id=1, replica_groups=mesh['slab'=4,'gx'=8] {'gx'}, dimensions={0} | all-to-all | bytes 8388608 | tf_op jit(solution)/shard_map/all_to_all | solution.py:444
  256.4 7.4 %shard_map.117 = (bf16[1,2,256,2048]{3,2,1,0:T(8,128)(2,1)}, f32[1,256,2048]{2,1,0:T(8,128)}) custom-call(f32[8,2,256,256]{3,2,1,0:T(8,128)} %all_to_all.15.x_ref, bf16[1,2,256,2048]{3,2,1,0:T(8,128)(2,1)} %src_ref.3, bf16[2,384,256]{2,1,0:T(8,128)(2,1)} %constant.108.clone.w_ref, f32[2,16,128]{2,1,0:T(8,128)} %get-tuple-element.7.tw_ref), custom_call_target="tpu_custom_call" | custom-call | tf_op jit(solution)/shard_map/pallas_call | solution.py:368
  (2 shorter events, 0.0 us)
Async XLA Ops:
  3.3 17.6 %collective-permute-start.2 = (bf16[128,2048]{1,0:T(8,128)(2,1)S(1)}, bf16[128,2048]{1,0:T(8,128)(2,1)S(1)}, u32[]{:S(2)}, u32[]{:S(2)}) collective-permute-start(bf16[128,2048]{1,0:T(8,128)(2,1)S(1)} %get-tuple-element.5), channel_id=1, source_target_pairs={{8,0},{16,8},{24,16},{9,1},{17,9},{25,17},{10,2},{18,10},{26,18},{... | collective-permute-start | bytes 1572872 | tf_op jit(solution)/shard_map/ppermute | solution.py:21
  4.6 26.7 %collective-permute-start.3 = (bf16[128,2048]{1,0:T(8,128)(2,1)S(1)}, bf16[128,2048]{1,0:T(8,128)(2,1)S(1)}, u32[]{:S(2)}, u32[]{:S(2)}) collective-permute-start(bf16[128,2048]{1,0:T(8,128)(2,1)S(1)} %get-tuple-element.2), channel_id=1, source_target_pairs={{8,0},{16,8},{24,16},{9,1},{17,9},{25,17},{10,2},{18,10},{26,18},{... | collective-permute-start | bytes 1572872 | tf_op jit(solution)/shard_map/ppermute | solution.py:21
  20.9 10.4 %copy-start.1 = (bf16[128,2048]{1,0:T(8,128)(2,1)}, bf16[128,2048]{1,0:T(8,128)(2,1)S(1)}, u32[]{:S(2)}) copy-start(bf16[128,2048]{1,0:T(8,128)(2,1)S(1)} %collective-permute-done.2.real_ref) | copy-start | bytes 1572868
  31.3 0.8 copy-start.2
  37.2 54.2 %all-to-all-start.1 = ((f32[8,2,128,256]{3,2,1,0:T(8,128)}), f32[8,2,128,256]{3,2,1,0:T(8,128)S(1)}, u32[]{:S(2)}, u32[]{:S(2)}) async-start(f32[8,2,128,256]{3,2,1,0:T(8,128)} %shard_map.115), calls=%async_computation.1 | async-start | bytes 4194304 | tf_op jit(solution)/shard_map/all_to_all | solution.py:439
  42.3 17.3 %collective-permute-start = (bf16[128,2048]{1,0:T(8,128)(2,1)}, bf16[128,2048]{1,0:T(8,128)(2,1)S(1)}, u32[]{:S(2)}, u32[]{:S(2)}) collective-permute-start(bf16[128,2048]{1,0:T(8,128)(2,1)} %get-tuple-element.4), channel_id=1, source_target_pairs={{8,0},{16,8},{24,16},{9,1},{17,9},{25,17},{10,2},{18,10},{26,18},{... | collective-permute-start | bytes 1572872 | tf_op jit(solution)/shard_map/ppermute | solution.py:21
  43.6 27.0 %collective-permute-start.1 = (bf16[128,2048]{1,0:T(8,128)(2,1)}, bf16[128,2048]{1,0:T(8,128)(2,1)S(1)}, u32[]{:S(2)}, u32[]{:S(2)}) collective-permute-start(bf16[128,2048]{1,0:T(8,128)(2,1)} %get-tuple-element.3), channel_id=1, source_target_pairs={{8,0},{16,8},{24,16},{9,1},{17,9},{25,17},{10,2},{18,10},{26,18},{... | collective-permute-start | bytes 1572872 | tf_op jit(solution)/shard_map/ppermute | solution.py:21
  59.6 11.1 %copy-start.3 = (bf16[128,2048]{1,0:T(8,128)(2,1)}, bf16[128,2048]{1,0:T(8,128)(2,1)S(1)}, u32[]{:S(2)}) copy-start(bf16[128,2048]{1,0:T(8,128)(2,1)S(1)} %collective-permute-done.real_ref) | copy-start | bytes 1572868
  70.6 0.8 copy-start.4
  91.4 1.3 copy-start
  92.7 53.4 %all-to-all-start = ((f32[8,2,128,256]{3,2,1,0:T(8,128)}), f32[8,2,128,256]{3,2,1,0:T(8,128)}, u32[]{:S(2)}, u32[]{:S(2)}) async-start(f32[8,2,128,256]{3,2,1,0:T(8,128)} %shard_map.114), calls=%async_computation | async-start | bytes 4194304 | tf_op jit(solution)/shard_map/all_to_all | solution.py:439

commit v10 on v8

--- a/solution.py
+++ b/solution.py
@@ -343,7 +343,7 @@
 def lanes_forward(lensed, handed, first, step, groups):
     length = lensed.shape[2]
     outer, inner, table, turn = lane_tables(length)
-    block = 64 if step % 64 == 0 and first % 64 == 0 else min(step, 32)
+    block = 128 if step % 128 == 0 and first % 128 == 0 else min(step, 32)
     offset = first // block
     return pl.pallas_call(
         lanes_forward_kernel,

time: 265 us -> 266 us (level)
  no operation moved by 1% of the time
where the time goes in v10:
time: 266 us; the launch traced here: 265 us
  blocking collectives  98.5 us (37%)
  waiting for transfers between devices  89.7 us (34%)
  Pallas kernels  43.8 us (16%)
  starting transfers between devices  12.2 us (5%)
  other arithmetic  11.4 us (4%)
  local copies, waits for them, and re-layouts  8.12 us (3%)
    all_to_all x1, blocking collectives, body(): lax.all_to_all(spatial, 'gx', split_axis=0, concat_axis=0, tiled=True)  98.5 us
    all_to_all x2, waiting for transfers between devices, body(): lax.all_to_all(field, 'gx', split_axis=0, concat_axis=0, tiled=True)  49.8 us
    ppermute x2, waiting for transfers between devices, shifted(): return lax.ppermute(block, axis, route)  39.9 us
    pallas_call x1, Pallas kernels, prelens(): pl.pallas_call(prelens_kernel, grid=(count // block,), in_specs=[pl.Block...  12.5 us
    pallas_call x2, Pallas kernels, lanes_forward(): pl.pallas_call(lanes_forward_kernel, grid=(step // block,), in_specs=[pl....  12.1 us
    pallas_call x1, Pallas kernels, rows_shift(): pl.pallas_call(rows_kernel, grid=(width // block,), in_specs=[pl.BlockSpe...  11.8 us
    all_to_all x2, starting transfers between devices, body(): lax.all_to_all(field, 'gx', split_axis=0, concat_axis=0, tiled=True)  9.68 us
    mul x1, other arithmetic, propagator(): return (real_part * scale, imag_part * scale)  8.44 us
  transfers between devices with their start and end apart: 4, of which 4 were waited for; matrix products, arithmetic and copies ran while one was open for 5% of the time, Pallas kernels for 7%

profile of v10, /device:TPU:0, one launch (start us, length us, event | category | flops | bytes accessed | tf_op | source)
XLA Modules:
  0.0 265.1 jit_solution(7576069763061975220)
XLA Ops:
  0.6 2.7 %slice_bitcast_fusion = (bf16[2,128,2048]{2,1,0:T(8,128)(2,1)S(1)}, bf16[2,128,2048]{2,1,0:T(8,128)(2,1)}) fusion(bf16[1,2,256,2048]{3,2,1,0:T(8,128)(2,1)} %param.11), kind=kLoop, calls=%fused_computation.13 | loop fusion | bytes 4194304 | tf_op jit(solution)/shard_map/squeeze | solution.py:436
  3.3 1.3 collective-permute-start.1
  5.3 12.5 %shard_map.113.pre_ref = f32[4,256,2048]{2,1,0:T(8,128)} custom-call(f32[1,1]{1,0:T(1,128)} %bitcast.8.base_ref, bf16[1,2,256,2048]{3,2,1,0:T(8,128)(2,1)} %wave_ref.1, bf16[1,2,256,2048]{3,2,1,0:T(8,128)(2,1)} %src_ref.3, f32[1,256,2048]{2,1,0:T(8,128)} %slow_ref.1, f32[1,256,2048]{2,1,0:T(8,128)} %refl_ref.1), custom_call_target="tpu_custom_call" | custom-call | tf_op jit(solution)/shard_map/pallas_call | solution.py:258
  17.8 0.1 fusion.29
  17.8 0.6 fusion.36
  18.4 12.9 %collective-permute-done.1.hand_ref = bf16[2,128,2048]{2,1,0:T(8,128)(2,1)S(1)} collective-permute-done((bf16[2,128,2048]{2,1,0:T(8,128)(2,1)S(1)}, bf16[2,128,2048]{2,1,0:T(8,128)(2,1)S(1)}, u32[]{:S(2)}, u32[]{:S(2)}) %collective-permute-start.1) | collective-permute-done | bytes 1048608 | tf_op jit(solution)/shard_map/ppermute | solution.py:21
  31.3 0.0 copy-start.1
  31.3 1.1 copy-done.1
  32.4 6.1 %shard_map.115 = f32[8,2,128,256]{3,2,1,0:T(8,128)} custom-call(f32[4,256,2048]{2,1,0:T(8,128)} %shard_map.113.pre_ref, bf16[2,128,2048]{2,1,0:T(8,128)(2,1)} %copy-done.1, bf16[2,384,256]{2,1,0:T(8,128)(2,1)} %constant.108.clone.w_ref, f32[2,16,128]{2,1,0:T(8,128)} %get-tuple-element.5.tw_ref), custom_call_target="tpu_custom_call" | custom-call | tf_op jit(solution)/shard_map/pallas_call | solution.py:348
  38.5 5.1 %all-to-all-start.1 = ((f32[8,2,128,256]{3,2,1,0:T(8,128)}), f32[8,2,128,256]{3,2,1,0:T(8,128)S(1)}, u32[]{:S(2)}, u32[]{:S(2)}) async-start(f32[8,2,128,256]{3,2,1,0:T(8,128)} %shard_map.115), calls=%async_computation.1 | async-start | bytes 4194304 | tf_op jit(solution)/shard_map/all_to_all | solution.py:438
  43.6 1.3 collective-permute-start
  44.9 27.0 %collective-permute-done.hand_ref = bf16[2,128,2048]{2,1,0:T(8,128)(2,1)S(1)} collective-permute-done((bf16[2,128,2048]{2,1,0:T(8,128)(2,1)}, bf16[2,128,2048]{2,1,0:T(8,128)(2,1)S(1)}, u32[]{:S(2)}, u32[]{:S(2)}) %collective-permute-start) | collective-permute-done | bytes 1048608 | tf_op jit(solution)/shard_map/ppermute | solution.py:21
  71.9 0.0 copy-start.2
  71.9 1.1 copy-done.2
  73.0 6.1 %shard_map.114 = f32[8,2,128,256]{3,2,1,0:T(8,128)} custom-call(f32[4,256,2048]{2,1,0:T(8,128)} %shard_map.113.pre_ref, bf16[2,128,2048]{2,1,0:T(8,128)(2,1)} %copy-done.2, bf16[2,384,256]{2,1,0:T(8,128)(2,1)} %constant.108.clone.w_ref, f32[2,16,128]{2,1,0:T(8,128)} %get-tuple-element.5.tw_ref), custom_call_target="tpu_custom_call" | custom-call | tf_op jit(solution)/shard_map/pallas_call | solution.py:348
  79.0 13.6 %all-to-all-done.1.refs_1_ = f32[8,2,128,256]{3,2,1,0:T(8,128)S(1)} async-done(((f32[8,2,128,256]{3,2,1,0:T(8,128)}), f32[8,2,128,256]{3,2,1,0:T(8,128)S(1)}, u32[]{:S(2)}, u32[]{:S(2)}) %all-to-all-start.1) | async-done | bytes 2097184 | tf_op jit(solution)/shard_map/all_to_all | solution.py:438
  92.6 0.0 copy-start
  92.6 1.3 copy-done
  94.0 4.6 %all-to-all-start = ((f32[8,2,128,256]{3,2,1,0:T(8,128)}), f32[8,2,128,256]{3,2,1,0:T(8,128)}, u32[]{:S(2)}, u32[]{:S(2)}) async-start(f32[8,2,128,256]{3,2,1,0:T(8,128)} %shard_map.114), calls=%async_computation | async-start | bytes 4194304 | tf_op jit(solution)/shard_map/all_to_all | solution.py:438
  98.5 2.0 copy.12.refs_4_
  100.5 8.4 %fusion.2 = (f32[1,2048,256]{2,1,0:T(8,128)S(1)}, f32[1,2048,256]{2,1,0:T(8,128)S(1)}) fusion(f32[256]{0:T(256)S(1)} %fusion.35, f32[2048]{0:T(1024)S(1)} %fusion.25), kind=kLoop, calls=%fused_computation.5 | loop fusion | flops 4718592 | bytes 4203520 | tf_op jit(solution)/shard_map/mul | solution.py:404
  109.0 2.2 pad_maximum_fusion.refs_2_
  111.2 36.2 %all-to-all-done.refs_0_ = f32[8,2,128,256]{3,2,1,0:T(8,128)} async-done(((f32[8,2,128,256]{3,2,1,0:T(8,128)}), f32[8,2,128,256]{3,2,1,0:T(8,128)}, u32[]{:S(2)}, u32[]{:S(2)}) %all-to-all-start) | async-done | bytes 2097184 | tf_op jit(solution)/shard_map/all_to_all | solution.py:438
  147.4 11.8 %shard_map.116 = f32[8,2,256,256]{3,2,1,0:T(8,128)} custom-call(f32[8,2,128,256]{3,2,1,0:T(8,128)} %all-to-all-done.refs_0_, f32[8,2,128,256]{3,2,1,0:T(8,128)} %copy-done, f32[2,2048,256]{2,1,0:T(8,128)} %pad_maximum_fusion.refs_2_, bf16[2,256,384]{2,1,0:T(8,128)(2,1)} %constant.109.clone.refs_3_, f32[2,16,128,1]{3,2,1,0:T(8,128)} %copy.12.refs_4_), custom_call_target="tpu_custom_call" | custom-call | tf_op jit(solution)/shard_map/pallas_call | solution.py:226
  159.2 98.5 %all_to_all.15.x_ref = f32[8,2,256,256]{3,2,1,0:T(8,128)} all-to-all(f32[8,2,256,256]{3,2,1,0:T(8,128)} %shard_map.116), channel_id=1, replica_groups=mesh['slab'=4,'gx'=8] {'gx'}, dimensions={0} | all-to-all | bytes 8388608 | tf_op jit(solution)/shard_map/all_to_all | solution.py:443
  257.7 7.4 %shard_map.117 = (bf16[1,2,256,2048]{3,2,1,0:T(8,128)(2,1)}, f32[1,256,2048]{2,1,0:T(8,128)}) custom-call(f32[8,2,256,256]{3,2,1,0:T(8,128)} %all_to_all.15.x_ref, bf16[1,2,256,2048]{3,2,1,0:T(8,128)(2,1)} %src_ref.3, bf16[2,384,256]{2,1,0:T(8,128)(2,1)} %constant.108.clone.w_ref, f32[2,16,128]{2,1,0:T(8,128)} %get-tuple-element.5.tw_ref), custom_call_target="tpu_custom_call" | custom-call | tf_op jit(solution)/shard_map/pallas_call | solution.py:367
  (2 shorter events, 0.0 us)
Async XLA Ops:
  3.3 28.0 %collective-permute-start.1 = (bf16[2,128,2048]{2,1,0:T(8,128)(2,1)S(1)}, bf16[2,128,2048]{2,1,0:T(8,128)(2,1)S(1)}, u32[]{:S(2)}, u32[]{:S(2)}) collective-permute-start(bf16[2,128,2048]{2,1,0:T(8,128)(2,1)S(1)} %get-tuple-element.2), channel_id=1, source_target_pairs={{8,0},{16,8},{24,16},{9,1},{17,9},{25,17},{10,2},{18,10},{26,18},{... | collective-permute-start | bytes 3145736 | tf_op jit(solution)/shard_map/ppermute | solution.py:21
  31.3 1.1 copy-start.1
  38.5 54.2 %all-to-all-start.1 = ((f32[8,2,128,256]{3,2,1,0:T(8,128)}), f32[8,2,128,256]{3,2,1,0:T(8,128)S(1)}, u32[]{:S(2)}, u32[]{:S(2)}) async-start(f32[8,2,128,256]{3,2,1,0:T(8,128)} %shard_map.115), calls=%async_computation.1 | async-start | bytes 4194304 | tf_op jit(solution)/shard_map/all_to_all | solution.py:438
  43.6 28.3 %collective-permute-start = (bf16[2,128,2048]{2,1,0:T(8,128)(2,1)}, bf16[2,128,2048]{2,1,0:T(8,128)(2,1)S(1)}, u32[]{:S(2)}, u32[]{:S(2)}) collective-permute-start(bf16[2,128,2048]{2,1,0:T(8,128)(2,1)} %get-tuple-element.3), channel_id=1, source_target_pairs={{8,0},{16,8},{24,16},{9,1},{17,9},{25,17},{10,2},{18,10},{26,18},{... | collective-permute-start | bytes 3145736 | tf_op jit(solution)/shard_map/ppermute | solution.py:21
  71.9 1.1 copy-start.2
  92.6 1.3 copy-start
  94.0 53.5 %all-to-all-start = ((f32[8,2,128,256]{3,2,1,0:T(8,128)}), f32[8,2,128,256]{3,2,1,0:T(8,128)}, u32[]{:S(2)}, u32[]{:S(2)}) async-start(f32[8,2,128,256]{3,2,1,0:T(8,128)} %shard_map.114), calls=%async_computation | async-start | bytes 4194304 | tf_op jit(solution)/shard_map/all_to_all | solution.py:438

commit v11 on v8

--- a/solution.py
+++ b/solution.py
@@ -284,15 +284,17 @@
         for a in range(outer)
     ]
     spec = fft_slabs(slabs, -1)
-    both = w_ref[0]
+    both = jnp.concatenate([w_ref[0], w_ref[1]], axis=1)
     count = lensed_real.shape[0]
     for k in range(outer):
         zr, zi = spec[k]
         tr = tw_ref[0, k:k + 1, :]
         ti = tw_ref[1, k:k + 1, :]
         zr, zi = zr * tr - zi * ti, zr * ti + zi * tr
-        high, low = split_bf16(jnp.concatenate([zr, zi], axis=0))
-        prod = jnp.dot(jnp.concatenate([high, low, high], axis=1), both, preferred_element_type=jnp.float32)
+        prod = jnp.dot(
+            jnp.concatenate([zr, zi], axis=0), both,
+            precision=lax.Precision.HIGH, preferred_element_type=jnp.float32,
+        )
         width = o_ref.shape[3]
         dest = (k * inner) // width
         lanes = slice((k * inner) % width, (k * inner) % width + inner)
@@ -342,7 +344,8 @@
 
 def lanes_forward(lensed, handed, first, step, groups):
     length = lensed.shape[2]
-    outer, inner, table, turn = lane_tables(length)
+    outer, inner, _, turn = lane_tables(length)
+    table = jnp.stack(dft_table(inner, -1.0))
     block = 64 if step % 64 == 0 and first % 64 == 0 else min(step, 32)
     offset = first // block
     return pl.pallas_call(
@@ -351,7 +354,7 @@
         in_specs=[
             pl.BlockSpec((4, block, length), lambda i: (0, offset + i, 0)),
             pl.BlockSpec((2, block, length), lambda i: (0, i, 0)),
-            pl.BlockSpec((2, 3 * inner, 2 * inner), lambda i: (0, 0, 0)),
+            pl.BlockSpec((2, inner, inner), lambda i: (0, 0, 0)),
             pl.BlockSpec((2, outer, inner), lambda i: (0, 0, 0)),
         ],
         out_specs=pl.BlockSpec((groups, 2, block, length // groups), lambda i: (0, 0, i, 0)),

time: 265 us -> 265 us (level)
  no operation moved by 1% of the time
where the time goes in v11:
time: 265 us; the launch traced here: 264 us
  blocking collectives  98.5 us (37%)
  waiting for transfers between devices  89.5 us (34%)
  Pallas kernels  42.4 us (16%)
  other arithmetic  12.3 us (5%)
  starting transfers between devices  12.2 us (5%)
  local copies, waits for them, and re-layouts  8.15 us (3%)
    all_to_all x1, blocking collectives, body(): lax.all_to_all(spatial, 'gx', split_axis=0, concat_axis=0, tiled=True)  98.5 us
    all_to_all x2, waiting for transfers between devices, body(): lax.all_to_all(field, 'gx', split_axis=0, concat_axis=0, tiled=True)  50.5 us
    ppermute x2, waiting for transfers between devices, shifted(): return lax.ppermute(block, axis, route)  39 us
    pallas_call x1, Pallas kernels, prelens(): pl.pallas_call(prelens_kernel, grid=(count // block,), in_specs=[pl.Block...  12.5 us
    pallas_call x1, Pallas kernels, rows_shift(): pl.pallas_call(rows_kernel, grid=(width // block,), in_specs=[pl.BlockSpe...  11.8 us
    pallas_call x2, Pallas kernels, lanes_forward(): pl.pallas_call(lanes_forward_kernel, grid=(step // block,), in_specs=[pl....  10.7 us
    all_to_all x2, starting transfers between devices, body(): lax.all_to_all(field, 'gx', split_axis=0, concat_axis=0, tiled=True)  9.68 us
    mul x1, other arithmetic, propagator(): return (real_part * scale, imag_part * scale)  8.44 us
  transfers between devices with their start and end apart: 4, of which 4 were waited for; matrix products, arithmetic and copies ran while one was open for 5% of the time, Pallas kernels for 7%

profile of v11, /device:TPU:0, one launch (start us, length us, event | category | flops | bytes accessed | tf_op | source)
XLA Modules:
  0.0 264.4 jit_solution(5546710141016338493)
XLA Ops:
  0.6 2.7 %slice_bitcast_fusion = (bf16[2,128,2048]{2,1,0:T(8,128)(2,1)S(1)}, bf16[2,128,2048]{2,1,0:T(8,128)(2,1)}) fusion(bf16[1,2,256,2048]{3,2,1,0:T(8,128)(2,1)} %param.9), kind=kLoop, calls=%fused_computation.13 | loop fusion | bytes 4194304 | tf_op jit(solution)/shard_map/squeeze | solution.py:439
  3.3 1.3 collective-permute-start.1
  5.3 12.5 %shard_map.95.pre_ref = f32[4,256,2048]{2,1,0:T(8,128)} custom-call(f32[1,1]{1,0:T(1,128)} %bitcast.8.base_ref, bf16[1,2,256,2048]{3,2,1,0:T(8,128)(2,1)} %wave_ref.1, bf16[1,2,256,2048]{3,2,1,0:T(8,128)(2,1)} %src_ref.3, f32[1,256,2048]{2,1,0:T(8,128)} %slow_ref.1, f32[1,256,2048]{2,1,0:T(8,128)} %refl_ref.1), custom_call_target="tpu_custom_call" | custom-call | tf_op jit(solution)/shard_map/pallas_call | solution.py:258
  17.8 0.1 fusion.37
  17.8 0.6 fusion.44
  18.4 0.3 fusion.16
  18.7 0.7 pad_maximum_fusion.1.w_ref
  19.4 12.0 %collective-permute-done.1.hand_ref = bf16[2,128,2048]{2,1,0:T(8,128)(2,1)S(1)} collective-permute-done((bf16[2,128,2048]{2,1,0:T(8,128)(2,1)S(1)}, bf16[2,128,2048]{2,1,0:T(8,128)(2,1)S(1)}, u32[]{:S(2)}, u32[]{:S(2)}) %collective-permute-start.1) | collective-permute-done | bytes 1048608 | tf_op jit(solution)/shard_map/ppermute | solution.py:21
  31.3 0.0 copy-start.1
  31.3 1.1 copy-done.1
  32.4 5.4 %shard_map.97 = f32[8,2,128,256]{3,2,1,0:T(8,128)} custom-call(f32[4,256,2048]{2,1,0:T(8,128)} %shard_map.95.pre_ref, bf16[2,128,2048]{2,1,0:T(8,128)(2,1)} %copy-done.1, f32[2,128,128]{2,1,0:T(8,128)} %pad_maximum_fusion.1.w_ref, f32[2,16,128]{2,1,0:T(8,128)} %get-tuple-element.5.tw_ref), custom_call_target="tpu_custom_call" | custom-call | tf_op jit(solution)/shard_map/pallas_call | solution.py:351
  37.8 5.1 %all-to-all-start.1 = ((f32[8,2,128,256]{3,2,1,0:T(8,128)}), f32[8,2,128,256]{3,2,1,0:T(8,128)S(1)}, u32[]{:S(2)}, u32[]{:S(2)}) async-start(f32[8,2,128,256]{3,2,1,0:T(8,128)} %shard_map.97), calls=%async_computation.1 | async-start | bytes 4194304 | tf_op jit(solution)/shard_map/all_to_all | solution.py:441
  42.9 1.3 collective-permute-start
  44.2 27.0 %collective-permute-done.hand_ref = bf16[2,128,2048]{2,1,0:T(8,128)(2,1)S(1)} collective-permute-done((bf16[2,128,2048]{2,1,0:T(8,128)(2,1)}, bf16[2,128,2048]{2,1,0:T(8,128)(2,1)S(1)}, u32[]{:S(2)}, u32[]{:S(2)}) %collective-permute-start) | collective-permute-done | bytes 1048608 | tf_op jit(solution)/shard_map/ppermute | solution.py:21
  71.2 0.0 copy-start.2
  71.2 1.1 copy-done.2
  72.3 5.4 %shard_map.96 = f32[8,2,128,256]{3,2,1,0:T(8,128)} custom-call(f32[4,256,2048]{2,1,0:T(8,128)} %shard_map.95.pre_ref, bf16[2,128,2048]{2,1,0:T(8,128)(2,1)} %copy-done.2, f32[2,128,128]{2,1,0:T(8,128)} %pad_maximum_fusion.1.w_ref, f32[2,16,128]{2,1,0:T(8,128)} %get-tuple-element.5.tw_ref), custom_call_target="tpu_custom_call" | custom-call | tf_op jit(solution)/shard_map/pallas_call | solution.py:351
  77.6 14.3 %all-to-all-done.1.refs_1_ = f32[8,2,128,256]{3,2,1,0:T(8,128)S(1)} async-done(((f32[8,2,128,256]{3,2,1,0:T(8,128)}), f32[8,2,128,256]{3,2,1,0:T(8,128)S(1)}, u32[]{:S(2)}, u32[]{:S(2)}) %all-to-all-start.1) | async-done | bytes 2097184 | tf_op jit(solution)/shard_map/all_to_all | solution.py:441
  91.9 0.0 copy-start
  91.9 1.3 copy-done
  93.3 4.6 %all-to-all-start = ((f32[8,2,128,256]{3,2,1,0:T(8,128)}), f32[8,2,128,256]{3,2,1,0:T(8,128)}, u32[]{:S(2)}, u32[]{:S(2)}) async-start(f32[8,2,128,256]{3,2,1,0:T(8,128)} %shard_map.96), calls=%async_computation | async-start | bytes 4194304 | tf_op jit(solution)/shard_map/all_to_all | solution.py:441
  97.8 2.0 copy.10.refs_4_
  99.8 8.4 %fusion.2 = (f32[1,2048,256]{2,1,0:T(8,128)S(1)}, f32[1,2048,256]{2,1,0:T(8,128)S(1)}) fusion(f32[256]{0:T(256)S(1)} %fusion.43, f32[2048]{0:T(1024)S(1)} %fusion.33), kind=kLoop, calls=%fused_computation.5 | loop fusion | flops 4718592 | bytes 4203520 | tf_op jit(solution)/shard_map/mul | solution.py:407
  108.3 2.2 pad_maximum_fusion.refs_2_
  110.5 36.2 %all-to-all-done.refs_0_ = f32[8,2,128,256]{3,2,1,0:T(8,128)} async-done(((f32[8,2,128,256]{3,2,1,0:T(8,128)}), f32[8,2,128,256]{3,2,1,0:T(8,128)}, u32[]{:S(2)}, u32[]{:S(2)}) %all-to-all-start) | async-done | bytes 2097184 | tf_op jit(solution)/shard_map/all_to_all | solution.py:441
  146.7 11.8 %shard_map.98 = f32[8,2,256,256]{3,2,1,0:T(8,128)} custom-call(f32[8,2,128,256]{3,2,1,0:T(8,128)} %all-to-all-done.refs_0_, f32[8,2,128,256]{3,2,1,0:T(8,128)} %copy-done, f32[2,2048,256]{2,1,0:T(8,128)} %pad_maximum_fusion.refs_2_, bf16[2,256,384]{2,1,0:T(8,128)(2,1)} %constant.124.clone.refs_3_, f32[2,16,128,1]{3,2,1,0:T(8,128)} %copy.10.refs_4_), custom_call_target="tpu_custom_call" | custom-call | tf_op jit(solution)/shard_map/pallas_call | solution.py:226
  158.5 98.5 %all_to_all.15.x_ref = f32[8,2,256,256]{3,2,1,0:T(8,128)} all-to-all(f32[8,2,256,256]{3,2,1,0:T(8,128)} %shard_map.98), channel_id=1, replica_groups=mesh['slab'=4,'gx'=8] {'gx'}, dimensions={0} | all-to-all | bytes 8388608 | tf_op jit(solution)/shard_map/all_to_all | solution.py:446
  257.0 7.4 %shard_map.99 = (bf16[1,2,256,2048]{3,2,1,0:T(8,128)(2,1)}, f32[1,256,2048]{2,1,0:T(8,128)}) custom-call(f32[8,2,256,256]{3,2,1,0:T(8,128)} %all_to_all.15.x_ref, bf16[1,2,256,2048]{3,2,1,0:T(8,128)(2,1)} %src_ref.3, bf16[2,384,256]{2,1,0:T(8,128)(2,1)} %constant.125.clone.w_ref, f32[2,16,128]{2,1,0:T(8,128)} %get-tuple-element.5.tw_ref), custom_call_target="tpu_custom_call" | custom-call | tf_op jit(solution)/shard_map/pallas_call | solution.py:370
  (2 shorter events, 0.0 us)
Async XLA Ops:
  3.3 28.0 %collective-permute-start.1 = (bf16[2,128,2048]{2,1,0:T(8,128)(2,1)S(1)}, bf16[2,128,2048]{2,1,0:T(8,128)(2,1)S(1)}, u32[]{:S(2)}, u32[]{:S(2)}) collective-permute-start(bf16[2,128,2048]{2,1,0:T(8,128)(2,1)S(1)} %get-tuple-element.2), channel_id=1, source_target_pairs={{8,0},{16,8},{24,16},{9,1},{17,9},{25,17},{10,2},{18,10},{26,18},{... | collective-permute-start | bytes 3145736 | tf_op jit(solution)/shard_map/ppermute | solution.py:21
  31.3 1.1 copy-start.1
  37.8 54.2 %all-to-all-start.1 = ((f32[8,2,128,256]{3,2,1,0:T(8,128)}), f32[8,2,128,256]{3,2,1,0:T(8,128)S(1)}, u32[]{:S(2)}, u32[]{:S(2)}) async-start(f32[8,2,128,256]{3,2,1,0:T(8,128)} %shard_map.97), calls=%async_computation.1 | async-start | bytes 4194304 | tf_op jit(solution)/shard_map/all_to_all | solution.py:441
  42.9 28.3 %collective-permute-start = (bf16[2,128,2048]{2,1,0:T(8,128)(2,1)}, bf16[2,128,2048]{2,1,0:T(8,128)(2,1)S(1)}, u32[]{:S(2)}, u32[]{:S(2)}) collective-permute-start(bf16[2,128,2048]{2,1,0:T(8,128)(2,1)} %get-tuple-element.3), channel_id=1, source_target_pairs={{8,0},{16,8},{24,16},{9,1},{17,9},{25,17},{10,2},{18,10},{26,18},{... | collective-permute-start | bytes 3145736 | tf_op jit(solution)/shard_map/ppermute | solution.py:21
  71.2 1.1 copy-start.2
  91.9 1.3 copy-start
  93.3 53.4 %all-to-all-start = ((f32[8,2,128,256]{3,2,1,0:T(8,128)}), f32[8,2,128,256]{3,2,1,0:T(8,128)}, u32[]{:S(2)}, u32[]{:S(2)}) async-start(f32[8,2,128,256]{3,2,1,0:T(8,128)} %shard_map.96), calls=%async_computation | async-start | bytes 4194304 | tf_op jit(solution)/shard_map/all_to_all | solution.py:441

commit v12 on v8

--- a/solution.py
+++ b/solution.py
@@ -363,7 +363,7 @@
     groups, _, step, width = back.shape
     length = groups * width
     outer, inner, table, turn = lane_tables(length)
-    block = min(step, 64)
+    block = min(step, 128)
     return pl.pallas_call(
         lanes_inverse_kernel,
         grid=(step // block,),

time: 265 us -> 264 us (level)
  no operation moved by 1% of the time
where the time goes in v12:
time: 264 us
  blocking collectives  98.5 us (37%)
  waiting for transfers between devices  90.8 us (34%)
  Pallas kernels  41.5 us (16%)
  starting transfers between devices  12.2 us (5%)
  other arithmetic  11.4 us (4%)
  local copies, waits for them, and re-layouts  8.12 us (3%)
    all_to_all x1, blocking collectives, body(): lax.all_to_all(spatial, 'gx', split_axis=0, concat_axis=0, tiled=True)  98.5 us
    all_to_all x2, waiting for transfers between devices, body(): lax.all_to_all(field, 'gx', split_axis=0, concat_axis=0, tiled=True)  50.8 us
    ppermute x2, waiting for transfers between devices, shifted(): return lax.ppermute(block, axis, route)  39.9 us
    pallas_call x1, Pallas kernels, prelens(): pl.pallas_call(prelens_kernel, grid=(count // block,), in_specs=[pl.Block...  12.5 us
    pallas_call x1, Pallas kernels, rows_shift(): pl.pallas_call(rows_kernel, grid=(width // block,), in_specs=[pl.BlockSpe...  11.8 us
    pallas_call x2, Pallas kernels, lanes_forward(): pl.pallas_call(lanes_forward_kernel, grid=(step // block,), in_specs=[pl....  10.1 us
    all_to_all x2, starting transfers between devices, body(): lax.all_to_all(field, 'gx', split_axis=0, concat_axis=0, tiled=True)  9.68 us
    mul x1, other arithmetic, propagator(): return (real_part * scale, imag_part * scale)  8.44 us
  transfers between devices with their start and end apart: 4, of which 4 were waited for; matrix products, arithmetic and copies ran while one was open for 5% of the time, Pallas kernels for 7%

profile of v12, /device:TPU:0, one launch (start us, length us, event | category | flops | bytes accessed | tf_op | source)
XLA Modules:
  0.0 263.8 jit_solution(16585316567651716360)
XLA Ops:
  0.6 2.7 %slice_bitcast_fusion = (bf16[2,128,2048]{2,1,0:T(8,128)(2,1)S(1)}, bf16[2,128,2048]{2,1,0:T(8,128)(2,1)}) fusion(bf16[1,2,256,2048]{3,2,1,0:T(8,128)(2,1)} %param.11), kind=kLoop, calls=%fused_computation.13 | loop fusion | bytes 4194304 | tf_op jit(solution)/shard_map/squeeze | solution.py:436
  3.3 1.3 collective-permute-start.1
  5.3 12.5 %shard_map.113.pre_ref = f32[4,256,2048]{2,1,0:T(8,128)} custom-call(f32[1,1]{1,0:T(1,128)} %bitcast.8.base_ref, bf16[1,2,256,2048]{3,2,1,0:T(8,128)(2,1)} %wave_ref.1, bf16[1,2,256,2048]{3,2,1,0:T(8,128)(2,1)} %src_ref.3, f32[1,256,2048]{2,1,0:T(8,128)} %slow_ref.1, f32[1,256,2048]{2,1,0:T(8,128)} %refl_ref.1), custom_call_target="tpu_custom_call" | custom-call | tf_op jit(solution)/shard_map/pallas_call | solution.py:258
  17.8 0.1 fusion.29
  17.8 0.6 fusion.36
  18.4 12.9 %collective-permute-done.1.hand_ref = bf16[2,128,2048]{2,1,0:T(8,128)(2,1)S(1)} collective-permute-done((bf16[2,128,2048]{2,1,0:T(8,128)(2,1)S(1)}, bf16[2,128,2048]{2,1,0:T(8,128)(2,1)S(1)}, u32[]{:S(2)}, u32[]{:S(2)}) %collective-permute-start.1) | collective-permute-done | bytes 1048608 | tf_op jit(solution)/shard_map/ppermute | solution.py:21
  31.3 0.0 copy-start.1
  31.3 1.1 copy-done.1
  32.4 5.1 %shard_map.115 = f32[8,2,128,256]{3,2,1,0:T(8,128)} custom-call(f32[4,256,2048]{2,1,0:T(8,128)} %shard_map.113.pre_ref, bf16[2,128,2048]{2,1,0:T(8,128)(2,1)} %copy-done.1, bf16[2,384,256]{2,1,0:T(8,128)(2,1)} %constant.108.clone.w_ref, f32[2,16,128]{2,1,0:T(8,128)} %get-tuple-element.5.tw_ref), custom_call_target="tpu_custom_call" | custom-call | tf_op jit(solution)/shard_map/pallas_call | solution.py:348
  37.5 5.1 %all-to-all-start.1 = ((f32[8,2,128,256]{3,2,1,0:T(8,128)}), f32[8,2,128,256]{3,2,1,0:T(8,128)S(1)}, u32[]{:S(2)}, u32[]{:S(2)}) async-start(f32[8,2,128,256]{3,2,1,0:T(8,128)} %shard_map.115), calls=%async_computation.1 | async-start | bytes 4194304 | tf_op jit(solution)/shard_map/all_to_all | solution.py:438
  42.6 1.3 collective-permute-start
  43.9 27.0 %collective-permute-done.hand_ref = bf16[2,128,2048]{2,1,0:T(8,128)(2,1)S(1)} collective-permute-done((bf16[2,128,2048]{2,1,0:T(8,128)(2,1)}, bf16[2,128,2048]{2,1,0:T(8,128)(2,1)S(1)}, u32[]{:S(2)}, u32[]{:S(2)}) %collective-permute-start) | collective-permute-done | bytes 1048608 | tf_op jit(solution)/shard_map/ppermute | solution.py:21
  70.9 0.0 copy-start.2
  70.9 1.1 copy-done.2
  71.9 5.1 %shard_map.114 = f32[8,2,128,256]{3,2,1,0:T(8,128)} custom-call(f32[4,256,2048]{2,1,0:T(8,128)} %shard_map.113.pre_ref, bf16[2,128,2048]{2,1,0:T(8,128)(2,1)} %copy-done.2, bf16[2,384,256]{2,1,0:T(8,128)(2,1)} %constant.108.clone.w_ref, f32[2,16,128]{2,1,0:T(8,128)} %get-tuple-element.5.tw_ref), custom_call_target="tpu_custom_call" | custom-call | tf_op jit(solution)/shard_map/pallas_call | solution.py:348
  77.0 14.6 %all-to-all-done.1.refs_1_ = f32[8,2,128,256]{3,2,1,0:T(8,128)S(1)} async-done(((f32[8,2,128,256]{3,2,1,0:T(8,128)}), f32[8,2,128,256]{3,2,1,0:T(8,128)S(1)}, u32[]{:S(2)}, u32[]{:S(2)}) %all-to-all-start.1) | async-done | bytes 2097184 | tf_op jit(solution)/shard_map/all_to_all | solution.py:438
  91.6 0.0 copy-start
  91.6 1.3 copy-done
  93.0 4.6 %all-to-all-start = ((f32[8,2,128,256]{3,2,1,0:T(8,128)}), f32[8,2,128,256]{3,2,1,0:T(8,128)}, u32[]{:S(2)}, u32[]{:S(2)}) async-start(f32[8,2,128,256]{3,2,1,0:T(8,128)} %shard_map.114), calls=%async_computation | async-start | bytes 4194304 | tf_op jit(solution)/shard_map/all_to_all | solution.py:438
  97.5 2.0 copy.12.refs_4_
  99.5 8.4 %fusion.2 = (f32[1,2048,256]{2,1,0:T(8,128)S(1)}, f32[1,2048,256]{2,1,0:T(8,128)S(1)}) fusion(f32[256]{0:T(256)S(1)} %fusion.35, f32[2048]{0:T(1024)S(1)} %fusion.25), kind=kLoop, calls=%fused_computation.5 | loop fusion | flops 4718592 | bytes 4203520 | tf_op jit(solution)/shard_map/mul | solution.py:404
  108.0 2.2 pad_maximum_fusion.refs_2_
  110.2 36.2 %all-to-all-done.refs_0_ = f32[8,2,128,256]{3,2,1,0:T(8,128)} async-done(((f32[8,2,128,256]{3,2,1,0:T(8,128)}), f32[8,2,128,256]{3,2,1,0:T(8,128)}, u32[]{:S(2)}, u32[]{:S(2)}) %all-to-all-start) | async-done | bytes 2097184 | tf_op jit(solution)/shard_map/all_to_all | solution.py:438
  146.4 11.8 %shard_map.116 = f32[8,2,256,256]{3,2,1,0:T(8,128)} custom-call(f32[8,2,128,256]{3,2,1,0:T(8,128)} %all-to-all-done.refs_0_, f32[8,2,128,256]{3,2,1,0:T(8,128)} %copy-done, f32[2,2048,256]{2,1,0:T(8,128)} %pad_maximum_fusion.refs_2_, bf16[2,256,384]{2,1,0:T(8,128)(2,1)} %constant.109.clone.refs_3_, f32[2,16,128,1]{3,2,1,0:T(8,128)} %copy.12.refs_4_), custom_call_target="tpu_custom_call" | custom-call | tf_op jit(solution)/shard_map/pallas_call | solution.py:226
  158.2 98.5 %all_to_all.15.x_ref = f32[8,2,256,256]{3,2,1,0:T(8,128)} all-to-all(f32[8,2,256,256]{3,2,1,0:T(8,128)} %shard_map.116), channel_id=1, replica_groups=mesh['slab'=4,'gx'=8] {'gx'}, dimensions={0} | all-to-all | bytes 8388608 | tf_op jit(solution)/shard_map/all_to_all | solution.py:443
  256.7 7.1 %shard_map.117 = (bf16[1,2,256,2048]{3,2,1,0:T(8,128)(2,1)}, f32[1,256,2048]{2,1,0:T(8,128)}) custom-call(f32[8,2,256,256]{3,2,1,0:T(8,128)} %all_to_all.15.x_ref, bf16[1,2,256,2048]{3,2,1,0:T(8,128)(2,1)} %src_ref.3, bf16[2,384,256]{2,1,0:T(8,128)(2,1)} %constant.108.clone.w_ref, f32[2,16,128]{2,1,0:T(8,128)} %get-tuple-element.5.tw_ref), custom_call_target="tpu_custom_call" | custom-call | tf_op jit(solution)/shard_map/pallas_call | solution.py:367
  (2 shorter events, 0.0 us)
Async XLA Ops:
  3.3 28.0 %collective-permute-start.1 = (bf16[2,128,2048]{2,1,0:T(8,128)(2,1)S(1)}, bf16[2,128,2048]{2,1,0:T(8,128)(2,1)S(1)}, u32[]{:S(2)}, u32[]{:S(2)}) collective-permute-start(bf16[2,128,2048]{2,1,0:T(8,128)(2,1)S(1)} %get-tuple-element.2), channel_id=1, source_target_pairs={{8,0},{16,8},{24,16},{9,1},{17,9},{25,17},{10,2},{18,10},{26,18},{... | collective-permute-start | bytes 3145736 | tf_op jit(solution)/shard_map/ppermute | solution.py:21
  31.3 1.1 copy-start.1
  37.5 54.2 %all-to-all-start.1 = ((f32[8,2,128,256]{3,2,1,0:T(8,128)}), f32[8,2,128,256]{3,2,1,0:T(8,128)S(1)}, u32[]{:S(2)}, u32[]{:S(2)}) async-start(f32[8,2,128,256]{3,2,1,0:T(8,128)} %shard_map.115), calls=%async_computation.1 | async-start | bytes 4194304 | tf_op jit(solution)/shard_map/all_to_all | solution.py:438
  42.6 28.3 %collective-permute-start = (bf16[2,128,2048]{2,1,0:T(8,128)(2,1)}, bf16[2,128,2048]{2,1,0:T(8,128)(2,1)S(1)}, u32[]{:S(2)}, u32[]{:S(2)}) collective-permute-start(bf16[2,128,2048]{2,1,0:T(8,128)(2,1)} %get-tuple-element.3), channel_id=1, source_target_pairs={{8,0},{16,8},{24,16},{9,1},{17,9},{25,17},{10,2},{18,10},{26,18},{... | collective-permute-start | bytes 3145736 | tf_op jit(solution)/shard_map/ppermute | solution.py:21
  70.9 1.1 copy-start.2
  91.6 1.3 copy-start
  93.0 53.5 %all-to-all-start = ((f32[8,2,128,256]{3,2,1,0:T(8,128)}), f32[8,2,128,256]{3,2,1,0:T(8,128)}, u32[]{:S(2)}, u32[]{:S(2)}) async-start(f32[8,2,128,256]{3,2,1,0:T(8,128)} %shard_map.114), calls=%async_computation | async-start | bytes 4194304 | tf_op jit(solution)/shard_map/all_to_all | solution.py:438

commit v13 on v12

--- a/solution.py
+++ b/solution.py
@@ -252,7 +252,7 @@
 
 def prelens(wavefield, source, slowness, reflectivity, base):
     _, _, count, length = wavefield.shape
-    block = min(count, 32)
+    block = min(count, 64)
     quad = lambda i: (0, 0, i, 0)
     flat = lambda i: (0, i, 0)
     return pl.pallas_call(

time: 264 us -> 264 us (level)
  transfers between devices with their start and end apart: 4 -> 4, of which waited for: 4 -> 4; matrix products, arithmetic and copies ran while one was open for 5% -> 5% of each run, Pallas kernels for 7% -> 6%
where the time goes in v13:
time: 264 us
  blocking collectives  98.5 us (37%)
  waiting for transfers between devices  91.6 us (35%)
  Pallas kernels  40.6 us (15%)
  starting transfers between devices  12.2 us (5%)
  other arithmetic  11.4 us (4%)
  local copies, waits for them, and re-layouts  8.12 us (3%)
    all_to_all x1, blocking collectives, body(): lax.all_to_all(spatial, 'gx', split_axis=0, concat_axis=0, tiled=True)  98.5 us
    all_to_all x2, waiting for transfers between devices, body(): lax.all_to_all(field, 'gx', split_axis=0, concat_axis=0, tiled=True)  50.8 us
    ppermute x2, waiting for transfers between devices, shifted(): return lax.ppermute(block, axis, route)  40.8 us
    pallas_call x1, Pallas kernels, rows_shift(): pl.pallas_call(rows_kernel, grid=(width // block,), in_specs=[pl.BlockSpe...  11.8 us
    pallas_call x1, Pallas kernels, prelens(): pl.pallas_call(prelens_kernel, grid=(count // block,), in_specs=[pl.Block...  11.6 us
    pallas_call x2, Pallas kernels, lanes_forward(): pl.pallas_call(lanes_forward_kernel, grid=(step // block,), in_specs=[pl....  10.1 us
    all_to_all x2, starting transfers between devices, body(): lax.all_to_all(field, 'gx', split_axis=0, concat_axis=0, tiled=True)  9.68 us
    mul x1, other arithmetic, propagator(): return (real_part * scale, imag_part * scale)  8.44 us
  transfers between devices with their start and end apart: 4, of which 4 were waited for; matrix products, arithmetic and copies ran while one was open for 5% of the time, Pallas kernels for 6%

profile of v13, /device:TPU:0, one launch (start us, length us, event | category | flops | bytes accessed | tf_op | source)
XLA Modules:
  0.0 263.8 jit_solution(3628829093554909602)
XLA Ops:
  0.6 2.7 %slice_bitcast_fusion = (bf16[2,128,2048]{2,1,0:T(8,128)(2,1)S(1)}, bf16[2,128,2048]{2,1,0:T(8,128)(2,1)}) fusion(bf16[1,2,256,2048]{3,2,1,0:T(8,128)(2,1)} %param.11), kind=kLoop, calls=%fused_computation.13 | loop fusion | bytes 4194304 | tf_op jit(solution)/shard_map/squeeze | solution.py:436
  3.3 1.3 collective-permute-start.1
  5.3 11.6 %shard_map.113.pre_ref = f32[4,256,2048]{2,1,0:T(8,128)} custom-call(f32[1,1]{1,0:T(1,128)} %bitcast.8.base_ref, bf16[1,2,256,2048]{3,2,1,0:T(8,128)(2,1)} %wave_ref.1, bf16[1,2,256,2048]{3,2,1,0:T(8,128)(2,1)} %src_ref.3, f32[1,256,2048]{2,1,0:T(8,128)} %slow_ref.1, f32[1,256,2048]{2,1,0:T(8,128)} %refl_ref.1), custom_call_target="tpu_custom_call" | custom-call | tf_op jit(solution)/shard_map/pallas_call | solution.py:258
  16.9 0.1 fusion.29
  17.0 0.6 fusion.36
  17.6 13.8 %collective-permute-done.1.hand_ref = bf16[2,128,2048]{2,1,0:T(8,128)(2,1)S(1)} collective-permute-done((bf16[2,128,2048]{2,1,0:T(8,128)(2,1)S(1)}, bf16[2,128,2048]{2,1,0:T(8,128)(2,1)S(1)}, u32[]{:S(2)}, u32[]{:S(2)}) %collective-permute-start.1) | collective-permute-done | bytes 1048608 | tf_op jit(solution)/shard_map/ppermute | solution.py:21
  31.3 0.0 copy-start.1
  31.3 1.1 copy-done.1
  32.4 5.1 %shard_map.115 = f32[8,2,128,256]{3,2,1,0:T(8,128)} custom-call(f32[4,256,2048]{2,1,0:T(8,128)} %shard_map.113.pre_ref, bf16[2,128,2048]{2,1,0:T(8,128)(2,1)} %copy-done.1, bf16[2,384,256]{2,1,0:T(8,128)(2,1)} %constant.108.clone.w_ref, f32[2,16,128]{2,1,0:T(8,128)} %get-tuple-element.5.tw_ref), custom_call_target="tpu_custom_call" | custom-call | tf_op jit(solution)/shard_map/pallas_call | solution.py:348
  37.5 5.1 %all-to-all-start.1 = ((f32[8,2,128,256]{3,2,1,0:T(8,128)}), f32[8,2,128,256]{3,2,1,0:T(8,128)S(1)}, u32[]{:S(2)}, u32[]{:S(2)}) async-start(f32[8,2,128,256]{3,2,1,0:T(8,128)} %shard_map.115), calls=%async_computation.1 | async-start | bytes 4194304 | tf_op jit(solution)/shard_map/all_to_all | solution.py:438
  42.6 1.3 collective-permute-start
  43.9 27.0 %collective-permute-done.hand_ref = bf16[2,128,2048]{2,1,0:T(8,128)(2,1)S(1)} collective-permute-done((bf16[2,128,2048]{2,1,0:T(8,128)(2,1)}, bf16[2,128,2048]{2,1,0:T(8,128)(2,1)S(1)}, u32[]{:S(2)}, u32[]{:S(2)}) %collective-permute-start) | collective-permute-done | bytes 1048608 | tf_op jit(solution)/shard_map/ppermute | solution.py:21
  70.9 0.0 copy-start.2
  70.9 1.1 copy-done.2
  71.9 5.1 %shard_map.114 = f32[8,2,128,256]{3,2,1,0:T(8,128)} custom-call(f32[4,256,2048]{2,1,0:T(8,128)} %shard_map.113.pre_ref, bf16[2,128,2048]{2,1,0:T(8,128)(2,1)} %copy-done.2, bf16[2,384,256]{2,1,0:T(8,128)(2,1)} %constant.108.clone.w_ref, f32[2,16,128]{2,1,0:T(8,128)} %get-tuple-element.5.tw_ref), custom_call_target="tpu_custom_call" | custom-call | tf_op jit(solution)/shard_map/pallas_call | solution.py:348
  77.0 14.6 %all-to-all-done.1.refs_1_ = f32[8,2,128,256]{3,2,1,0:T(8,128)S(1)} async-done(((f32[8,2,128,256]{3,2,1,0:T(8,128)}), f32[8,2,128,256]{3,2,1,0:T(8,128)S(1)}, u32[]{:S(2)}, u32[]{:S(2)}) %all-to-all-start.1) | async-done | bytes 2097184 | tf_op jit(solution)/shard_map/all_to_all | solution.py:438
  91.6 0.0 copy-start
  91.6 1.3 copy-done
  93.0 4.6 %all-to-all-start = ((f32[8,2,128,256]{3,2,1,0:T(8,128)}), f32[8,2,128,256]{3,2,1,0:T(8,128)}, u32[]{:S(2)}, u32[]{:S(2)}) async-start(f32[8,2,128,256]{3,2,1,0:T(8,128)} %shard_map.114), calls=%async_computation | async-start | bytes 4194304 | tf_op jit(solution)/shard_map/all_to_all | solution.py:438
  97.5 2.0 copy.12.refs_4_
  99.5 8.4 %fusion.2 = (f32[1,2048,256]{2,1,0:T(8,128)S(1)}, f32[1,2048,256]{2,1,0:T(8,128)S(1)}) fusion(f32[256]{0:T(256)S(1)} %fusion.35, f32[2048]{0:T(1024)S(1)} %fusion.25), kind=kLoop, calls=%fused_computation.5 | loop fusion | flops 4718592 | bytes 4203520 | tf_op jit(solution)/shard_map/mul | solution.py:404
  108.0 2.2 pad_maximum_fusion.refs_2_
  110.2 36.2 %all-to-all-done.refs_0_ = f32[8,2,128,256]{3,2,1,0:T(8,128)} async-done(((f32[8,2,128,256]{3,2,1,0:T(8,128)}), f32[8,2,128,256]{3,2,1,0:T(8,128)}, u32[]{:S(2)}, u32[]{:S(2)}) %all-to-all-start) | async-done | bytes 2097184 | tf_op jit(solution)/shard_map/all_to_all | solution.py:438
  146.4 11.8 %shard_map.116 = f32[8,2,256,256]{3,2,1,0:T(8,128)} custom-call(f32[8,2,128,256]{3,2,1,0:T(8,128)} %all-to-all-done.refs_0_, f32[8,2,128,256]{3,2,1,0:T(8,128)} %copy-done, f32[2,2048,256]{2,1,0:T(8,128)} %pad_maximum_fusion.refs_2_, bf16[2,256,384]{2,1,0:T(8,128)(2,1)} %constant.109.clone.refs_3_, f32[2,16,128,1]{3,2,1,0:T(8,128)} %copy.12.refs_4_), custom_call_target="tpu_custom_call" | custom-call | tf_op jit(solution)/shard_map/pallas_call | solution.py:226
  158.2 98.5 %all_to_all.15.x_ref = f32[8,2,256,256]{3,2,1,0:T(8,128)} all-to-all(f32[8,2,256,256]{3,2,1,0:T(8,128)} %shard_map.116), channel_id=1, replica_groups=mesh['slab'=4,'gx'=8] {'gx'}, dimensions={0} | all-to-all | bytes 8388608 | tf_op jit(solution)/shard_map/all_to_all | solution.py:443
  256.7 7.1 %shard_map.117 = (bf16[1,2,256,2048]{3,2,1,0:T(8,128)(2,1)}, f32[1,256,2048]{2,1,0:T(8,128)}) custom-call(f32[8,2,256,256]{3,2,1,0:T(8,128)} %all_to_all.15.x_ref, bf16[1,2,256,2048]{3,2,1,0:T(8,128)(2,1)} %src_ref.3, bf16[2,384,256]{2,1,0:T(8,128)(2,1)} %constant.108.clone.w_ref, f32[2,16,128]{2,1,0:T(8,128)} %get-tuple-element.5.tw_ref), custom_call_target="tpu_custom_call" | custom-call | tf_op jit(solution)/shard_map/pallas_call | solution.py:367
  (2 shorter events, 0.0 us)
Async XLA Ops:
  3.3 28.0 %collective-permute-start.1 = (bf16[2,128,2048]{2,1,0:T(8,128)(2,1)S(1)}, bf16[2,128,2048]{2,1,0:T(8,128)(2,1)S(1)}, u32[]{:S(2)}, u32[]{:S(2)}) collective-permute-start(bf16[2,128,2048]{2,1,0:T(8,128)(2,1)S(1)} %get-tuple-element.2), channel_id=1, source_target_pairs={{8,0},{16,8},{24,16},{9,1},{17,9},{25,17},{10,2},{18,10},{26,18},{... | collective-permute-start | bytes 3145736 | tf_op jit(solution)/shard_map/ppermute | solution.py:21
  31.3 1.1 copy-start.1
  37.5 54.2 %all-to-all-start.1 = ((f32[8,2,128,256]{3,2,1,0:T(8,128)}), f32[8,2,128,256]{3,2,1,0:T(8,128)S(1)}, u32[]{:S(2)}, u32[]{:S(2)}) async-start(f32[8,2,128,256]{3,2,1,0:T(8,128)} %shard_map.115), calls=%async_computation.1 | async-start | bytes 4194304 | tf_op jit(solution)/shard_map/all_to_all | solution.py:438
  42.6 28.3 %collective-permute-start = (bf16[2,128,2048]{2,1,0:T(8,128)(2,1)}, bf16[2,128,2048]{2,1,0:T(8,128)(2,1)S(1)}, u32[]{:S(2)}, u32[]{:S(2)}) collective-permute-start(bf16[2,128,2048]{2,1,0:T(8,128)(2,1)} %get-tuple-element.3), channel_id=1, source_target_pairs={{8,0},{16,8},{24,16},{9,1},{17,9},{25,17},{10,2},{18,10},{26,18},{... | collective-permute-start | bytes 3145736 | tf_op jit(solution)/shard_map/ppermute | solution.py:21
  70.9 1.1 copy-start.2
  91.6 1.3 copy-start
  93.0 53.5 %all-to-all-start = ((f32[8,2,128,256]{3,2,1,0:T(8,128)}), f32[8,2,128,256]{3,2,1,0:T(8,128)}, u32[]{:S(2)}, u32[]{:S(2)}) async-start(f32[8,2,128,256]{3,2,1,0:T(8,128)} %shard_map.114), calls=%async_computation | async-start | bytes 4194304 | tf_op jit(solution)/shard_map/all_to_all | solution.py:438

commit v14 on v13

--- a/solution.py
+++ b/solution.py
@@ -252,7 +252,7 @@
 
 def prelens(wavefield, source, slowness, reflectivity, base):
     _, _, count, length = wavefield.shape
-    block = min(count, 64)
+    block = min(count, 128)
     quad = lambda i: (0, 0, i, 0)
     flat = lambda i: (0, i, 0)
     return pl.pallas_call(

time: 264 us -> 264 us (level)
  transfers between devices with their start and end apart: 4 -> 4, of which waited for: 4 -> 4; matrix products, arithmetic and copies ran while one was open for 5% -> 5% of each run, Pallas kernels for 6% -> 7%
where the time goes in v14:
time: 264 us
  blocking collectives  98.5 us (37%)
  waiting for transfers between devices  90.5 us (34%)
  Pallas kernels  41.8 us (16%)
  starting transfers between devices  12.2 us (5%)
  other arithmetic  11.4 us (4%)
  local copies, waits for them, and re-layouts  8.12 us (3%)
    all_to_all x1, blocking collectives, body(): lax.all_to_all(spatial, 'gx', split_axis=0, concat_axis=0, tiled=True)  98.5 us
    all_to_all x2, waiting for transfers between devices, body(): lax.all_to_all(field, 'gx', split_axis=0, concat_axis=0, tiled=True)  50.8 us
    ppermute x2, waiting for transfers between devices, shifted(): return lax.ppermute(block, axis, route)  39.6 us
    pallas_call x1, Pallas kernels, prelens(): pl.pallas_call(prelens_kernel, grid=(count // block,), in_specs=[pl.Block...  12.8 us
    pallas_call x1, Pallas kernels, rows_shift(): pl.pallas_call(rows_kernel, grid=(width // block,), in_specs=[pl.BlockSpe...  11.8 us
    pallas_call x2, Pallas kernels, lanes_forward(): pl.pallas_call(lanes_forward_kernel, grid=(step // block,), in_specs=[pl....  10.1 us
    all_to_all x2, starting transfers between devices, body(): lax.all_to_all(field, 'gx', split_axis=0, concat_axis=0, tiled=True)  9.68 us
    mul x1, other arithmetic, propagator(): return (real_part * scale, imag_part * scale)  8.44 us
  transfers between devices with their start and end apart: 4, of which 4 were waited for; matrix products, arithmetic and copies ran while one was open for 5% of the time, Pallas kernels for 7%

profile of v14, /device:TPU:0, one launch (start us, length us, event | category | flops | bytes accessed | tf_op | source)
XLA Modules:
  0.0 263.8 jit_solution(4501049994524953059)
XLA Ops:
  0.6 2.7 %slice_bitcast_fusion = (bf16[2,128,2048]{2,1,0:T(8,128)(2,1)S(1)}, bf16[2,128,2048]{2,1,0:T(8,128)(2,1)}) fusion(bf16[1,2,256,2048]{3,2,1,0:T(8,128)(2,1)} %param.11), kind=kLoop, calls=%fused_computation.13 | loop fusion | bytes 4194304 | tf_op jit(solution)/shard_map/squeeze | solution.py:436
  3.3 1.3 collective-permute-start.1
  5.3 12.8 %shard_map.113.pre_ref = f32[4,256,2048]{2,1,0:T(8,128)} custom-call(f32[1,1]{1,0:T(1,128)} %bitcast.8.base_ref, bf16[1,2,256,2048]{3,2,1,0:T(8,128)(2,1)} %wave_ref.1, bf16[1,2,256,2048]{3,2,1,0:T(8,128)(2,1)} %src_ref.3, f32[1,256,2048]{2,1,0:T(8,128)} %slow_ref.1, f32[1,256,2048]{2,1,0:T(8,128)} %refl_ref.1), custom_call_target="tpu_custom_call" | custom-call | tf_op jit(solution)/shard_map/pallas_call | solution.py:258
  18.0 0.1 fusion.29
  18.1 0.6 fusion.36
  18.7 12.6 %collective-permute-done.1.hand_ref = bf16[2,128,2048]{2,1,0:T(8,128)(2,1)S(1)} collective-permute-done((bf16[2,128,2048]{2,1,0:T(8,128)(2,1)S(1)}, bf16[2,128,2048]{2,1,0:T(8,128)(2,1)S(1)}, u32[]{:S(2)}, u32[]{:S(2)}) %collective-permute-start.1) | collective-permute-done | bytes 1048608 | tf_op jit(solution)/shard_map/ppermute | solution.py:21
  31.3 0.0 copy-start.1
  31.3 1.1 copy-done.1
  32.4 5.1 %shard_map.115 = f32[8,2,128,256]{3,2,1,0:T(8,128)} custom-call(f32[4,256,2048]{2,1,0:T(8,128)} %shard_map.113.pre_ref, bf16[2,128,2048]{2,1,0:T(8,128)(2,1)} %copy-done.1, bf16[2,384,256]{2,1,0:T(8,128)(2,1)} %constant.108.clone.w_ref, f32[2,16,128]{2,1,0:T(8,128)} %get-tuple-element.5.tw_ref), custom_call_target="tpu_custom_call" | custom-call | tf_op jit(solution)/shard_map/pallas_call | solution.py:348
  37.5 5.1 %all-to-all-start.1 = ((f32[8,2,128,256]{3,2,1,0:T(8,128)}), f32[8,2,128,256]{3,2,1,0:T(8,128)S(1)}, u32[]{:S(2)}, u32[]{:S(2)}) async-start(f32[8,2,128,256]{3,2,1,0:T(8,128)} %shard_map.115), calls=%async_computation.1 | async-start | bytes 4194304 | tf_op jit(solution)/shard_map/all_to_all | solution.py:438
  42.6 1.3 collective-permute-start
  43.9 27.0 %collective-permute-done.hand_ref = bf16[2,128,2048]{2,1,0:T(8,128)(2,1)S(1)} collective-permute-done((bf16[2,128,2048]{2,1,0:T(8,128)(2,1)}, bf16[2,128,2048]{2,1,0:T(8,128)(2,1)S(1)}, u32[]{:S(2)}, u32[]{:S(2)}) %collective-permute-start) | collective-permute-done | bytes 1048608 | tf_op jit(solution)/shard_map/ppermute | solution.py:21
  70.9 0.0 copy-start.2
  70.9 1.1 copy-done.2
  71.9 5.1 %shard_map.114 = f32[8,2,128,256]{3,2,1,0:T(8,128)} custom-call(f32[4,256,2048]{2,1,0:T(8,128)} %shard_map.113.pre_ref, bf16[2,128,2048]{2,1,0:T(8,128)(2,1)} %copy-done.2, bf16[2,384,256]{2,1,0:T(8,128)(2,1)} %constant.108.clone.w_ref, f32[2,16,128]{2,1,0:T(8,128)} %get-tuple-element.5.tw_ref), custom_call_target="tpu_custom_call" | custom-call | tf_op jit(solution)/shard_map/pallas_call | solution.py:348
  77.0 14.6 %all-to-all-done.1.refs_1_ = f32[8,2,128,256]{3,2,1,0:T(8,128)S(1)} async-done(((f32[8,2,128,256]{3,2,1,0:T(8,128)}), f32[8,2,128,256]{3,2,1,0:T(8,128)S(1)}, u32[]{:S(2)}, u32[]{:S(2)}) %all-to-all-start.1) | async-done | bytes 2097184 | tf_op jit(solution)/shard_map/all_to_all | solution.py:438
  91.6 0.0 copy-start
  91.6 1.3 copy-done
  93.0 4.6 %all-to-all-start = ((f32[8,2,128,256]{3,2,1,0:T(8,128)}), f32[8,2,128,256]{3,2,1,0:T(8,128)}, u32[]{:S(2)}, u32[]{:S(2)}) async-start(f32[8,2,128,256]{3,2,1,0:T(8,128)} %shard_map.114), calls=%async_computation | async-start | bytes 4194304 | tf_op jit(solution)/shard_map/all_to_all | solution.py:438
  97.5 2.0 copy.12.refs_4_
  99.5 8.4 %fusion.2 = (f32[1,2048,256]{2,1,0:T(8,128)S(1)}, f32[1,2048,256]{2,1,0:T(8,128)S(1)}) fusion(f32[256]{0:T(256)S(1)} %fusion.35, f32[2048]{0:T(1024)S(1)} %fusion.25), kind=kLoop, calls=%fused_computation.5 | loop fusion | flops 4718592 | bytes 4203520 | tf_op jit(solution)/shard_map/mul | solution.py:404
  108.0 2.2 pad_maximum_fusion.refs_2_
  110.2 36.2 %all-to-all-done.refs_0_ = f32[8,2,128,256]{3,2,1,0:T(8,128)} async-done(((f32[8,2,128,256]{3,2,1,0:T(8,128)}), f32[8,2,128,256]{3,2,1,0:T(8,128)}, u32[]{:S(2)}, u32[]{:S(2)}) %all-to-all-start) | async-done | bytes 2097184 | tf_op jit(solution)/shard_map/all_to_all | solution.py:438
  146.4 11.8 %shard_map.116 = f32[8,2,256,256]{3,2,1,0:T(8,128)} custom-call(f32[8,2,128,256]{3,2,1,0:T(8,128)} %all-to-all-done.refs_0_, f32[8,2,128,256]{3,2,1,0:T(8,128)} %copy-done, f32[2,2048,256]{2,1,0:T(8,128)} %pad_maximum_fusion.refs_2_, bf16[2,256,384]{2,1,0:T(8,128)(2,1)} %constant.109.clone.refs_3_, f32[2,16,128,1]{3,2,1,0:T(8,128)} %copy.12.refs_4_), custom_call_target="tpu_custom_call" | custom-call | tf_op jit(solution)/shard_map/pallas_call | solution.py:226
  158.2 98.5 %all_to_all.15.x_ref = f32[8,2,256,256]{3,2,1,0:T(8,128)} all-to-all(f32[8,2,256,256]{3,2,1,0:T(8,128)} %shard_map.116), channel_id=1, replica_groups=mesh['slab'=4,'gx'=8] {'gx'}, dimensions={0} | all-to-all | bytes 8388608 | tf_op jit(solution)/shard_map/all_to_all | solution.py:443
  256.7 7.1 %shard_map.117 = (bf16[1,2,256,2048]{3,2,1,0:T(8,128)(2,1)}, f32[1,256,2048]{2,1,0:T(8,128)}) custom-call(f32[8,2,256,256]{3,2,1,0:T(8,128)} %all_to_all.15.x_ref, bf16[1,2,256,2048]{3,2,1,0:T(8,128)(2,1)} %src_ref.3, bf16[2,384,256]{2,1,0:T(8,128)(2,1)} %constant.108.clone.w_ref, f32[2,16,128]{2,1,0:T(8,128)} %get-tuple-element.5.tw_ref), custom_call_target="tpu_custom_call" | custom-call | tf_op jit(solution)/shard_map/pallas_call | solution.py:367
  (2 shorter events, 0.0 us)
Async XLA Ops:
  3.3 28.0 %collective-permute-start.1 = (bf16[2,128,2048]{2,1,0:T(8,128)(2,1)S(1)}, bf16[2,128,2048]{2,1,0:T(8,128)(2,1)S(1)}, u32[]{:S(2)}, u32[]{:S(2)}) collective-permute-start(bf16[2,128,2048]{2,1,0:T(8,128)(2,1)S(1)} %get-tuple-element.2), channel_id=1, source_target_pairs={{8,0},{16,8},{24,16},{9,1},{17,9},{25,17},{10,2},{18,10},{26,18},{... | collective-permute-start | bytes 3145736 | tf_op jit(solution)/shard_map/ppermute | solution.py:21
  31.3 1.1 copy-start.1
  37.5 54.2 %all-to-all-start.1 = ((f32[8,2,128,256]{3,2,1,0:T(8,128)}), f32[8,2,128,256]{3,2,1,0:T(8,128)S(1)}, u32[]{:S(2)}, u32[]{:S(2)}) async-start(f32[8,2,128,256]{3,2,1,0:T(8,128)} %shard_map.115), calls=%async_computation.1 | async-start | bytes 4194304 | tf_op jit(solution)/shard_map/all_to_all | solution.py:438
  42.6 28.3 %collective-permute-start = (bf16[2,128,2048]{2,1,0:T(8,128)(2,1)}, bf16[2,128,2048]{2,1,0:T(8,128)(2,1)S(1)}, u32[]{:S(2)}, u32[]{:S(2)}) collective-permute-start(bf16[2,128,2048]{2,1,0:T(8,128)(2,1)} %get-tuple-element.3), channel_id=1, source_target_pairs={{8,0},{16,8},{24,16},{9,1},{17,9},{25,17},{10,2},{18,10},{26,18},{... | collective-permute-start | bytes 3145736 | tf_op jit(solution)/shard_map/ppermute | solution.py:21
  70.9 1.1 copy-start.2
  91.6 1.3 copy-start
  93.0 53.5 %all-to-all-start = ((f32[8,2,128,256]{3,2,1,0:T(8,128)}), f32[8,2,128,256]{3,2,1,0:T(8,128)}, u32[]{:S(2)}, u32[]{:S(2)}) async-start(f32[8,2,128,256]{3,2,1,0:T(8,128)} %shard_map.114), calls=%async_computation | async-start | bytes 4194304 | tf_op jit(solution)/shard_map/all_to_all | solution.py:438

commit v15 on v14

--- a/solution.py
+++ b/solution.py
@@ -252,7 +252,7 @@
 
 def prelens(wavefield, source, slowness, reflectivity, base):
     _, _, count, length = wavefield.shape
-    block = min(count, 128)
+    block = min(count, 256)
     quad = lambda i: (0, 0, i, 0)
     flat = lambda i: (0, i, 0)
     return pl.pallas_call(

time: 264 us -> 264 us (level)
  transfers between devices with their start and end apart: 4 -> 4, of which waited for: 4 -> 4; matrix products, arithmetic and copies ran while one was open for 5% -> 5% of each run, Pallas kernels for 7% -> 8%
where the time goes in v15:
time: 264 us
  blocking collectives  98.5 us (37%)
  waiting for transfers between devices  88 us (33%)
  Pallas kernels  44.2 us (17%)
  starting transfers between devices  12.2 us (5%)
  other arithmetic  11.4 us (4%)
  local copies, waits for them, and re-layouts  8.12 us (3%)
    all_to_all x1, blocking collectives, body(): lax.all_to_all(spatial, 'gx', split_axis=0, concat_axis=0, tiled=True)  98.5 us
    all_to_all x2, waiting for transfers between devices, body(): lax.all_to_all(field, 'gx', split_axis=0, concat_axis=0, tiled=True)  51 us
    ppermute x2, waiting for transfers between devices, shifted(): return lax.ppermute(block, axis, route)  37 us
    pallas_call x1, Pallas kernels, prelens(): pl.pallas_call(prelens_kernel, grid=(count // block,), in_specs=[pl.Block...  15.2 us
    pallas_call x1, Pallas kernels, rows_shift(): pl.pallas_call(rows_kernel, grid=(width // block,), in_specs=[pl.BlockSpe...  11.8 us
    pallas_call x2, Pallas kernels, lanes_forward(): pl.pallas_call(lanes_forward_kernel, grid=(step // block,), in_specs=[pl....  10.1 us
    all_to_all x2, starting transfers between devices, body(): lax.all_to_all(field, 'gx', split_axis=0, concat_axis=0, tiled=True)  9.5 us
    mul x1, other arithmetic, propagator(): return (real_part * scale, imag_part * scale)  8.44 us
  transfers between devices with their start and end apart: 4, of which 4 were waited for; matrix products, arithmetic and copies ran while one was open for 5% of the time, Pallas kernels for 8%

profile of v15, /device:TPU:0, one launch (start us, length us, event | category | flops | bytes accessed | tf_op | source)
XLA Modules:
  0.0 263.8 jit_solution(10126645072316426134)
XLA Ops:
  0.6 2.7 %slice_bitcast_fusion = (bf16[2,128,2048]{2,1,0:T(8,128)(2,1)S(1)}, bf16[2,128,2048]{2,1,0:T(8,128)(2,1)}) fusion(bf16[1,2,256,2048]{3,2,1,0:T(8,128)(2,1)} %param.11), kind=kLoop, calls=%fused_computation.13 | loop fusion | bytes 4194304 | tf_op jit(solution)/shard_map/squeeze | solution.py:436
  3.3 1.3 collective-permute-start.1
  5.3 15.2 %shard_map.113.pre_ref = f32[4,256,2048]{2,1,0:T(8,128)} custom-call(f32[1,1]{1,0:T(1,128)} %bitcast.8.base_ref, bf16[1,2,256,2048]{3,2,1,0:T(8,128)(2,1)} %wave_ref.1, bf16[1,2,256,2048]{3,2,1,0:T(8,128)(2,1)} %src_ref.3, f32[1,256,2048]{2,1,0:T(8,128)} %slow_ref.1, f32[1,256,2048]{2,1,0:T(8,128)} %refl_ref.1), custom_call_target="tpu_custom_call" | custom-call | tf_op jit(solution)/shard_map/pallas_call | solution.py:258
  20.5 0.1 fusion.29
  20.6 0.6 fusion.36
  21.2 10.2 %collective-permute-done.1.hand_ref = bf16[2,128,2048]{2,1,0:T(8,128)(2,1)S(1)} collective-permute-done((bf16[2,128,2048]{2,1,0:T(8,128)(2,1)S(1)}, bf16[2,128,2048]{2,1,0:T(8,128)(2,1)S(1)}, u32[]{:S(2)}, u32[]{:S(2)}) %collective-permute-start.1) | collective-permute-done | bytes 1048608 | tf_op jit(solution)/shard_map/ppermute | solution.py:21
  31.3 0.0 copy-start.1
  31.3 1.1 copy-done.1
  32.4 5.1 %shard_map.115 = f32[8,2,128,256]{3,2,1,0:T(8,128)} custom-call(f32[4,256,2048]{2,1,0:T(8,128)} %shard_map.113.pre_ref, bf16[2,128,2048]{2,1,0:T(8,128)(2,1)} %copy-done.1, bf16[2,384,256]{2,1,0:T(8,128)(2,1)} %constant.108.clone.w_ref, f32[2,16,128]{2,1,0:T(8,128)} %get-tuple-element.5.tw_ref), custom_call_target="tpu_custom_call" | custom-call | tf_op jit(solution)/shard_map/pallas_call | solution.py:348
  37.5 5.1 %all-to-all-start.1 = ((f32[8,2,128,256]{3,2,1,0:T(8,128)}), f32[8,2,128,256]{3,2,1,0:T(8,128)S(1)}, u32[]{:S(2)}, u32[]{:S(2)}) async-start(f32[8,2,128,256]{3,2,1,0:T(8,128)} %shard_map.115), calls=%async_computation.1 | async-start | bytes 4194304 | tf_op jit(solution)/shard_map/all_to_all | solution.py:438
  42.6 1.5 collective-permute-start
  44.0 26.8 %collective-permute-done.hand_ref = bf16[2,128,2048]{2,1,0:T(8,128)(2,1)S(1)} collective-permute-done((bf16[2,128,2048]{2,1,0:T(8,128)(2,1)}, bf16[2,128,2048]{2,1,0:T(8,128)(2,1)S(1)}, u32[]{:S(2)}, u32[]{:S(2)}) %collective-permute-start) | collective-permute-done | bytes 1048608 | tf_op jit(solution)/shard_map/ppermute | solution.py:21
  70.9 0.0 copy-start.2
  70.9 1.1 copy-done.2
  71.9 5.1 %shard_map.114 = f32[8,2,128,256]{3,2,1,0:T(8,128)} custom-call(f32[4,256,2048]{2,1,0:T(8,128)} %shard_map.113.pre_ref, bf16[2,128,2048]{2,1,0:T(8,128)(2,1)} %copy-done.2, bf16[2,384,256]{2,1,0:T(8,128)(2,1)} %constant.108.clone.w_ref, f32[2,16,128]{2,1,0:T(8,128)} %get-tuple-element.5.tw_ref), custom_call_target="tpu_custom_call" | custom-call | tf_op jit(solution)/shard_map/pallas_call | solution.py:348
  77.0 14.6 %all-to-all-done.1.refs_1_ = f32[8,2,128,256]{3,2,1,0:T(8,128)S(1)} async-done(((f32[8,2,128,256]{3,2,1,0:T(8,128)}), f32[8,2,128,256]{3,2,1,0:T(8,128)S(1)}, u32[]{:S(2)}, u32[]{:S(2)}) %all-to-all-start.1) | async-done | bytes 2097184 | tf_op jit(solution)/shard_map/all_to_all | solution.py:438
  91.6 0.0 copy-start
  91.6 1.3 copy-done
  93.0 4.4 %all-to-all-start = ((f32[8,2,128,256]{3,2,1,0:T(8,128)}), f32[8,2,128,256]{3,2,1,0:T(8,128)}, u32[]{:S(2)}, u32[]{:S(2)}) async-start(f32[8,2,128,256]{3,2,1,0:T(8,128)} %shard_map.114), calls=%async_computation | async-start | bytes 4194304 | tf_op jit(solution)/shard_map/all_to_all | solution.py:438
  97.3 2.0 copy.12.refs_4_
  99.4 8.4 %fusion.2 = (f32[1,2048,256]{2,1,0:T(8,128)S(1)}, f32[1,2048,256]{2,1,0:T(8,128)S(1)}) fusion(f32[256]{0:T(256)S(1)} %fusion.35, f32[2048]{0:T(1024)S(1)} %fusion.25), kind=kLoop, calls=%fused_computation.5 | loop fusion | flops 4718592 | bytes 4203520 | tf_op jit(solution)/shard_map/mul | solution.py:404
  107.8 2.2 pad_maximum_fusion.refs_2_
  110.0 36.4 %all-to-all-done.refs_0_ = f32[8,2,128,256]{3,2,1,0:T(8,128)} async-done(((f32[8,2,128,256]{3,2,1,0:T(8,128)}), f32[8,2,128,256]{3,2,1,0:T(8,128)}, u32[]{:S(2)}, u32[]{:S(2)}) %all-to-all-start) | async-done | bytes 2097184 | tf_op jit(solution)/shard_map/all_to_all | solution.py:438
  146.4 11.8 %shard_map.116 = f32[8,2,256,256]{3,2,1,0:T(8,128)} custom-call(f32[8,2,128,256]{3,2,1,0:T(8,128)} %all-to-all-done.refs_0_, f32[8,2,128,256]{3,2,1,0:T(8,128)} %copy-done, f32[2,2048,256]{2,1,0:T(8,128)} %pad_maximum_fusion.refs_2_, bf16[2,256,384]{2,1,0:T(8,128)(2,1)} %constant.109.clone.refs_3_, f32[2,16,128,1]{3,2,1,0:T(8,128)} %copy.12.refs_4_), custom_call_target="tpu_custom_call" | custom-call | tf_op jit(solution)/shard_map/pallas_call | solution.py:226
  158.2 98.5 %all_to_all.15.x_ref = f32[8,2,256,256]{3,2,1,0:T(8,128)} all-to-all(f32[8,2,256,256]{3,2,1,0:T(8,128)} %shard_map.116), channel_id=1, replica_groups=mesh['slab'=4,'gx'=8] {'gx'}, dimensions={0} | all-to-all | bytes 8388608 | tf_op jit(solution)/shard_map/all_to_all | solution.py:443
  256.7 7.1 %shard_map.117 = (bf16[1,2,256,2048]{3,2,1,0:T(8,128)(2,1)}, f32[1,256,2048]{2,1,0:T(8,128)}) custom-call(f32[8,2,256,256]{3,2,1,0:T(8,128)} %all_to_all.15.x_ref, bf16[1,2,256,2048]{3,2,1,0:T(8,128)(2,1)} %src_ref.3, bf16[2,384,256]{2,1,0:T(8,128)(2,1)} %constant.108.clone.w_ref, f32[2,16,128]{2,1,0:T(8,128)} %get-tuple-element.5.tw_ref), custom_call_target="tpu_custom_call" | custom-call | tf_op jit(solution)/shard_map/pallas_call | solution.py:367
  (2 shorter events, 0.0 us)
Async XLA Ops:
  3.3 28.0 %collective-permute-start.1 = (bf16[2,128,2048]{2,1,0:T(8,128)(2,1)S(1)}, bf16[2,128,2048]{2,1,0:T(8,128)(2,1)S(1)}, u32[]{:S(2)}, u32[]{:S(2)}) collective-permute-start(bf16[2,128,2048]{2,1,0:T(8,128)(2,1)S(1)} %get-tuple-element.2), channel_id=1, source_target_pairs={{8,0},{16,8},{24,16},{9,1},{17,9},{25,17},{10,2},{18,10},{26,18},{... | collective-permute-start | bytes 3145736 | tf_op jit(solution)/shard_map/ppermute | solution.py:21
  31.3 1.1 copy-start.1
  37.5 54.2 %all-to-all-start.1 = ((f32[8,2,128,256]{3,2,1,0:T(8,128)}), f32[8,2,128,256]{3,2,1,0:T(8,128)S(1)}, u32[]{:S(2)}, u32[]{:S(2)}) async-start(f32[8,2,128,256]{3,2,1,0:T(8,128)} %shard_map.115), calls=%async_computation.1 | async-start | bytes 4194304 | tf_op jit(solution)/shard_map/all_to_all | solution.py:438
  42.6 28.3 %collective-permute-start = (bf16[2,128,2048]{2,1,0:T(8,128)(2,1)}, bf16[2,128,2048]{2,1,0:T(8,128)(2,1)S(1)}, u32[]{:S(2)}, u32[]{:S(2)}) collective-permute-start(bf16[2,128,2048]{2,1,0:T(8,128)(2,1)} %get-tuple-element.3), channel_id=1, source_target_pairs={{8,0},{16,8},{24,16},{9,1},{17,9},{25,17},{10,2},{18,10},{26,18},{... | collective-permute-start | bytes 3145736 | tf_op jit(solution)/shard_map/ppermute | solution.py:21
  70.9 1.1 copy-start.2
  91.6 1.3 copy-start
  93.0 53.5 %all-to-all-start = ((f32[8,2,128,256]{3,2,1,0:T(8,128)}), f32[8,2,128,256]{3,2,1,0:T(8,128)}, u32[]{:S(2)}, u32[]{:S(2)}) async-start(f32[8,2,128,256]{3,2,1,0:T(8,128)} %shard_map.114), calls=%async_computation | async-start | bytes 4194304 | tf_op jit(solution)/shard_map/all_to_all | solution.py:438
